TPU v7x, 256 devices: a whole 4x4x8 slice. The times are simulated.
256 devices in a mesh: blk: 64 (over z, x_lo, y), circ: 4 (over x_hi, core).
Axes of the slice: x: 4 (x_hi: 2, x_lo: 2; x = x_hi * 2 + x_lo), y: 4, z: 8, core: 2. Of those that a mesh axis runs over, the one named last changes fastest.
Arguments:
- panels: float32 [4, 8192], P(None, ('blk', 'circ')), may hold values from -2 to 2, as said below
- node_of_panel: int32 [8192], P(('blk', 'circ')), may hold values from 0 to 2047, as said below
- stiffener_rows: int32 [32], replicated, may hold values from 0 to 511
- density_start: float32 [16, 8192], P(None, ('blk', 'circ')), may hold values from -6 to 6
- motion_start: float32 [16, 512, 1024], P(None, 'blk', 'circ'), may hold values from -6 to 6
- force: float32 [16, 512, 1024], P(None, 'blk', 'circ'), may hold values from -128 to 128
- stiffness: float32 [512, 1024], P('blk', 'circ'), may hold values from 0.5 to 2
Outputs:
- source_density: float32 [16, 8192], P(None, ('blk', 'circ'))
- surface_pressure: float32 [16, 8192], P(None, ('blk', 'circ'))
- shell_motion: float32 [16, 512, 1024], P(None, 'blk', 'circ')
Inputs may be any that keep to these rules, and one draw needn't show every extreme that they name: `panels`: every panel lies between 0.98 and 1.02 from the z axis, with z between -2 and 2 and area between 0.5 and 2 times 8 pi / 8192. `node_of_panel`: counted as row * 256 + column within the tile of the device that holds the panel. `stiffener_rows`: A row may be listed more than once.
All inputs are finite; a program needn't handle non-finite values.
Results may differ from a plain program's by a relative error of at most 0.0029.
Values may be sent and summed in bfloat16 or wider, within the bound.
No kernel may reach another device: no remote copies, remote signals or barrier semaphores. Data moves between devices by JAX's collectives and lax.ppermute only.
A program may use at most 64 MiB of HBM per device.

v0:
```python
import math

import jax
import jax.numpy as jnp
from jax import lax
from jax.sharding import PartitionSpec as P

ITERS = 4
SWEEPS = 2


wave_number = 4.0
single_scale = 30.0
double_scale = 6.0
hoop_spring = 40.0
inertia_term = 4.0
loss_factor = 0.2
relaxation = 0.3


def gather_columns(block):
    count = lax.axis_size("blk") * lax.axis_size("circ")
    index = lax.axis_index("blk") * lax.axis_size("circ") + lax.axis_index("circ")
    bits = count.bit_length() - 1
    held = block
    for level in reversed(range(bits)):
        bit = 1 << level
        pairs = [(i, i ^ bit) for i in range(count)]
        other = lax.ppermute(held, ("blk", "circ"), pairs)
        low = (index & bit) == 0
        first = jnp.where(low, held, other)
        second = jnp.where(low, other, held)
        held = jnp.stack([first, second], axis=0)
    order = list(reversed(range(bits)))
    held = jnp.transpose(held, order + [bits, bits + 1])
    held = held.reshape((count,) + block.shape)
    return jnp.transpose(held, (1, 0, 2)).reshape(block.shape[0], count * block.shape[1])


def with_halo(field, width):
    rows = lax.axis_size("blk")
    cols = lax.axis_size("circ")
    above = lax.ppermute(field[:, -width:, :], "blk", [(i, i + 1) for i in range(rows - 1)])
    below = lax.ppermute(field[:, :width, :], "blk", [(i + 1, i) for i in range(rows - 1)])
    field = jnp.concatenate([above, field, below], axis=1)
    left = lax.ppermute(field[:, :, -width:], "circ", [(i, (i + 1) % cols) for i in range(cols)])
    right = lax.ppermute(field[:, :, :width], "circ", [(i, (i - 1) % cols) for i in range(cols)])
    return jnp.concatenate([left, field, right], axis=2)


def laplace_inner(extended):
    return (
        extended[..., 2:, 1:-1]
        + extended[..., :-2, 1:-1]
        + extended[..., 1:-1, 2:]
        + extended[..., 1:-1, :-2]
        - 4.0 * extended[..., 1:-1, 1:-1]
    )


def trim(field, width):
    return field[..., width:field.shape[-2] - width, width:field.shape[-1] - width]


def kernel_blocks(targets, sources):
    radial = jnp.sqrt(targets[0] * targets[0] + targets[1] * targets[1])
    normal_x = (targets[0] / radial)[:, None]
    normal_y = (targets[1] / radial)[:, None]
    delta_x = targets[0][:, None] - sources[0][None, :]
    delta_y = targets[1][:, None] - sources[1][None, :]
    delta_z = targets[2][:, None] - sources[2][None, :]
    areas = sources[3][None, :]
    dist_sq = delta_x * delta_x + delta_y * delta_y + delta_z * delta_z + areas / math.pi
    distance = jnp.sqrt(dist_sq)
    inverse = 1.0 / distance
    phase_arg = wave_number * distance
    cosine = jnp.cos(phase_arg)
    sine_part = jnp.sin(phase_arg)
    weight = areas * (1.0 / (4.0 * math.pi)) * inverse
    single = single_scale * weight
    double = double_scale * weight * (normal_x * delta_x + normal_y * delta_y) * inverse * inverse
    real_stack = jnp.concatenate(
        [single * cosine, double * (-cosine - phase_arg * sine_part)], axis=0
    )
    imag_stack = jnp.concatenate(
        [single * sine_part, double * (phase_arg * cosine - sine_part)], axis=0
    )
    return (real_stack.astype(jnp.bfloat16), imag_stack.astype(jnp.bfloat16))


def form_kernels(targets, sources):
    width = sources.shape[1]
    block_cols = width
    block_count = width // block_cols
    source_blocks = jnp.transpose(sources.reshape(4, block_count, block_cols), (1, 0, 2))
    real_blocks, imag_blocks = lax.map(lambda block: kernel_blocks(targets, block), source_blocks)
    rows_out = real_blocks.shape[1]
    real_stack = jnp.transpose(real_blocks, (1, 0, 2)).reshape(rows_out, width)
    imag_stack = jnp.transpose(imag_blocks, (1, 0, 2)).reshape(rows_out, width)
    return (real_stack, imag_stack)


def fold_columns(real_stack, imag_stack):

    def fold_step(running, shard_piece, first_col):
        half = shard_piece.shape[0] // 2
        rotated = jnp.concatenate([-shard_piece[half:], shard_piece[:half]], axis=0)
        first = jnp.einsum("lc,rc->lr", shard_piece, real_stack, preferred_element_type=jnp.float32)
        second = jnp.einsum("lc,rc->lr", rotated, imag_stack, preferred_element_type=jnp.float32)
        return first + second

    return fold_step


def relax(motion, bend, load, stiffness, hoop_rows):
    half = motion.shape[0] // 2
    shift = hoop_spring * hoop_rows - inertia_term
    applied_re = bend[:half] - loss_factor * bend[half:] + shift * motion[:half]
    applied_im = bend[half:] + loss_factor * bend[:half] + shift * motion[half:]
    resid_re = load[:half] - applied_re
    resid_im = load[half:] - applied_im
    diag_re = 20.0 * stiffness + shift
    diag_im = 20.0 * loss_factor * stiffness
    denom = diag_re * diag_re + diag_im * diag_im
    update_re = (resid_re * diag_re + resid_im * diag_im) / denom
    update_im = (resid_im * diag_re - resid_re * diag_im) / denom
    return motion + relaxation * jnp.concatenate([update_re, update_im], axis=0)


def per_device(
    panels, node_of_panel, stiffener_rows, density_start, motion_start, force, stiffness
):
    panel_dev = panels.shape[1]
    channels = density_start.shape[0]
    axial, circum = stiffness.shape
    width = 2 * SWEEPS
    blk_index = lax.axis_index("blk")
    devices = lax.axis_size("blk") * lax.axis_size("circ")
    total_rows = axial * lax.axis_size("blk")
    rows_global = blk_index * axial - width + jnp.arange(axial + 2 * width, dtype=jnp.int32)
    inside = ((rows_global >= 0) & (rows_global < total_rows))[:, None]
    hoop_rows = jnp.any(rows_global[:, None] == stiffener_rows[None, :], axis=1).astype(
        jnp.float32
    )[:, None]
    panel_weight = panels[3] * (panel_dev * devices / (8.0 * math.pi))
    joined = gather_columns(jnp.concatenate([panels, density_start], axis=0))
    sources = joined[:4]
    target_rows = panels.shape[1]
    real_stack, imag_stack = form_kernels(panels, sources)
    fold_step = fold_columns(real_stack, imag_stack)
    density = density_start
    motion = motion_start
    pressure = jnp.zeros_like(density_start)
    for round_index in range(ITERS):
        flat_motion = motion.reshape(channels, axial * circum)
        neumann = jnp.take(flat_motion, node_of_panel, axis=1)
        density_bf = density.astype(jnp.bfloat16)
        if round_index == 0:
            gathered = joined[4:].astype(jnp.bfloat16)
        else:
            gathered = gather_columns(density_bf)
        start_sum = jnp.zeros((channels, 2 * target_rows), jnp.float32)
        combined = fold_step(start_sum, gathered, jnp.int32(0))
        single_part = combined[:, :target_rows]
        double_part = combined[:, target_rows:]
        pressure = single_part
        density = 0.5 * density + neumann - double_part
        fluid = jnp.zeros((channels, axial * circum), jnp.float32)
        fluid = fluid.at[:, node_of_panel].add(panel_weight[None, :] * pressure)
        load = force - fluid.reshape(channels, axial, circum)
        state = with_halo(jnp.concatenate([motion, load, stiffness[None]], axis=0), width)
        motion_ext = state[:channels]
        load_ext = state[channels:2 * channels]
        stiff_ext = state[2 * channels]
        for sweep_index in range(SWEEPS):
            edge = 2 * sweep_index + 1
            moment = trim(stiff_ext, edge) * laplace_inner(motion_ext)
            moment = jnp.where(inside[edge:inside.shape[0] - edge], moment, 0.0)
            bend = laplace_inner(moment)
            edge += 1
            rows_at = slice(edge, inside.shape[0] - edge)
            motion_ext = relax(
                trim(motion_ext, 2), bend, trim(load_ext, edge), trim(stiff_ext, edge), hoop_rows[rows_at]
            )
            motion_ext = jnp.where(inside[rows_at], motion_ext, 0.0)
        motion = motion_ext
    return (density, pressure, motion)


def solution(mesh):
    in_specs = (
        P(None, ("blk", "circ")),
        P(("blk", "circ")),
        P(),
        P(None, ("blk", "circ")),
        P(None, "blk", "circ"),
        P(None, "blk", "circ"),
        P("blk", "circ"),
    )
    out_specs = (P(None, ("blk", "circ")), P(None, ("blk", "circ")), P(None, "blk", "circ"))
    return jax.shard_map(
        per_device, mesh=mesh, in_specs=in_specs, out_specs=out_specs, check_vma=False
    )
```

profile of v0, /device:TPU:128, one launch (start us, length us, event | category | flops | bytes accessed | tf_op | source)
XLA Modules:
  0.0 328.4 jit_solution(6186140195612259802)
XLA Ops:
  1.8 7.2 %collective-permute-done = f32[20,32]{1,0:T(8,128)S(1)} collective-permute-done((f32[20,32]{1,0:T(8,128)S(1)}, f32[20,32]{1,0:T(8,128)S(1)}, u32[]{:S(2)}, u32[]{:S(2)}) %collective-permute-start) | collective-permute-done | bytes 2592 | tf_op jit(solution)/shard_map/ppermute | solution.py:29
  27.5 3.8 %collective-permute-done.4 = f32[2,2,2,2,20,32]{5,3,4,2,1,0:T(2,128)S(1)} collective-permute-done((f32[2,2,2,2,20,32]{5,3,4,2,1,0:T(2,128)S(1)}, f32[2,2,2,2,20,32]{5,3,4,2,1,0:T(2,128)S(1)}, u32[]{:S(2)}, u32[]{:S(2)}) %collective-permute-start.4) | collective-permute-done | bytes 40992 | tf_op jit(solution)/shard_map/ppermute | solution.py:29
  35.4 3.7 %collective-permute-done.5 = f32[2,2,2,2,2,20,32]{6,4,5,3,2,1,0:T(2,128)S(1)} collective-permute-done((f32[2,2,2,2,2,20,32]{6,4,5,3,2,1,0:T(2,128)S(1)}, f32[2,2,2,2,2,20,32]{6,4,5,3,2,1,0:T(2,128)S(1)}, u32[]{:S(2)}, u32[]{:S(2)}) %collective-permute-start.5) | collective-permute-done | bytes 81952 | tf_op jit(solution)/shard_map/ppermute | solution.py:29
  42.9 9.1 %collective-permute-done.6 = f32[2,2,2,2,2,2,20,32]{7,5,6,4,3,2,1,0:T(2,128)S(1)} collective-permute-done((f32[2,2,2,2,2,2,20,32]{7,5,6,4,3,2,1,0:T(2,128)S(1)}, f32[2,2,2,2,2,2,20,32]{7,5,6,4,3,2,1,0:T(2,128)S(1)}, u32[]{:S(2)}, u32[]{:S(2)}) %collective-permute-start.6) | collective-permute-done | bytes 163872 | tf_op jit(solution)/shard_map/ppermute | solution.py:29
  66.9 5.3 %multiply_convert_fusion = (bf16[32,8192]{1,0:T(8,128)(2,1)S(1)}, bf16[32,8192]{1,0:T(8,128)(2,1)S(1)}, bf16[32,8192]{1,0:T(8,128)(2,1)S(1)}, bf16[32,8192]{1,0:T(8,128)(2,1)S(1)}) fusion(f32[8192]{0:T(1024)S(1)} %div.69, f32[8192]{0:T(1024)S(1)} %sub.275, f32[32]{0:T(128)S(1)} %get-tuple-element.179, f32[8192]{0:T(1024)S(1)} %sub.270, ...), kind=kLoop, calls=%fused_computation.40 | loop fusion | flops 8650752 | bytes 2261632 | tf_op jit(solution)/shard_map/convert.1
  73.5 7.2 %collective-permute-done.12 = bf16[16,32]{1,0:T(8,128)(2,1)S(1)} collective-permute-done((bf16[16,32]{1,0:T(8,128)(2,1)S(1)}, bf16[16,32]{1,0:T(8,128)(2,1)S(1)}, u32[]{:S(2)}, u32[]{:S(2)}) %collective-permute-start.12) | collective-permute-done | bytes 1056 | tf_op jit(solution)/shard_map/ppermute | solution.py:29
  93.5 3.8 %collective-permute-start.16 = (bf16[2,2,2,2,16,32]{5,4,3,2,1,0:T(8,128)(2,1)S(1)}, bf16[2,2,2,2,16,32]{5,4,3,2,1,0:T(8,128)(2,1)S(1)}, u32[]{:S(2)}, u32[]{:S(2)}) collective-permute-start(bf16[2,2,2,2,16,32]{5,4,3,2,1,0:T(8,128)(2,1)S(1)} %pad_maximum_fusion.28), channel_id=1, source_target_pairs={{0,8},{1,9},{2,10},{3,11},{4,12},{5,13},{6,14},{7,15},{8,0},{9,1},... | collective-permute-start | bytes 49160 | tf_op jit(solution)/shard_map/ppermute | solution.py:29
  108.2 4.7 %collective-permute-done.18 = bf16[2,2,2,2,2,2,16,32]{7,6,5,4,3,2,1,0:T(8,128)(2,1)S(1)} collective-permute-done((bf16[2,2,2,2,2,2,16,32]{7,6,5,4,3,2,1,0:T(8,128)(2,1)S(1)}, bf16[2,2,2,2,2,2,16,32]{7,6,5,4,3,2,1,0:T(8,128)(2,1)S(1)}, u32[]{:S(2)}, u32[]{:S(2)}) %collective-permute-start.18) | collective-permute-done | bytes 65568 | tf_op jit(solution)/shard_map/ppermute | solution.py:29
  123.9 5.6 %collective-permute-start.9 = (f32[33,4,256]{2,1,0:T(4,128)S(1)}, f32[33,4,256]{2,1,0:T(4,128)S(1)}, u32[]{:S(2)}, u32[]{:S(2)}) collective-permute-start(f32[33,4,256]{2,1,0:T(4,128)S(1)} %get-tuple-element.105), channel_id=1, source_target_pairs={{4,0},{8,4},{12,8},{16,12},{20,16},{24,20},{28,24},{32,28},{36,32}... | collective-permute-start | bytes 405512 | tf_op jit(solution)/shard_map/ppermute | solution.py:44
  132.6 8.3 %collective-permute-done.8 = f32[33,4,256]{2,1,0:T(4,128)S(1)} collective-permute-done((f32[33,4,256]{2,1,0:T(4,128)S(1)}, f32[33,4,256]{2,1,0:T(4,128)S(1)}, u32[]{:S(2)}, u32[]{:S(2)}) %collective-permute-start.8) | collective-permute-done | bytes 135200 | tf_op jit(solution)/shard_map/ppermute | solution.py:43
  143.3 4.8 %collective-permute-done.11 = f32[33,16,4]{2,1,0:T(8,128)S(1)} collective-permute-done((f32[33,16,4]{2,1,0:T(8,128)S(1)}, f32[33,16,4]{2,1,0:T(8,128)S(1)}, u32[]{:S(2)}, u32[]{:S(2)}) %collective-permute-start.11) | collective-permute-done | bytes 8480 | tf_op jit(solution)/shard_map/ppermute | solution.py:47
  155.8 7.5 %collective-permute-done.24 = bf16[16,32]{1,0:T(8,128)(2,1)S(1)} collective-permute-done((bf16[16,32]{1,0:T(8,128)(2,1)S(1)}, bf16[16,32]{1,0:T(8,128)(2,1)S(1)}, u32[]{:S(2)}, u32[]{:S(2)}) %collective-permute-start.24) | collective-permute-done | bytes 1056 | tf_op jit(solution)/shard_map/ppermute | solution.py:29
  172.0 3.9 %collective-permute-done.27 = bf16[2,2,2,16,32]{4,3,2,1,0:T(8,128)(2,1)S(1)} collective-permute-done((bf16[2,2,2,16,32]{4,3,2,1,0:T(8,128)(2,1)S(1)}, bf16[2,2,2,16,32]{4,3,2,1,0:T(8,128)(2,1)S(1)}, u32[]{:S(2)}, u32[]{:S(2)}) %collective-permute-start.27) | collective-permute-done | bytes 8224 | tf_op jit(solution)/shard_map/ppermute | solution.py:29
  176.0 5.8 %collective-permute-done.28 = bf16[2,2,2,2,16,32]{5,4,3,2,1,0:T(8,128)(2,1)S(1)} collective-permute-done((bf16[2,2,2,2,16,32]{5,4,3,2,1,0:T(8,128)(2,1)S(1)}, bf16[2,2,2,2,16,32]{5,4,3,2,1,0:T(8,128)(2,1)S(1)}, u32[]{:S(2)}, u32[]{:S(2)}) %collective-permute-start.28) | collective-permute-done | bytes 16416 | tf_op jit(solution)/shard_map/ppermute | solution.py:29
  182.0 6.3 %collective-permute-done.29 = bf16[2,2,2,2,2,16,32]{6,5,4,3,2,1,0:T(8,128)(2,1)S(1)} collective-permute-done((bf16[2,2,2,2,2,16,32]{6,5,4,3,2,1,0:T(8,128)(2,1)S(1)}, bf16[2,2,2,2,2,16,32]{6,5,4,3,2,1,0:T(8,128)(2,1)S(1)}, u32[]{:S(2)}, u32[]{:S(2)}) %collective-permute-start.29) | collective-permute-done | bytes 32800 | tf_op jit(solution)/shard_map/ppermute | solution.py:29
  191.2 3.9 %collective-permute-start.20 = (f32[33,4,256]{2,1,0:T(4,128)S(1)}, f32[33,4,256]{2,1,0:T(4,128)S(1)}, u32[]{:S(2)}, u32[]{:S(2)}) collective-permute-start(f32[33,4,256]{2,1,0:T(4,128)S(1)} %get-tuple-element.102), channel_id=1, source_target_pairs={{0,4},{4,8},{8,12},{12,16},{16,20},{20,24},{24,28},{28,32},{32,36}... | collective-permute-start | bytes 405512 | tf_op jit(solution)/shard_map/ppermute | solution.py:43
  197.8 4.6 %collective-permute-done.20 = f32[33,4,256]{2,1,0:T(4,128)S(1)} collective-permute-done((f32[33,4,256]{2,1,0:T(4,128)S(1)}, f32[33,4,256]{2,1,0:T(4,128)S(1)}, u32[]{:S(2)}, u32[]{:S(2)}) %collective-permute-start.20) | collective-permute-done | bytes 135200 | tf_op jit(solution)/shard_map/ppermute | solution.py:43
  207.4 5.3 %collective-permute-done.22 = f32[33,16,4]{2,1,0:T(8,128)S(1)} collective-permute-done((f32[33,16,4]{2,1,0:T(8,128)S(1)}, f32[33,16,4]{2,1,0:T(8,128)S(1)}, u32[]{:S(2)}, u32[]{:S(2)}) %collective-permute-start.22) | collective-permute-done | bytes 8480 | tf_op jit(solution)/shard_map/ppermute | solution.py:46
  224.4 7.5 %collective-permute-done.36 = bf16[16,32]{1,0:T(8,128)(2,1)S(1)} collective-permute-done((bf16[16,32]{1,0:T(8,128)(2,1)S(1)}, bf16[16,32]{1,0:T(8,128)(2,1)S(1)}, u32[]{:S(2)}, u32[]{:S(2)}) %collective-permute-start.36) | collective-permute-done | bytes 1056 | tf_op jit(solution)/shard_map/ppermute | solution.py:29
  232.0 4.5 %collective-permute-done.37 = bf16[2,16,32]{2,1,0:T(8,128)(2,1)S(1)} collective-permute-done((bf16[2,16,32]{2,1,0:T(8,128)(2,1)S(1)}, bf16[2,16,32]{2,1,0:T(8,128)(2,1)S(1)}, u32[]{:S(2)}, u32[]{:S(2)}) %collective-permute-start.37) | collective-permute-done | bytes 2080 | tf_op jit(solution)/shard_map/ppermute | solution.py:29
  236.7 3.7 %collective-permute-done.38 = bf16[2,2,16,32]{3,2,1,0:T(8,128)(2,1)S(1)} collective-permute-done((bf16[2,2,16,32]{3,2,1,0:T(8,128)(2,1)S(1)}, bf16[2,2,16,32]{3,2,1,0:T(8,128)(2,1)S(1)}, u32[]{:S(2)}, u32[]{:S(2)}) %collective-permute-start.38) | collective-permute-done | bytes 4128 | tf_op jit(solution)/shard_map/ppermute | solution.py:29
  240.5 3.9 %collective-permute-done.39 = bf16[2,2,2,16,32]{4,3,2,1,0:T(8,128)(2,1)S(1)} collective-permute-done((bf16[2,2,2,16,32]{4,3,2,1,0:T(8,128)(2,1)S(1)}, bf16[2,2,2,16,32]{4,3,2,1,0:T(8,128)(2,1)S(1)}, u32[]{:S(2)}, u32[]{:S(2)}) %collective-permute-start.39) | collective-permute-done | bytes 8224 | tf_op jit(solution)/shard_map/ppermute | solution.py:29
  244.6 5.8 %collective-permute-done.40 = bf16[2,2,2,2,16,32]{5,4,3,2,1,0:T(8,128)(2,1)S(1)} collective-permute-done((bf16[2,2,2,2,16,32]{5,4,3,2,1,0:T(8,128)(2,1)S(1)}, bf16[2,2,2,2,16,32]{5,4,3,2,1,0:T(8,128)(2,1)S(1)}, u32[]{:S(2)}, u32[]{:S(2)}) %collective-permute-start.40) | collective-permute-done | bytes 16416 | tf_op jit(solution)/shard_map/ppermute | solution.py:29
  250.5 5.0 %collective-permute-done.41 = bf16[2,2,2,2,2,16,32]{6,5,4,3,2,1,0:T(8,128)(2,1)S(1)} collective-permute-done((bf16[2,2,2,2,2,16,32]{6,5,4,3,2,1,0:T(8,128)(2,1)S(1)}, bf16[2,2,2,2,2,16,32]{6,5,4,3,2,1,0:T(8,128)(2,1)S(1)}, u32[]{:S(2)}, u32[]{:S(2)}) %collective-permute-start.41) | collective-permute-done | bytes 32800 | tf_op jit(solution)/shard_map/ppermute | solution.py:29
  256.7 7.0 %collective-permute-done.42 = bf16[2,2,2,2,2,2,16,32]{7,6,5,4,3,2,1,0:T(8,128)(2,1)S(1)} collective-permute-done((bf16[2,2,2,2,2,2,16,32]{7,6,5,4,3,2,1,0:T(8,128)(2,1)S(1)}, bf16[2,2,2,2,2,2,16,32]{7,6,5,4,3,2,1,0:T(8,128)(2,1)S(1)}, u32[]{:S(2)}, u32[]{:S(2)}) %collective-permute-start.42) | collective-permute-done | bytes 65568 | tf_op jit(solution)/shard_map/ppermute | solution.py:29
  276.4 3.9 %collective-permute-start.32 = (f32[33,4,256]{2,1,0:T(4,128)S(1)}, f32[33,4,256]{2,1,0:T(4,128)S(1)}, u32[]{:S(2)}, u32[]{:S(2)}) collective-permute-start(f32[33,4,256]{2,1,0:T(4,128)S(1)} %get-tuple-element.100), channel_id=1, source_target_pairs={{0,4},{4,8},{8,12},{12,16},{16,20},{20,24},{24,28},{28,32},{32,36}... | collective-permute-start | bytes 405512 | tf_op jit(solution)/shard_map/ppermute | solution.py:43
  282.0 6.2 %collective-permute-done.32 = f32[33,4,256]{2,1,0:T(4,128)S(1)} collective-permute-done((f32[33,4,256]{2,1,0:T(4,128)S(1)}, f32[33,4,256]{2,1,0:T(4,128)S(1)}, u32[]{:S(2)}, u32[]{:S(2)}) %collective-permute-start.32) | collective-permute-done | bytes 135200 | tf_op jit(solution)/shard_map/ppermute | solution.py:43
  289.1 4.6 %collective-permute-done.35 = f32[33,16,4]{2,1,0:T(8,128)S(1)} collective-permute-done((f32[33,16,4]{2,1,0:T(8,128)S(1)}, f32[33,16,4]{2,1,0:T(8,128)S(1)}, u32[]{:S(2)}, u32[]{:S(2)}) %collective-permute-start.35) | collective-permute-done | bytes 8480 | tf_op jit(solution)/shard_map/ppermute | solution.py:47
  293.7 4.5 %collective-permute-done.34 = f32[33,16,4]{2,1,0:T(8,128)S(1)} collective-permute-done((f32[33,16,4]{2,1,0:T(8,128)S(1)}, f32[33,16,4]{2,1,0:T(8,128)S(1)}, u32[]{:S(2)}, u32[]{:S(2)}) %collective-permute-start.34) | collective-permute-done | bytes 8480 | tf_op jit(solution)/shard_map/ppermute | solution.py:46
  303.6 4.2 %collective-permute-start.44 = (f32[33,4,256]{2,1,0:T(4,128)S(1)}, f32[33,4,256]{2,1,0:T(4,128)S(1)}, u32[]{:S(2)}, u32[]{:S(2)}) collective-permute-start(f32[33,4,256]{2,1,0:T(4,128)S(1)} %get-tuple-element.98), channel_id=1, source_target_pairs={{0,4},{4,8},{8,12},{12,16},{16,20},{20,24},{24,28},{28,32},{32,36}... | collective-permute-start | bytes 405512 | tf_op jit(solution)/shard_map/ppermute | solution.py:43
  308.8 5.9 %collective-permute-done.44 = f32[33,4,256]{2,1,0:T(4,128)S(1)} collective-permute-done((f32[33,4,256]{2,1,0:T(4,128)S(1)}, f32[33,4,256]{2,1,0:T(4,128)S(1)}, u32[]{:S(2)}, u32[]{:S(2)}) %collective-permute-start.44) | collective-permute-done | bytes 135200 | tf_op jit(solution)/shard_map/ppermute | solution.py:43
  316.3 4.8 %collective-permute-done.47 = f32[33,16,4]{2,1,0:T(8,128)S(1)} collective-permute-done((f32[33,16,4]{2,1,0:T(8,128)S(1)}, f32[33,16,4]{2,1,0:T(8,128)S(1)}, u32[]{:S(2)}, u32[]{:S(2)}) %collective-permute-start.47) | collective-permute-done | bytes 8480 | tf_op jit(solution)/shard_map/ppermute | solution.py:47
  (349 shorter events, 153.4 us)
Async XLA Ops:
  1.4 7.6 %collective-permute-start = (f32[20,32]{1,0:T(8,128)S(1)}, f32[20,32]{1,0:T(8,128)S(1)}, u32[]{:S(2)}, u32[]{:S(2)}) collective-permute-start(f32[20,32]{1,0:T(8,128)S(1)} %pad_maximum_fusion.39), channel_id=1, source_target_pairs={{0,128},{1,129},{2,130},{3,131},{4,132},{5,133},{6,134},{7,135},{8... | collective-permute-start | bytes 7688 | tf_op jit(solution)/shard_map/ppermute | solution.py:29
  23.5 7.9 %collective-permute-start.4 = (f32[2,2,2,2,20,32]{5,3,4,2,1,0:T(2,128)S(1)}, f32[2,2,2,2,20,32]{5,3,4,2,1,0:T(2,128)S(1)}, u32[]{:S(2)}, u32[]{:S(2)}) collective-permute-start(f32[2,2,2,2,20,32]{5,3,4,2,1,0:T(2,128)S(1)} %pad_maximum_fusion.23), channel_id=1, source_target_pairs={{0,8},{1,9},{2,10},{3,11},{4,12},{5,13},{6,14},{7,15},{8,0},{9,1},... | collective-permute-start | bytes 122888 | tf_op jit(solution)/shard_map/ppermute | solution.py:29
  31.7 7.4 %collective-permute-start.5 = (f32[2,2,2,2,2,20,32]{6,4,5,3,2,1,0:T(2,128)S(1)}, f32[2,2,2,2,2,20,32]{6,4,5,3,2,1,0:T(2,128)S(1)}, u32[]{:S(2)}, u32[]{:S(2)}) collective-permute-start(f32[2,2,2,2,2,20,32]{6,4,5,3,2,1,0:T(2,128)S(1)} %pad_maximum_fusion.19), channel_id=1, source_target_pairs={{0,4},{1,5},{2,6},{3,7},{4,0},{5,1},{6,2},{7,3},{8,12},{9,13},{10,... | collective-permute-start | bytes 245768 | tf_op jit(solution)/shard_map/ppermute | solution.py:29
  39.7 12.2 %collective-permute-start.6 = (f32[2,2,2,2,2,2,20,32]{7,5,6,4,3,2,1,0:T(2,128)S(1)}, f32[2,2,2,2,2,2,20,32]{7,5,6,4,3,2,1,0:T(2,128)S(1)}, u32[]{:S(2)}, u32[]{:S(2)}) collective-permute-start(f32[2,2,2,2,2,2,20,32]{7,5,6,4,3,2,1,0:T(2,128)S(1)} %pad_maximum_fusion.11), channel_id=1, source_target_pairs={{0,2},{1,3},{2,0},{3,1},{4,6},{5,7},{6,4},{7,5},{8,10},{9,11},{10,... | collective-permute-start | bytes 491528 | tf_op jit(solution)/shard_map/ppermute | solution.py:29
  73.1 7.5 %collective-permute-start.12 = (bf16[16,32]{1,0:T(8,128)(2,1)S(1)}, bf16[16,32]{1,0:T(8,128)(2,1)S(1)}, u32[]{:S(2)}, u32[]{:S(2)}) collective-permute-start(bf16[16,32]{1,0:T(8,128)(2,1)S(1)} %get-tuple-element.173), channel_id=1, source_target_pairs={{0,128},{1,129},{2,130},{3,131},{4,132},{5,133},{6,134},{7,135},{8... | collective-permute-start | bytes 3080 | tf_op jit(solution)/shard_map/ppermute | solution.py:29
  93.5 6.2 %collective-permute-start.16 = (bf16[2,2,2,2,16,32]{5,4,3,2,1,0:T(8,128)(2,1)S(1)}, bf16[2,2,2,2,16,32]{5,4,3,2,1,0:T(8,128)(2,1)S(1)}, u32[]{:S(2)}, u32[]{:S(2)}) collective-permute-start(bf16[2,2,2,2,16,32]{5,4,3,2,1,0:T(8,128)(2,1)S(1)} %pad_maximum_fusion.28), channel_id=1, source_target_pairs={{0,8},{1,9},{2,10},{3,11},{4,12},{5,13},{6,14},{7,15},{8,0},{9,1},... | collective-permute-start | bytes 49160 | tf_op jit(solution)/shard_map/ppermute | solution.py:29
  99.7 5.1 %collective-permute-start.17 = (bf16[2,2,2,2,2,16,32]{6,5,4,3,2,1,0:T(8,128)(2,1)S(1)}, bf16[2,2,2,2,2,16,32]{6,5,4,3,2,1,0:T(8,128)(2,1)S(1)}, u32[]{:S(2)}, u32[]{:S(2)}) collective-permute-start(bf16[2,2,2,2,2,16,32]{6,5,4,3,2,1,0:T(8,128)(2,1)S(1)} %pad_maximum_fusion.24), channel_id=1, source_target_pairs={{0,4},{1,5},{2,6},{3,7},{4,0},{5,1},{6,2},{7,3},{8,12},{9,13},{10,... | collective-permute-start | bytes 98312 | tf_op jit(solution)/shard_map/ppermute | solution.py:29
  104.9 8.0 %collective-permute-start.18 = (bf16[2,2,2,2,2,2,16,32]{7,6,5,4,3,2,1,0:T(8,128)(2,1)S(1)}, bf16[2,2,2,2,2,2,16,32]{7,6,5,4,3,2,1,0:T(8,128)(2,1)S(1)}, u32[]{:S(2)}, u32[]{:S(2)}) collective-permute-start(bf16[2,2,2,2,2,2,16,32]{7,6,5,4,3,2,1,0:T(8,128)(2,1)S(1)} %pad_maximum_fusion.20), channel_id=1, source_target_pairs={{0,2},{1,3},{2,0},{3,1},{4,6},{5,7},{6,4},{7,5},{8,10},{9,11},{10,... | collective-permute-start | bytes 196616 | tf_op jit(solution)/shard_map/ppermute | solution.py:29
  123.9 8.7 %collective-permute-start.9 = (f32[33,4,256]{2,1,0:T(4,128)S(1)}, f32[33,4,256]{2,1,0:T(4,128)S(1)}, u32[]{:S(2)}, u32[]{:S(2)}) collective-permute-start(f32[33,4,256]{2,1,0:T(4,128)S(1)} %get-tuple-element.105), channel_id=1, source_target_pairs={{4,0},{8,4},{12,8},{16,12},{20,16},{24,20},{28,24},{32,28},{36,32}... | collective-permute-start | bytes 405512 | tf_op jit(solution)/shard_map/ppermute | solution.py:44
  129.5 11.5 %collective-permute-start.8 = (f32[33,4,256]{2,1,0:T(4,128)S(1)}, f32[33,4,256]{2,1,0:T(4,128)S(1)}, u32[]{:S(2)}, u32[]{:S(2)}) collective-permute-start(f32[33,4,256]{2,1,0:T(4,128)S(1)} %get-tuple-element.104), channel_id=1, source_target_pairs={{0,4},{4,8},{8,12},{12,16},{16,20},{20,24},{24,28},{28,32},{32,36}... | collective-permute-start | bytes 405512 | tf_op jit(solution)/shard_map/ppermute | solution.py:43
  141.2 7.0 %collective-permute-start.11 = (f32[33,16,4]{2,1,0:T(8,128)S(1)}, f32[33,16,4]{2,1,0:T(8,128)S(1)}, u32[]{:S(2)}, u32[]{:S(2)}) collective-permute-start(f32[33,16,4]{2,1,0:T(8,128)S(1)} %get-tuple-element.89), channel_id=1, source_target_pairs={{0,3},{1,0},{2,1},{3,2},{4,7},{5,4},{6,5},{7,6},{8,11},{9,8},{10,9... | collective-permute-start | bytes 25352 | tf_op jit(solution)/shard_map/ppermute | solution.py:47
  142.6 8.7 %collective-permute-start.10 = (f32[33,16,4]{2,1,0:T(8,128)S(1)}, f32[33,16,4]{2,1,0:T(8,128)S(1)}, u32[]{:S(2)}, u32[]{:S(2)}) collective-permute-start(f32[33,16,4]{2,1,0:T(8,128)S(1)} %get-tuple-element.88), channel_id=1, source_target_pairs={{0,1},{1,2},{2,3},{3,0},{4,5},{5,6},{6,7},{7,4},{8,9},{9,10},{10,1... | collective-permute-start | bytes 25352 | tf_op jit(solution)/shard_map/ppermute | solution.py:46
  155.8 7.5 %collective-permute-start.24 = (bf16[16,32]{1,0:T(8,128)(2,1)S(1)}, bf16[16,32]{1,0:T(8,128)(2,1)S(1)}, u32[]{:S(2)}, u32[]{:S(2)}) collective-permute-start(bf16[16,32]{1,0:T(8,128)(2,1)S(1)} %get-tuple-element.51), channel_id=1, source_target_pairs={{0,128},{1,129},{2,130},{3,131},{4,132},{5,133},{6,134},{7,135},{8... | collective-permute-start | bytes 3080 | tf_op jit(solution)/shard_map/ppermute | solution.py:29
  175.9 5.9 %collective-permute-start.28 = (bf16[2,2,2,2,16,32]{5,4,3,2,1,0:T(8,128)(2,1)S(1)}, bf16[2,2,2,2,16,32]{5,4,3,2,1,0:T(8,128)(2,1)S(1)}, u32[]{:S(2)}, u32[]{:S(2)}) collective-permute-start(bf16[2,2,2,2,16,32]{5,4,3,2,1,0:T(8,128)(2,1)S(1)} %pad_maximum_fusion.29), channel_id=1, source_target_pairs={{0,8},{1,9},{2,10},{3,11},{4,12},{5,13},{6,14},{7,15},{8,0},{9,1},... | collective-permute-start | bytes 49160 | tf_op jit(solution)/shard_map/ppermute | solution.py:29
  181.8 6.4 %collective-permute-start.29 = (bf16[2,2,2,2,2,16,32]{6,5,4,3,2,1,0:T(8,128)(2,1)S(1)}, bf16[2,2,2,2,2,16,32]{6,5,4,3,2,1,0:T(8,128)(2,1)S(1)}, u32[]{:S(2)}, u32[]{:S(2)}) collective-permute-start(bf16[2,2,2,2,2,16,32]{6,5,4,3,2,1,0:T(8,128)(2,1)S(1)} %pad_maximum_fusion.25), channel_id=1, source_target_pairs={{0,4},{1,5},{2,6},{3,7},{4,0},{5,1},{6,2},{7,3},{8,12},{9,13},{10,... | collective-permute-start | bytes 98312 | tf_op jit(solution)/shard_map/ppermute | solution.py:29
  188.3 9.4 %collective-permute-start.30 = (bf16[2,2,2,2,2,2,16,32]{7,6,5,4,3,2,1,0:T(8,128)(2,1)S(1)}, bf16[2,2,2,2,2,2,16,32]{7,6,5,4,3,2,1,0:T(8,128)(2,1)S(1)}, u32[]{:S(2)}, u32[]{:S(2)}) collective-permute-start(bf16[2,2,2,2,2,2,16,32]{7,6,5,4,3,2,1,0:T(8,128)(2,1)S(1)} %pad_maximum_fusion.21), channel_id=1, source_target_pairs={{0,2},{1,3},{2,0},{3,1},{4,6},{5,7},{6,4},{7,5},{8,10},{9,11},{10,... | collective-permute-start | bytes 196616 | tf_op jit(solution)/shard_map/ppermute | solution.py:29
  189.3 8.5 %collective-permute-start.21 = (f32[33,4,256]{2,1,0:T(4,128)S(1)}, f32[33,4,256]{2,1,0:T(4,128)S(1)}, u32[]{:S(2)}, u32[]{:S(2)}) collective-permute-start(f32[33,4,256]{2,1,0:T(4,128)S(1)} %get-tuple-element.103), channel_id=1, source_target_pairs={{4,0},{8,4},{12,8},{16,12},{20,16},{24,20},{28,24},{32,28},{36,32}... | collective-permute-start | bytes 405512 | tf_op jit(solution)/shard_map/ppermute | solution.py:44
  191.2 11.2 %collective-permute-start.20 = (f32[33,4,256]{2,1,0:T(4,128)S(1)}, f32[33,4,256]{2,1,0:T(4,128)S(1)}, u32[]{:S(2)}, u32[]{:S(2)}) collective-permute-start(f32[33,4,256]{2,1,0:T(4,128)S(1)} %get-tuple-element.102), channel_id=1, source_target_pairs={{0,4},{4,8},{8,12},{12,16},{16,20},{20,24},{24,28},{28,32},{32,36}... | collective-permute-start | bytes 405512 | tf_op jit(solution)/shard_map/ppermute | solution.py:43
  202.7 10.0 %collective-permute-start.22 = (f32[33,16,4]{2,1,0:T(8,128)S(1)}, f32[33,16,4]{2,1,0:T(8,128)S(1)}, u32[]{:S(2)}, u32[]{:S(2)}) collective-permute-start(f32[33,16,4]{2,1,0:T(8,128)S(1)} %get-tuple-element.86), channel_id=1, source_target_pairs={{0,1},{1,2},{2,3},{3,0},{4,5},{5,6},{6,7},{7,4},{8,9},{9,10},{10,1... | collective-permute-start | bytes 25352 | tf_op jit(solution)/shard_map/ppermute | solution.py:46
  203.4 13.8 %collective-permute-start.31 = (bf16[2,2,2,2,2,2,2,16,32]{8,7,6,5,4,3,2,1,0:T(8,128)(2,1)S(1)}, bf16[2,2,2,2,2,2,2,16,32]{8,7,6,5,4,3,2,1,0:T(8,128)(2,1)S(1)}, u32[]{:S(2)}, u32[]{:S(2)}) collective-permute-start(bf16[2,2,2,2,2,2,2,16,32]{8,7,6,5,4,3,2,1,0:T(8,128)(2,1)S(1)} %pad_maximum_fusion.17), channel_id=1, source_target_pairs={{0,1},{1,0},{2,3},{3,2},{4,5},{5,4},{6,7},{7,6},{8,9},{9,8},{10,11... | collective-permute-start | bytes 393224 | tf_op jit(solution)/shard_map/ppermute | solution.py:29
  224.3 7.5 %collective-permute-start.36 = (bf16[16,32]{1,0:T(8,128)(2,1)S(1)}, bf16[16,32]{1,0:T(8,128)(2,1)S(1)}, u32[]{:S(2)}, u32[]{:S(2)}) collective-permute-start(bf16[16,32]{1,0:T(8,128)(2,1)S(1)} %get-tuple-element.167), channel_id=1, source_target_pairs={{0,128},{1,129},{2,130},{3,131},{4,132},{5,133},{6,134},{7,135},{8... | collective-permute-start | bytes 3080 | tf_op jit(solution)/shard_map/ppermute | solution.py:29
  244.5 5.9 %collective-permute-start.40 = (bf16[2,2,2,2,16,32]{5,4,3,2,1,0:T(8,128)(2,1)S(1)}, bf16[2,2,2,2,16,32]{5,4,3,2,1,0:T(8,128)(2,1)S(1)}, u32[]{:S(2)}, u32[]{:S(2)}) collective-permute-start(bf16[2,2,2,2,16,32]{5,4,3,2,1,0:T(8,128)(2,1)S(1)} %pad_maximum_fusion.30), channel_id=1, source_target_pairs={{0,8},{1,9},{2,10},{3,11},{4,12},{5,13},{6,14},{7,15},{8,0},{9,1},... | collective-permute-start | bytes 49160 | tf_op jit(solution)/shard_map/ppermute | solution.py:29
  250.4 5.1 %collective-permute-start.41 = (bf16[2,2,2,2,2,16,32]{6,5,4,3,2,1,0:T(8,128)(2,1)S(1)}, bf16[2,2,2,2,2,16,32]{6,5,4,3,2,1,0:T(8,128)(2,1)S(1)}, u32[]{:S(2)}, u32[]{:S(2)}) collective-permute-start(bf16[2,2,2,2,2,16,32]{6,5,4,3,2,1,0:T(8,128)(2,1)S(1)} %pad_maximum_fusion.26), channel_id=1, source_target_pairs={{0,4},{1,5},{2,6},{3,7},{4,0},{5,1},{6,2},{7,3},{8,12},{9,13},{10,... | collective-permute-start | bytes 98312 | tf_op jit(solution)/shard_map/ppermute | solution.py:29
  255.5 8.2 %collective-permute-start.42 = (bf16[2,2,2,2,2,2,16,32]{7,6,5,4,3,2,1,0:T(8,128)(2,1)S(1)}, bf16[2,2,2,2,2,2,16,32]{7,6,5,4,3,2,1,0:T(8,128)(2,1)S(1)}, u32[]{:S(2)}, u32[]{:S(2)}) collective-permute-start(bf16[2,2,2,2,2,2,16,32]{7,6,5,4,3,2,1,0:T(8,128)(2,1)S(1)} %pad_maximum_fusion.22), channel_id=1, source_target_pairs={{0,2},{1,3},{2,0},{3,1},{4,6},{5,7},{6,4},{7,5},{8,10},{9,11},{10,... | collective-permute-start | bytes 196616 | tf_op jit(solution)/shard_map/ppermute | solution.py:29
  274.5 7.5 %collective-permute-start.33 = (f32[33,4,256]{2,1,0:T(4,128)S(1)}, f32[33,4,256]{2,1,0:T(4,128)S(1)}, u32[]{:S(2)}, u32[]{:S(2)}) collective-permute-start(f32[33,4,256]{2,1,0:T(4,128)S(1)} %get-tuple-element.101), channel_id=1, source_target_pairs={{4,0},{8,4},{12,8},{16,12},{20,16},{24,20},{28,24},{32,28},{36,32}... | collective-permute-start | bytes 405512 | tf_op jit(solution)/shard_map/ppermute | solution.py:44
  276.4 11.8 %collective-permute-start.32 = (f32[33,4,256]{2,1,0:T(4,128)S(1)}, f32[33,4,256]{2,1,0:T(4,128)S(1)}, u32[]{:S(2)}, u32[]{:S(2)}) collective-permute-start(f32[33,4,256]{2,1,0:T(4,128)S(1)} %get-tuple-element.100), channel_id=1, source_target_pairs={{0,4},{4,8},{8,12},{12,16},{16,20},{20,24},{24,28},{28,32},{32,36}... | collective-permute-start | bytes 405512 | tf_op jit(solution)/shard_map/ppermute | solution.py:43
  288.5 5.2 %collective-permute-start.35 = (f32[33,16,4]{2,1,0:T(8,128)S(1)}, f32[33,16,4]{2,1,0:T(8,128)S(1)}, u32[]{:S(2)}, u32[]{:S(2)}) collective-permute-start(f32[33,16,4]{2,1,0:T(8,128)S(1)} %get-tuple-element.85), channel_id=1, source_target_pairs={{0,3},{1,0},{2,1},{3,2},{4,7},{5,4},{6,5},{7,6},{8,11},{9,8},{10,9... | collective-permute-start | bytes 25352 | tf_op jit(solution)/shard_map/ppermute | solution.py:47
  288.6 9.6 %collective-permute-start.34 = (f32[33,16,4]{2,1,0:T(8,128)S(1)}, f32[33,16,4]{2,1,0:T(8,128)S(1)}, u32[]{:S(2)}, u32[]{:S(2)}) collective-permute-start(f32[33,16,4]{2,1,0:T(8,128)S(1)} %get-tuple-element.84), channel_id=1, source_target_pairs={{0,1},{1,2},{2,3},{3,0},{4,5},{5,6},{6,7},{7,4},{8,9},{9,10},{10,1... | collective-permute-start | bytes 25352 | tf_op jit(solution)/shard_map/ppermute | solution.py:46
  301.7 7.1 %collective-permute-start.45 = (f32[33,4,256]{2,1,0:T(4,128)S(1)}, f32[33,4,256]{2,1,0:T(4,128)S(1)}, u32[]{:S(2)}, u32[]{:S(2)}) collective-permute-start(f32[33,4,256]{2,1,0:T(4,128)S(1)} %get-tuple-element.99), channel_id=1, source_target_pairs={{4,0},{8,4},{12,8},{16,12},{20,16},{24,20},{28,24},{32,28},{36,32}... | collective-permute-start | bytes 405512 | tf_op jit(solution)/shard_map/ppermute | solution.py:44
  303.6 11.1 %collective-permute-start.44 = (f32[33,4,256]{2,1,0:T(4,128)S(1)}, f32[33,4,256]{2,1,0:T(4,128)S(1)}, u32[]{:S(2)}, u32[]{:S(2)}) collective-permute-start(f32[33,4,256]{2,1,0:T(4,128)S(1)} %get-tuple-element.98), channel_id=1, source_target_pairs={{0,4},{4,8},{8,12},{12,16},{16,20},{20,24},{24,28},{28,32},{32,36}... | collective-permute-start | bytes 405512 | tf_op jit(solution)/shard_map/ppermute | solution.py:43
  315.0 6.1 %collective-permute-start.47 = (f32[33,16,4]{2,1,0:T(8,128)S(1)}, f32[33,16,4]{2,1,0:T(8,128)S(1)}, u32[]{:S(2)}, u32[]{:S(2)}) collective-permute-start(f32[33,16,4]{2,1,0:T(8,128)S(1)} %get-tuple-element.83), channel_id=1, source_target_pairs={{0,3},{1,0},{2,1},{3,2},{4,7},{5,4},{6,5},{7,6},{8,11},{9,8},{10,9... | collective-permute-start | bytes 25352 | tf_op jit(solution)/shard_map/ppermute | solution.py:47
  315.1 8.8 %collective-permute-start.46 = (f32[33,16,4]{2,1,0:T(8,128)S(1)}, f32[33,16,4]{2,1,0:T(8,128)S(1)}, u32[]{:S(2)}, u32[]{:S(2)}) collective-permute-start(f32[33,16,4]{2,1,0:T(8,128)S(1)} %get-tuple-element.82), channel_id=1, source_target_pairs={{0,1},{1,2},{2,3},{3,0},{4,5},{5,6},{6,7},{7,4},{8,9},{9,10},{10,1... | collective-permute-start | bytes 25352 | tf_op jit(solution)/shard_map/ppermute | solution.py:46
  (37 other events, 343.1 us)
where the time goes:
time: 335 us; the launch traced here: 328 us
  waiting for transfers between devices  190 us (57%)
  starting transfers between devices  64.2 us (19%)
  other arithmetic  36.9 us (11%)
  local copies, waits for them, and re-layouts  28.8 us (9%)
  matrix products  6.17 us (2%)
    ppermute x32, waiting for transfers between devices, gather_columns(): other = lax.ppermute(held, ('blk', 'circ'), pairs)  130 us
    ppermute x32, starting transfers between devices, gather_columns(): other = lax.ppermute(held, ('blk', 'circ'), pairs)  35.4 us
    ppermute x4, waiting for transfers between devices, with_halo(): lax.ppermute(field[:, -width:, :], 'blk', [(i, i + 1) for i in range(rows...  25.1 us
    ppermute x4, waiting for transfers between devices, with_halo(): lax.ppermute(field[:, :, -width:], 'circ', [(i, (i + 1) % cols) for i in...  15.8 us
    ppermute x4, waiting for transfers between devices, with_halo(): lax.ppermute(field[:, :, :width], 'circ', [(i, (i - 1) % cols) for i in r...  15.7 us
    ppermute x4, starting transfers between devices, with_halo(): lax.ppermute(field[:, -width:, :], 'blk', [(i, i + 1) for i in range(rows...  13.9 us
    ppermute x4, starting transfers between devices, with_halo(): lax.ppermute(field[:, :width, :], 'blk', [(i + 1, i) for i in range(rows...  11.3 us
    another operation x60, other arithmetic, gather_columns(): held = jnp.stack([first, second], axis=0)  7.87 us
  transfers between devices with their start and end apart: 48, of which 45 were waited for; matrix products, arithmetic and copies ran while one was open for 4% of the time, Pallas kernels for 0%

commit v1 on v0

--- a/solution.py
+++ b/solution.py
@@ -20,17 +20,13 @@
 
 def gather_columns(block):
     count = lax.axis_size("blk") * lax.axis_size("circ")
-    index = lax.axis_index("blk") * lax.axis_size("circ") + lax.axis_index("circ")
     bits = count.bit_length() - 1
     held = block
     for level in reversed(range(bits)):
         bit = 1 << level
         pairs = [(i, i ^ bit) for i in range(count)]
         other = lax.ppermute(held, ("blk", "circ"), pairs)
-        low = (index & bit) == 0
-        first = jnp.where(low, held, other)
-        second = jnp.where(low, other, held)
-        held = jnp.stack([first, second], axis=0)
+        held = jnp.stack([held, other], axis=0)
     order = list(reversed(range(bits)))
     held = jnp.transpose(held, order + [bits, bits + 1])
     held = held.reshape((count,) + block.shape)

time: 335 us -> 327 us (0.976)
  waiting for transfers between devices: 190 us -> 178 us
  starting transfers between devices: 64.2 us -> 68 us
    ppermute x32, waiting for transfers between devices: 130 us -> 119 us  [gather_columns(): other = lax.ppermute(held, ('blk', 'circ'), pairs)]
    ppermute x32, starting transfers between devices: 35.4 us -> 38.8 us  [gather_columns(): other = lax.ppermute(held, ('blk', 'circ'), pairs)]
    another operation x62 -> x31, other arithmetic: 13.3 us -> 10.4 us  [the longest x60 7.87 us: gather_columns(): held = jnp.stack([first, second], axis=0)]
  transfers between devices with their start and end apart: 48 -> 48, of which waited for: 45 -> 42; matrix products, arithmetic and copies ran while one was open for 4% -> 5% of each run, Pallas kernels for 0% -> 0%
where the time goes in v1:
time: 327 us; the launch traced here: 321 us
  waiting for transfers between devices  178 us (54%)
  starting transfers between devices  68 us (21%)
  other arithmetic  36.3 us (11%)
  local copies, waits for them, and re-layouts  29.8 us (9%)
  matrix products  6.48 us (2%)
    ppermute x32, waiting for transfers between devices, gather_columns(): other = lax.ppermute(held, ('blk', 'circ'), pairs)  119 us
    ppermute x32, starting transfers between devices, gather_columns(): other = lax.ppermute(held, ('blk', 'circ'), pairs)  38.8 us
    ppermute x4, waiting for transfers between devices, with_halo(): lax.ppermute(field[:, -width:, :], 'blk', [(i, i + 1) for i in range(rows...  25 us
    ppermute x4, waiting for transfers between devices, with_halo(): lax.ppermute(field[:, :, :width], 'circ', [(i, (i - 1) % cols) for i in r...  17.2 us
    ppermute x4, waiting for transfers between devices, with_halo(): lax.ppermute(field[:, :, -width:], 'circ', [(i, (i + 1) % cols) for i in...  14.3 us
    ppermute x4, starting transfers between devices, with_halo(): lax.ppermute(field[:, -width:, :], 'blk', [(i, i + 1) for i in range(rows...  13.8 us
    ppermute x4, starting transfers between devices, with_halo(): lax.ppermute(field[:, :width, :], 'blk', [(i + 1, i) for i in range(rows...  11.4 us
  transfers between devices with their start and end apart: 48, of which 42 were waited for; matrix products, arithmetic and copies ran while one was open for 5% of the time, Pallas kernels for 0%

profile of v1, /device:TPU:128, one launch (start us, length us, event | category | flops | bytes accessed | tf_op | source)
XLA Modules:
  0.0 321.4 jit_solution(15151449725649033709)
XLA Ops:
  1.8 7.1 %collective-permute-done = f32[20,32]{1,0:T(8,128)S(1)} collective-permute-done((f32[20,32]{1,0:T(8,128)S(1)}, f32[20,32]{1,0:T(8,128)S(1)}, u32[]{:S(2)}, u32[]{:S(2)}) %collective-permute-start) | collective-permute-done | bytes 2592 | tf_op jit(solution)/shard_map/ppermute | solution.py:28
  10.6 3.2 collective-permute-done.1
  22.7 3.3 %collective-permute-start.4 = (f32[2,2,2,2,20,32]{5,3,4,2,1,0:T(2,128)S(1)}, f32[2,2,2,2,20,32]{5,3,4,2,1,0:T(2,128)S(1)}, u32[]{:S(2)}, u32[]{:S(2)}) collective-permute-start(f32[2,2,2,2,20,32]{5,3,4,2,1,0:T(2,128)S(1)} %get-tuple-element.115), channel_id=1, source_target_pairs={{0,8},{1,9},{2,10},{3,11},{4,12},{5,13},{6,14},{7,15},{8,0},{9,1},... | collective-permute-start | bytes 122888 | tf_op jit(solution)/shard_map/ppermute | solution.py:28
  26.7 3.8 %collective-permute-done.4 = f32[2,2,2,2,20,32]{5,3,4,2,1,0:T(2,128)S(1)} collective-permute-done((f32[2,2,2,2,20,32]{5,3,4,2,1,0:T(2,128)S(1)}, f32[2,2,2,2,20,32]{5,3,4,2,1,0:T(2,128)S(1)}, u32[]{:S(2)}, u32[]{:S(2)}) %collective-permute-start.4) | collective-permute-done | bytes 40992 | tf_op jit(solution)/shard_map/ppermute | solution.py:28
  41.8 9.0 %collective-permute-done.6 = f32[2,2,2,2,2,2,20,32]{7,5,6,4,3,2,1,0:T(2,128)S(1)} collective-permute-done((f32[2,2,2,2,2,2,20,32]{7,5,6,4,3,2,1,0:T(2,128)S(1)}, f32[2,2,2,2,2,2,20,32]{7,5,6,4,3,2,1,0:T(2,128)S(1)}, u32[]{:S(2)}, u32[]{:S(2)}) %collective-permute-start.6) | collective-permute-done | bytes 163872 | tf_op jit(solution)/shard_map/ppermute | solution.py:28
  63.5 5.3 %multiply_convert_fusion = (bf16[32,8192]{1,0:T(8,128)(2,1)S(1)}, bf16[32,8192]{1,0:T(8,128)(2,1)S(1)}, bf16[32,8192]{1,0:T(8,128)(2,1)S(1)}, bf16[32,8192]{1,0:T(8,128)(2,1)S(1)}) fusion(f32[8192]{0:T(1024)S(1)} %div.69, f32[8192]{0:T(1024)S(1)} %sub.275, f32[32]{0:T(128)S(1)} %get-tuple-element.173, f32[8192]{0:T(1024)S(1)} %sub.270, ...), kind=kLoop, calls=%fused_computation.38 | loop fusion | flops 8650752 | bytes 2261632 | tf_op jit(solution)/shard_map/convert.1
  70.3 7.0 %collective-permute-done.12 = bf16[16,32]{1,0:T(8,128)(2,1)S(1)} collective-permute-done((bf16[16,32]{1,0:T(8,128)(2,1)S(1)}, bf16[16,32]{1,0:T(8,128)(2,1)S(1)}, u32[]{:S(2)}, u32[]{:S(2)}) %collective-permute-start.12) | collective-permute-done | bytes 1056 | tf_op jit(solution)/shard_map/ppermute | solution.py:28
  89.7 4.3 %collective-permute-start.16 = (bf16[2,2,2,2,16,32]{5,4,3,2,1,0:T(8,128)(2,1)S(1)}, bf16[2,2,2,2,16,32]{5,4,3,2,1,0:T(8,128)(2,1)S(1)}, u32[]{:S(2)}, u32[]{:S(2)}) collective-permute-start(bf16[2,2,2,2,16,32]{5,4,3,2,1,0:T(8,128)(2,1)S(1)} %get-tuple-element.133), channel_id=1, source_target_pairs={{0,8},{1,9},{2,10},{3,11},{4,12},{5,13},{6,14},{7,15},{8,0},{9,1},... | collective-permute-start | bytes 49160 | tf_op jit(solution)/shard_map/ppermute | solution.py:28
  104.8 4.6 %collective-permute-done.18 = bf16[2,2,2,2,2,2,16,32]{7,6,5,4,3,2,1,0:T(8,128)(2,1)S(1)} collective-permute-done((bf16[2,2,2,2,2,2,16,32]{7,6,5,4,3,2,1,0:T(8,128)(2,1)S(1)}, bf16[2,2,2,2,2,2,16,32]{7,6,5,4,3,2,1,0:T(8,128)(2,1)S(1)}, u32[]{:S(2)}, u32[]{:S(2)}) %collective-permute-start.18) | collective-permute-done | bytes 65568 | tf_op jit(solution)/shard_map/ppermute | solution.py:28
  121.7 5.6 %collective-permute-start.9 = (f32[33,4,256]{2,1,0:T(4,128)S(1)}, f32[33,4,256]{2,1,0:T(4,128)S(1)}, u32[]{:S(2)}, u32[]{:S(2)}) collective-permute-start(f32[33,4,256]{2,1,0:T(4,128)S(1)} %get-tuple-element.97), channel_id=1, source_target_pairs={{4,0},{8,4},{12,8},{16,12},{20,16},{24,20},{28,24},{32,28},{36,32}... | collective-permute-start | bytes 405512 | tf_op jit(solution)/shard_map/ppermute | solution.py:40
  130.8 8.3 %collective-permute-done.8 = f32[33,4,256]{2,1,0:T(4,128)S(1)} collective-permute-done((f32[33,4,256]{2,1,0:T(4,128)S(1)}, f32[33,4,256]{2,1,0:T(4,128)S(1)}, u32[]{:S(2)}, u32[]{:S(2)}) %collective-permute-start.8) | collective-permute-done | bytes 135200 | tf_op jit(solution)/shard_map/ppermute | solution.py:39
  141.7 5.7 %collective-permute-done.11 = f32[33,16,4]{2,1,0:T(8,128)S(1)} collective-permute-done((f32[33,16,4]{2,1,0:T(8,128)S(1)}, f32[33,16,4]{2,1,0:T(8,128)S(1)}, u32[]{:S(2)}, u32[]{:S(2)}) %collective-permute-start.11) | collective-permute-done | bytes 8480 | tf_op jit(solution)/shard_map/ppermute | solution.py:43
  154.8 7.5 %collective-permute-done.24 = bf16[16,32]{1,0:T(8,128)(2,1)S(1)} collective-permute-done((bf16[16,32]{1,0:T(8,128)(2,1)S(1)}, bf16[16,32]{1,0:T(8,128)(2,1)S(1)}, u32[]{:S(2)}, u32[]{:S(2)}) %collective-permute-start.24) | collective-permute-done | bytes 1056 | tf_op jit(solution)/shard_map/ppermute | solution.py:28
  163.5 3.4 %collective-permute-done.25 = bf16[2,16,32]{2,1,0:T(8,128)(2,1)S(1)} collective-permute-done((bf16[2,16,32]{2,1,0:T(8,128)(2,1)S(1)}, bf16[2,16,32]{2,1,0:T(8,128)(2,1)S(1)}, u32[]{:S(2)}, u32[]{:S(2)}) %collective-permute-start.25) | collective-permute-done | bytes 2080 | tf_op jit(solution)/shard_map/ppermute | solution.py:28
  170.8 3.9 %collective-permute-done.27 = bf16[2,2,2,16,32]{4,3,2,1,0:T(8,128)(2,1)S(1)} collective-permute-done((bf16[2,2,2,16,32]{4,3,2,1,0:T(8,128)(2,1)S(1)}, bf16[2,2,2,16,32]{4,3,2,1,0:T(8,128)(2,1)S(1)}, u32[]{:S(2)}, u32[]{:S(2)}) %collective-permute-start.27) | collective-permute-done | bytes 8224 | tf_op jit(solution)/shard_map/ppermute | solution.py:28
  174.9 5.7 %collective-permute-done.28 = bf16[2,2,2,2,16,32]{5,4,3,2,1,0:T(8,128)(2,1)S(1)} collective-permute-done((bf16[2,2,2,2,16,32]{5,4,3,2,1,0:T(8,128)(2,1)S(1)}, bf16[2,2,2,2,16,32]{5,4,3,2,1,0:T(8,128)(2,1)S(1)}, u32[]{:S(2)}, u32[]{:S(2)}) %collective-permute-start.28) | collective-permute-done | bytes 16416 | tf_op jit(solution)/shard_map/ppermute | solution.py:28
  182.7 3.9 %collective-permute-start.20 = (f32[33,4,256]{2,1,0:T(4,128)S(1)}, f32[33,4,256]{2,1,0:T(4,128)S(1)}, u32[]{:S(2)}, u32[]{:S(2)}) collective-permute-start(f32[33,4,256]{2,1,0:T(4,128)S(1)} %get-tuple-element.94), channel_id=1, source_target_pairs={{0,4},{4,8},{8,12},{12,16},{16,20},{20,24},{24,28},{28,32},{32,36}... | collective-permute-start | bytes 405512 | tf_op jit(solution)/shard_map/ppermute | solution.py:39
  189.3 4.5 %collective-permute-done.20 = f32[33,4,256]{2,1,0:T(4,128)S(1)} collective-permute-done((f32[33,4,256]{2,1,0:T(4,128)S(1)}, f32[33,4,256]{2,1,0:T(4,128)S(1)}, u32[]{:S(2)}, u32[]{:S(2)}) %collective-permute-start.20) | collective-permute-done | bytes 135200 | tf_op jit(solution)/shard_map/ppermute | solution.py:39
  198.9 5.2 %collective-permute-done.22 = f32[33,16,4]{2,1,0:T(8,128)S(1)} collective-permute-done((f32[33,16,4]{2,1,0:T(8,128)S(1)}, f32[33,16,4]{2,1,0:T(8,128)S(1)}, u32[]{:S(2)}, u32[]{:S(2)}) %collective-permute-start.22) | collective-permute-done | bytes 8480 | tf_op jit(solution)/shard_map/ppermute | solution.py:42
  216.1 7.5 %collective-permute-done.36 = bf16[16,32]{1,0:T(8,128)(2,1)S(1)} collective-permute-done((bf16[16,32]{1,0:T(8,128)(2,1)S(1)}, bf16[16,32]{1,0:T(8,128)(2,1)S(1)}, u32[]{:S(2)}, u32[]{:S(2)}) %collective-permute-start.36) | collective-permute-done | bytes 1056 | tf_op jit(solution)/shard_map/ppermute | solution.py:28
  224.3 3.9 %collective-permute-done.37 = bf16[2,16,32]{2,1,0:T(8,128)(2,1)S(1)} collective-permute-done((bf16[2,16,32]{2,1,0:T(8,128)(2,1)S(1)}, bf16[2,16,32]{2,1,0:T(8,128)(2,1)S(1)}, u32[]{:S(2)}, u32[]{:S(2)}) %collective-permute-start.37) | collective-permute-done | bytes 2080 | tf_op jit(solution)/shard_map/ppermute | solution.py:28
  232.1 3.9 %collective-permute-done.39 = bf16[2,2,2,16,32]{4,3,2,1,0:T(8,128)(2,1)S(1)} collective-permute-done((bf16[2,2,2,16,32]{4,3,2,1,0:T(8,128)(2,1)S(1)}, bf16[2,2,2,16,32]{4,3,2,1,0:T(8,128)(2,1)S(1)}, u32[]{:S(2)}, u32[]{:S(2)}) %collective-permute-start.39) | collective-permute-done | bytes 8224 | tf_op jit(solution)/shard_map/ppermute | solution.py:28
  236.1 5.8 %collective-permute-done.40 = bf16[2,2,2,2,16,32]{5,4,3,2,1,0:T(8,128)(2,1)S(1)} collective-permute-done((bf16[2,2,2,2,16,32]{5,4,3,2,1,0:T(8,128)(2,1)S(1)}, bf16[2,2,2,2,16,32]{5,4,3,2,1,0:T(8,128)(2,1)S(1)}, u32[]{:S(2)}, u32[]{:S(2)}) %collective-permute-start.40) | collective-permute-done | bytes 16416 | tf_op jit(solution)/shard_map/ppermute | solution.py:28
  242.0 5.0 %collective-permute-done.41 = bf16[2,2,2,2,2,16,32]{6,5,4,3,2,1,0:T(8,128)(2,1)S(1)} collective-permute-done((bf16[2,2,2,2,2,16,32]{6,5,4,3,2,1,0:T(8,128)(2,1)S(1)}, bf16[2,2,2,2,2,16,32]{6,5,4,3,2,1,0:T(8,128)(2,1)S(1)}, u32[]{:S(2)}, u32[]{:S(2)}) %collective-permute-start.41) | collective-permute-done | bytes 32800 | tf_op jit(solution)/shard_map/ppermute | solution.py:28
  248.4 7.0 %collective-permute-done.42 = bf16[2,2,2,2,2,2,16,32]{7,6,5,4,3,2,1,0:T(8,128)(2,1)S(1)} collective-permute-done((bf16[2,2,2,2,2,2,16,32]{7,6,5,4,3,2,1,0:T(8,128)(2,1)S(1)}, bf16[2,2,2,2,2,2,16,32]{7,6,5,4,3,2,1,0:T(8,128)(2,1)S(1)}, u32[]{:S(2)}, u32[]{:S(2)}) %collective-permute-start.42) | collective-permute-done | bytes 65568 | tf_op jit(solution)/shard_map/ppermute | solution.py:28
  269.0 3.9 %collective-permute-start.32 = (f32[33,4,256]{2,1,0:T(4,128)S(1)}, f32[33,4,256]{2,1,0:T(4,128)S(1)}, u32[]{:S(2)}, u32[]{:S(2)}) collective-permute-start(f32[33,4,256]{2,1,0:T(4,128)S(1)} %get-tuple-element.92), channel_id=1, source_target_pairs={{0,4},{4,8},{8,12},{12,16},{16,20},{20,24},{24,28},{28,32},{32,36}... | collective-permute-start | bytes 405512 | tf_op jit(solution)/shard_map/ppermute | solution.py:39
  274.5 6.2 %collective-permute-done.32 = f32[33,4,256]{2,1,0:T(4,128)S(1)} collective-permute-done((f32[33,4,256]{2,1,0:T(4,128)S(1)}, f32[33,4,256]{2,1,0:T(4,128)S(1)}, u32[]{:S(2)}, u32[]{:S(2)}) %collective-permute-start.32) | collective-permute-done | bytes 135200 | tf_op jit(solution)/shard_map/ppermute | solution.py:39
  281.8 5.9 %collective-permute-done.35 = f32[33,16,4]{2,1,0:T(8,128)S(1)} collective-permute-done((f32[33,16,4]{2,1,0:T(8,128)S(1)}, f32[33,16,4]{2,1,0:T(8,128)S(1)}, u32[]{:S(2)}, u32[]{:S(2)}) %collective-permute-start.35) | collective-permute-done | bytes 8480 | tf_op jit(solution)/shard_map/ppermute | solution.py:43
  296.3 4.1 %collective-permute-start.44 = (f32[33,4,256]{2,1,0:T(4,128)S(1)}, f32[33,4,256]{2,1,0:T(4,128)S(1)}, u32[]{:S(2)}, u32[]{:S(2)}) collective-permute-start(f32[33,4,256]{2,1,0:T(4,128)S(1)} %get-tuple-element.90), channel_id=1, source_target_pairs={{0,4},{4,8},{8,12},{12,16},{16,20},{20,24},{24,28},{28,32},{32,36}... | collective-permute-start | bytes 405512 | tf_op jit(solution)/shard_map/ppermute | solution.py:39
  301.5 6.0 %collective-permute-done.44 = f32[33,4,256]{2,1,0:T(4,128)S(1)} collective-permute-done((f32[33,4,256]{2,1,0:T(4,128)S(1)}, f32[33,4,256]{2,1,0:T(4,128)S(1)}, u32[]{:S(2)}, u32[]{:S(2)}) %collective-permute-start.44) | collective-permute-done | bytes 135200 | tf_op jit(solution)/shard_map/ppermute | solution.py:39
  309.0 4.2 %collective-permute-done.47 = f32[33,16,4]{2,1,0:T(8,128)S(1)} collective-permute-done((f32[33,16,4]{2,1,0:T(8,128)S(1)}, f32[33,16,4]{2,1,0:T(8,128)S(1)}, u32[]{:S(2)}, u32[]{:S(2)}) %collective-permute-start.47) | collective-permute-done | bytes 8480 | tf_op jit(solution)/shard_map/ppermute | solution.py:43
  313.2 3.9 %collective-permute-done.46 = f32[33,16,4]{2,1,0:T(8,128)S(1)} collective-permute-done((f32[33,16,4]{2,1,0:T(8,128)S(1)}, f32[33,16,4]{2,1,0:T(8,128)S(1)}, u32[]{:S(2)}, u32[]{:S(2)}) %collective-permute-start.46) | collective-permute-done | bytes 8480 | tf_op jit(solution)/shard_map/ppermute | solution.py:42
  (367 shorter events, 150.4 us)
Async XLA Ops:
  1.4 7.6 %collective-permute-start = (f32[20,32]{1,0:T(8,128)S(1)}, f32[20,32]{1,0:T(8,128)S(1)}, u32[]{:S(2)}, u32[]{:S(2)}) collective-permute-start(f32[20,32]{1,0:T(8,128)S(1)} %get-tuple-element.159), channel_id=1, source_target_pairs={{0,128},{1,129},{2,130},{3,131},{4,132},{5,133},{6,134},{7,135},{8... | collective-permute-start | bytes 7688 | tf_op jit(solution)/shard_map/ppermute | solution.py:28
  22.7 7.9 %collective-permute-start.4 = (f32[2,2,2,2,20,32]{5,3,4,2,1,0:T(2,128)S(1)}, f32[2,2,2,2,20,32]{5,3,4,2,1,0:T(2,128)S(1)}, u32[]{:S(2)}, u32[]{:S(2)}) collective-permute-start(f32[2,2,2,2,20,32]{5,3,4,2,1,0:T(2,128)S(1)} %get-tuple-element.115), channel_id=1, source_target_pairs={{0,8},{1,9},{2,10},{3,11},{4,12},{5,13},{6,14},{7,15},{8,0},{9,1},... | collective-permute-start | bytes 122888 | tf_op jit(solution)/shard_map/ppermute | solution.py:28
  30.8 7.5 %collective-permute-start.5 = (f32[2,2,2,2,2,20,32]{6,4,5,3,2,1,0:T(2,128)S(1)}, f32[2,2,2,2,2,20,32]{6,4,5,3,2,1,0:T(2,128)S(1)}, u32[]{:S(2)}, u32[]{:S(2)}) collective-permute-start(f32[2,2,2,2,2,20,32]{6,4,5,3,2,1,0:T(2,128)S(1)} %get-tuple-element.89), channel_id=1, source_target_pairs={{0,4},{1,5},{2,6},{3,7},{4,0},{5,1},{6,2},{7,3},{8,12},{9,13},{10,... | collective-permute-start | bytes 245768 | tf_op jit(solution)/shard_map/ppermute | solution.py:28
  38.7 12.2 %collective-permute-start.6 = (f32[2,2,2,2,2,2,20,32]{7,5,6,4,3,2,1,0:T(2,128)S(1)}, f32[2,2,2,2,2,2,20,32]{7,5,6,4,3,2,1,0:T(2,128)S(1)}, u32[]{:S(2)}, u32[]{:S(2)}) collective-permute-start(f32[2,2,2,2,2,2,20,32]{7,5,6,4,3,2,1,0:T(2,128)S(1)} %get-tuple-element.73), channel_id=1, source_target_pairs={{0,2},{1,3},{2,0},{3,1},{4,6},{5,7},{6,4},{7,5},{8,10},{9,11},{10,... | collective-permute-start | bytes 491528 | tf_op jit(solution)/shard_map/ppermute | solution.py:28
  69.7 7.5 %collective-permute-start.12 = (bf16[16,32]{1,0:T(8,128)(2,1)S(1)}, bf16[16,32]{1,0:T(8,128)(2,1)S(1)}, u32[]{:S(2)}, u32[]{:S(2)}) collective-permute-start(bf16[16,32]{1,0:T(8,128)(2,1)S(1)} %get-tuple-element.167), channel_id=1, source_target_pairs={{0,128},{1,129},{2,130},{3,131},{4,132},{5,133},{6,134},{7,135},{8... | collective-permute-start | bytes 3080 | tf_op jit(solution)/shard_map/ppermute | solution.py:28
  89.7 6.7 %collective-permute-start.16 = (bf16[2,2,2,2,16,32]{5,4,3,2,1,0:T(8,128)(2,1)S(1)}, bf16[2,2,2,2,16,32]{5,4,3,2,1,0:T(8,128)(2,1)S(1)}, u32[]{:S(2)}, u32[]{:S(2)}) collective-permute-start(bf16[2,2,2,2,16,32]{5,4,3,2,1,0:T(8,128)(2,1)S(1)} %get-tuple-element.133), channel_id=1, source_target_pairs={{0,8},{1,9},{2,10},{3,11},{4,12},{5,13},{6,14},{7,15},{8,0},{9,1},... | collective-permute-start | bytes 49160 | tf_op jit(solution)/shard_map/ppermute | solution.py:28
  96.4 5.1 %collective-permute-start.17 = (bf16[2,2,2,2,2,16,32]{6,5,4,3,2,1,0:T(8,128)(2,1)S(1)}, bf16[2,2,2,2,2,16,32]{6,5,4,3,2,1,0:T(8,128)(2,1)S(1)}, u32[]{:S(2)}, u32[]{:S(2)}) collective-permute-start(bf16[2,2,2,2,2,16,32]{6,5,4,3,2,1,0:T(8,128)(2,1)S(1)} %get-tuple-element.125), channel_id=1, source_target_pairs={{0,4},{1,5},{2,6},{3,7},{4,0},{5,1},{6,2},{7,3},{8,12},{9,13},{10,... | collective-permute-start | bytes 98312 | tf_op jit(solution)/shard_map/ppermute | solution.py:28
  101.5 8.0 %collective-permute-start.18 = (bf16[2,2,2,2,2,2,16,32]{7,6,5,4,3,2,1,0:T(8,128)(2,1)S(1)}, bf16[2,2,2,2,2,2,16,32]{7,6,5,4,3,2,1,0:T(8,128)(2,1)S(1)}, u32[]{:S(2)}, u32[]{:S(2)}) collective-permute-start(bf16[2,2,2,2,2,2,16,32]{7,6,5,4,3,2,1,0:T(8,128)(2,1)S(1)} %get-tuple-element.109), channel_id=1, source_target_pairs={{0,2},{1,3},{2,0},{3,1},{4,6},{5,7},{6,4},{7,5},{8,10},{9,11},{10,... | collective-permute-start | bytes 196616 | tf_op jit(solution)/shard_map/ppermute | solution.py:28
  121.7 9.1 %collective-permute-start.9 = (f32[33,4,256]{2,1,0:T(4,128)S(1)}, f32[33,4,256]{2,1,0:T(4,128)S(1)}, u32[]{:S(2)}, u32[]{:S(2)}) collective-permute-start(f32[33,4,256]{2,1,0:T(4,128)S(1)} %get-tuple-element.97), channel_id=1, source_target_pairs={{4,0},{8,4},{12,8},{16,12},{20,16},{24,20},{28,24},{32,28},{36,32}... | collective-permute-start | bytes 405512 | tf_op jit(solution)/shard_map/ppermute | solution.py:40
  127.3 11.8 %collective-permute-start.8 = (f32[33,4,256]{2,1,0:T(4,128)S(1)}, f32[33,4,256]{2,1,0:T(4,128)S(1)}, u32[]{:S(2)}, u32[]{:S(2)}) collective-permute-start(f32[33,4,256]{2,1,0:T(4,128)S(1)} %get-tuple-element.96), channel_id=1, source_target_pairs={{0,4},{4,8},{8,12},{12,16},{16,20},{20,24},{24,28},{28,32},{32,36}... | collective-permute-start | bytes 405512 | tf_op jit(solution)/shard_map/ppermute | solution.py:39
  139.4 7.9 %collective-permute-start.11 = (f32[33,16,4]{2,1,0:T(8,128)S(1)}, f32[33,16,4]{2,1,0:T(8,128)S(1)}, u32[]{:S(2)}, u32[]{:S(2)}) collective-permute-start(f32[33,16,4]{2,1,0:T(8,128)S(1)} %get-tuple-element.81), channel_id=1, source_target_pairs={{0,3},{1,0},{2,1},{3,2},{4,7},{5,4},{6,5},{7,6},{8,11},{9,8},{10,9... | collective-permute-start | bytes 25352 | tf_op jit(solution)/shard_map/ppermute | solution.py:43
  141.2 8.4 %collective-permute-start.10 = (f32[33,16,4]{2,1,0:T(8,128)S(1)}, f32[33,16,4]{2,1,0:T(8,128)S(1)}, u32[]{:S(2)}, u32[]{:S(2)}) collective-permute-start(f32[33,16,4]{2,1,0:T(8,128)S(1)} %get-tuple-element.80), channel_id=1, source_target_pairs={{0,1},{1,2},{2,3},{3,0},{4,5},{5,6},{6,7},{7,4},{8,9},{9,10},{10,1... | collective-permute-start | bytes 25352 | tf_op jit(solution)/shard_map/ppermute | solution.py:42
  154.8 7.5 %collective-permute-start.24 = (bf16[16,32]{1,0:T(8,128)(2,1)S(1)}, bf16[16,32]{1,0:T(8,128)(2,1)S(1)}, u32[]{:S(2)}, u32[]{:S(2)}) collective-permute-start(bf16[16,32]{1,0:T(8,128)(2,1)S(1)} %get-tuple-element.51), channel_id=1, source_target_pairs={{0,128},{1,129},{2,130},{3,131},{4,132},{5,133},{6,134},{7,135},{8... | collective-permute-start | bytes 3080 | tf_op jit(solution)/shard_map/ppermute | solution.py:28
  174.7 5.9 %collective-permute-start.28 = (bf16[2,2,2,2,16,32]{5,4,3,2,1,0:T(8,128)(2,1)S(1)}, bf16[2,2,2,2,16,32]{5,4,3,2,1,0:T(8,128)(2,1)S(1)}, u32[]{:S(2)}, u32[]{:S(2)}) collective-permute-start(bf16[2,2,2,2,16,32]{5,4,3,2,1,0:T(8,128)(2,1)S(1)} %get-tuple-element.131), channel_id=1, source_target_pairs={{0,8},{1,9},{2,10},{3,11},{4,12},{5,13},{6,14},{7,15},{8,0},{9,1},... | collective-permute-start | bytes 49160 | tf_op jit(solution)/shard_map/ppermute | solution.py:28
  180.6 6.0 %collective-permute-start.29 = (bf16[2,2,2,2,2,16,32]{6,5,4,3,2,1,0:T(8,128)(2,1)S(1)}, bf16[2,2,2,2,2,16,32]{6,5,4,3,2,1,0:T(8,128)(2,1)S(1)}, u32[]{:S(2)}, u32[]{:S(2)}) collective-permute-start(bf16[2,2,2,2,2,16,32]{6,5,4,3,2,1,0:T(8,128)(2,1)S(1)} %get-tuple-element.123), channel_id=1, source_target_pairs={{0,4},{1,5},{2,6},{3,7},{4,0},{5,1},{6,2},{7,3},{8,12},{9,13},{10,... | collective-permute-start | bytes 98312 | tf_op jit(solution)/shard_map/ppermute | solution.py:28
  180.8 8.6 %collective-permute-start.21 = (f32[33,4,256]{2,1,0:T(4,128)S(1)}, f32[33,4,256]{2,1,0:T(4,128)S(1)}, u32[]{:S(2)}, u32[]{:S(2)}) collective-permute-start(f32[33,4,256]{2,1,0:T(4,128)S(1)} %get-tuple-element.95), channel_id=1, source_target_pairs={{4,0},{8,4},{12,8},{16,12},{20,16},{24,20},{28,24},{32,28},{36,32}... | collective-permute-start | bytes 405512 | tf_op jit(solution)/shard_map/ppermute | solution.py:40
  182.7 11.1 %collective-permute-start.20 = (f32[33,4,256]{2,1,0:T(4,128)S(1)}, f32[33,4,256]{2,1,0:T(4,128)S(1)}, u32[]{:S(2)}, u32[]{:S(2)}) collective-permute-start(f32[33,4,256]{2,1,0:T(4,128)S(1)} %get-tuple-element.94), channel_id=1, source_target_pairs={{0,4},{4,8},{8,12},{12,16},{16,20},{20,24},{24,28},{28,32},{32,36}... | collective-permute-start | bytes 405512 | tf_op jit(solution)/shard_map/ppermute | solution.py:39
  186.7 8.0 %collective-permute-start.30 = (bf16[2,2,2,2,2,2,16,32]{7,6,5,4,3,2,1,0:T(8,128)(2,1)S(1)}, bf16[2,2,2,2,2,2,16,32]{7,6,5,4,3,2,1,0:T(8,128)(2,1)S(1)}, u32[]{:S(2)}, u32[]{:S(2)}) collective-permute-start(bf16[2,2,2,2,2,2,16,32]{7,6,5,4,3,2,1,0:T(8,128)(2,1)S(1)} %get-tuple-element.105), channel_id=1, source_target_pairs={{0,2},{1,3},{2,0},{3,1},{4,6},{5,7},{6,4},{7,5},{8,10},{9,11},{10,... | collective-permute-start | bytes 196616 | tf_op jit(solution)/shard_map/ppermute | solution.py:28
  194.2 9.9 %collective-permute-start.22 = (f32[33,16,4]{2,1,0:T(8,128)S(1)}, f32[33,16,4]{2,1,0:T(8,128)S(1)}, u32[]{:S(2)}, u32[]{:S(2)}) collective-permute-start(f32[33,16,4]{2,1,0:T(8,128)S(1)} %get-tuple-element.78), channel_id=1, source_target_pairs={{0,1},{1,2},{2,3},{3,0},{4,5},{5,6},{6,7},{7,4},{8,9},{9,10},{10,1... | collective-permute-start | bytes 25352 | tf_op jit(solution)/shard_map/ppermute | solution.py:42
  194.8 13.9 %collective-permute-start.31 = (bf16[2,2,2,2,2,2,2,16,32]{8,7,6,5,4,3,2,1,0:T(8,128)(2,1)S(1)}, bf16[2,2,2,2,2,2,2,16,32]{8,7,6,5,4,3,2,1,0:T(8,128)(2,1)S(1)}, u32[]{:S(2)}, u32[]{:S(2)}) collective-permute-start(bf16[2,2,2,2,2,2,2,16,32]{8,7,6,5,4,3,2,1,0:T(8,128)(2,1)S(1)} %get-tuple-element.85), channel_id=1, source_target_pairs={{0,1},{1,0},{2,3},{3,2},{4,5},{5,4},{6,7},{7,6},{8,9},{9,8},{10,11... | collective-permute-start | bytes 393224 | tf_op jit(solution)/shard_map/ppermute | solution.py:28
  216.0 7.5 %collective-permute-start.36 = (bf16[16,32]{1,0:T(8,128)(2,1)S(1)}, bf16[16,32]{1,0:T(8,128)(2,1)S(1)}, u32[]{:S(2)}, u32[]{:S(2)}) collective-permute-start(bf16[16,32]{1,0:T(8,128)(2,1)S(1)} %get-tuple-element.161), channel_id=1, source_target_pairs={{0,128},{1,129},{2,130},{3,131},{4,132},{5,133},{6,134},{7,135},{8... | collective-permute-start | bytes 3080 | tf_op jit(solution)/shard_map/ppermute | solution.py:28
  236.0 5.9 %collective-permute-start.40 = (bf16[2,2,2,2,16,32]{5,4,3,2,1,0:T(8,128)(2,1)S(1)}, bf16[2,2,2,2,16,32]{5,4,3,2,1,0:T(8,128)(2,1)S(1)}, u32[]{:S(2)}, u32[]{:S(2)}) collective-permute-start(bf16[2,2,2,2,16,32]{5,4,3,2,1,0:T(8,128)(2,1)S(1)} %get-tuple-element.129), channel_id=1, source_target_pairs={{0,8},{1,9},{2,10},{3,11},{4,12},{5,13},{6,14},{7,15},{8,0},{9,1},... | collective-permute-start | bytes 49160 | tf_op jit(solution)/shard_map/ppermute | solution.py:28
  241.9 5.1 %collective-permute-start.41 = (bf16[2,2,2,2,2,16,32]{6,5,4,3,2,1,0:T(8,128)(2,1)S(1)}, bf16[2,2,2,2,2,16,32]{6,5,4,3,2,1,0:T(8,128)(2,1)S(1)}, u32[]{:S(2)}, u32[]{:S(2)}) collective-permute-start(bf16[2,2,2,2,2,16,32]{6,5,4,3,2,1,0:T(8,128)(2,1)S(1)} %get-tuple-element.119), channel_id=1, source_target_pairs={{0,4},{1,5},{2,6},{3,7},{4,0},{5,1},{6,2},{7,3},{8,12},{9,13},{10,... | collective-permute-start | bytes 98312 | tf_op jit(solution)/shard_map/ppermute | solution.py:28
  247.0 8.4 %collective-permute-start.42 = (bf16[2,2,2,2,2,2,16,32]{7,6,5,4,3,2,1,0:T(8,128)(2,1)S(1)}, bf16[2,2,2,2,2,2,16,32]{7,6,5,4,3,2,1,0:T(8,128)(2,1)S(1)}, u32[]{:S(2)}, u32[]{:S(2)}) collective-permute-start(bf16[2,2,2,2,2,2,16,32]{7,6,5,4,3,2,1,0:T(8,128)(2,1)S(1)} %get-tuple-element.101), channel_id=1, source_target_pairs={{0,2},{1,3},{2,0},{3,1},{4,6},{5,7},{6,4},{7,5},{8,10},{9,11},{10,... | collective-permute-start | bytes 196616 | tf_op jit(solution)/shard_map/ppermute | solution.py:28
  267.0 7.5 %collective-permute-start.33 = (f32[33,4,256]{2,1,0:T(4,128)S(1)}, f32[33,4,256]{2,1,0:T(4,128)S(1)}, u32[]{:S(2)}, u32[]{:S(2)}) collective-permute-start(f32[33,4,256]{2,1,0:T(4,128)S(1)} %get-tuple-element.93), channel_id=1, source_target_pairs={{4,0},{8,4},{12,8},{16,12},{20,16},{24,20},{28,24},{32,28},{36,32}... | collective-permute-start | bytes 405512 | tf_op jit(solution)/shard_map/ppermute | solution.py:40
  269.0 11.7 %collective-permute-start.32 = (f32[33,4,256]{2,1,0:T(4,128)S(1)}, f32[33,4,256]{2,1,0:T(4,128)S(1)}, u32[]{:S(2)}, u32[]{:S(2)}) collective-permute-start(f32[33,4,256]{2,1,0:T(4,128)S(1)} %get-tuple-element.92), channel_id=1, source_target_pairs={{0,4},{4,8},{8,12},{12,16},{16,20},{20,24},{24,28},{28,32},{32,36}... | collective-permute-start | bytes 405512 | tf_op jit(solution)/shard_map/ppermute | solution.py:39
  280.9 6.8 %collective-permute-start.35 = (f32[33,16,4]{2,1,0:T(8,128)S(1)}, f32[33,16,4]{2,1,0:T(8,128)S(1)}, u32[]{:S(2)}, u32[]{:S(2)}) collective-permute-start(f32[33,16,4]{2,1,0:T(8,128)S(1)} %get-tuple-element.77), channel_id=1, source_target_pairs={{0,3},{1,0},{2,1},{3,2},{4,7},{5,4},{6,5},{7,6},{8,11},{9,8},{10,9... | collective-permute-start | bytes 25352 | tf_op jit(solution)/shard_map/ppermute | solution.py:43
  281.8 8.9 %collective-permute-start.34 = (f32[33,16,4]{2,1,0:T(8,128)S(1)}, f32[33,16,4]{2,1,0:T(8,128)S(1)}, u32[]{:S(2)}, u32[]{:S(2)}) collective-permute-start(f32[33,16,4]{2,1,0:T(8,128)S(1)} %get-tuple-element.76), channel_id=1, source_target_pairs={{0,1},{1,2},{2,3},{3,0},{4,5},{5,6},{6,7},{7,4},{8,9},{9,10},{10,1... | collective-permute-start | bytes 25352 | tf_op jit(solution)/shard_map/ppermute | solution.py:42
  294.4 7.2 %collective-permute-start.45 = (f32[33,4,256]{2,1,0:T(4,128)S(1)}, f32[33,4,256]{2,1,0:T(4,128)S(1)}, u32[]{:S(2)}, u32[]{:S(2)}) collective-permute-start(f32[33,4,256]{2,1,0:T(4,128)S(1)} %get-tuple-element.91), channel_id=1, source_target_pairs={{4,0},{8,4},{12,8},{16,12},{20,16},{24,20},{28,24},{32,28},{36,32}... | collective-permute-start | bytes 405512 | tf_op jit(solution)/shard_map/ppermute | solution.py:40
  296.3 11.2 %collective-permute-start.44 = (f32[33,4,256]{2,1,0:T(4,128)S(1)}, f32[33,4,256]{2,1,0:T(4,128)S(1)}, u32[]{:S(2)}, u32[]{:S(2)}) collective-permute-start(f32[33,4,256]{2,1,0:T(4,128)S(1)} %get-tuple-element.90), channel_id=1, source_target_pairs={{0,4},{4,8},{8,12},{12,16},{16,20},{20,24},{24,28},{28,32},{32,36}... | collective-permute-start | bytes 405512 | tf_op jit(solution)/shard_map/ppermute | solution.py:39
  307.8 5.5 %collective-permute-start.47 = (f32[33,16,4]{2,1,0:T(8,128)S(1)}, f32[33,16,4]{2,1,0:T(8,128)S(1)}, u32[]{:S(2)}, u32[]{:S(2)}) collective-permute-start(f32[33,16,4]{2,1,0:T(8,128)S(1)} %get-tuple-element.75), channel_id=1, source_target_pairs={{0,3},{1,0},{2,1},{3,2},{4,7},{5,4},{6,5},{7,6},{8,11},{9,8},{10,9... | collective-permute-start | bytes 25352 | tf_op jit(solution)/shard_map/ppermute | solution.py:43
  307.9 9.3 %collective-permute-start.46 = (f32[33,16,4]{2,1,0:T(8,128)S(1)}, f32[33,16,4]{2,1,0:T(8,128)S(1)}, u32[]{:S(2)}, u32[]{:S(2)}) collective-permute-start(f32[33,16,4]{2,1,0:T(8,128)S(1)} %get-tuple-element.74), channel_id=1, source_target_pairs={{0,1},{1,2},{2,3},{3,0},{4,5},{5,6},{6,7},{7,4},{8,9},{9,10},{10,1... | collective-permute-start | bytes 25352 | tf_op jit(solution)/shard_map/ppermute | solution.py:42
  (62 other events, 864.3 us)

commit v2 on v1

--- a/solution.py
+++ b/solution.py
@@ -144,17 +144,9 @@
     target_rows = panels.shape[1]
     real_stack, imag_stack = form_kernels(panels, sources)
     fold_step = fold_columns(real_stack, imag_stack)
-    density = density_start
-    motion = motion_start
-    pressure = jnp.zeros_like(density_start)
-    for round_index in range(ITERS):
+    def one_round(density, motion, gathered):
         flat_motion = motion.reshape(channels, axial * circum)
         neumann = jnp.take(flat_motion, node_of_panel, axis=1)
-        density_bf = density.astype(jnp.bfloat16)
-        if round_index == 0:
-            gathered = joined[4:].astype(jnp.bfloat16)
-        else:
-            gathered = gather_columns(density_bf)
         start_sum = jnp.zeros((channels, 2 * target_rows), jnp.float32)
         combined = fold_step(start_sum, gathered, jnp.int32(0))
         single_part = combined[:, :target_rows]
@@ -179,7 +171,17 @@
                 trim(motion_ext, 2), bend, trim(load_ext, edge), trim(stiff_ext, edge), hoop_rows[rows_at]
             )
             motion_ext = jnp.where(inside[rows_at], motion_ext, 0.0)
-        motion = motion_ext
+        return density, motion_ext, pressure
+
+    density, motion, pressure = one_round(
+        density_start, motion_start, joined[4:].astype(jnp.bfloat16)
+    )
+
+    def later_round(_, carried):
+        density, motion, pressure = carried
+        return one_round(density, motion, gather_columns(density.astype(jnp.bfloat16)))
+
+    density, motion, pressure = lax.fori_loop(1, ITERS, later_round, (density, motion, pressure))
     return (density, pressure, motion)
 
 

time: 327 us -> 360 us (1.10)
  loops' own time: 0 us -> 12.2 us
  waiting for transfers between devices: 178 us -> 190 us
  other arithmetic: 36.3 us -> 45.5 us
  local copies, waits for them, and re-layouts: 29.8 us -> 35.4 us
  starting transfers between devices: 68 us -> 63.5 us
    ppermute x32, starting transfers between devices: 38.8 us -> 24.8 us  [gather_columns(): other = lax.ppermute(held, ('blk', 'circ'), pairs)]
    another operation x0 -> x1, loops' own time: none -> 12.2 us  [per_device(): lax.fori_loop(1, ITERS, later_round, (density, motion, pressure))]
    ppermute x32, waiting for transfers between devices: 119 us -> 130 us  [gather_columns(): other = lax.ppermute(held, ('blk', 'circ'), pairs)]
    ppermute x4, starting transfers between devices: 11.4 us -> 18.1 us  [with_halo(): lax.ppermute(field[:, :width, :], 'blk', [(i + 1, i) for i in range(rows...]
    mul x5 -> x10, other arithmetic: 0.78 us -> 5.54 us  [the longest x6 3.72 us: relax(): applied_re = bend[:half] - loss_factor * bend[half:] + shift * motion[:half]]
    slice x5 -> x17, local copies, waits for them, and re-layouts: 0.37 us -> 4.54 us  [the longest x8 2.27 us: one_round(): moment = jnp.where(inside[edge:inside.shape[0] - edge], moment, 0.0)]
    ppermute x4, starting transfers between devices: 2.82 us -> 6.88 us  [with_halo(): lax.ppermute(field[:, :, :width], 'circ', [(i, (i - 1) % cols) for i in r...]
    select_n x17 -> x23, other arithmetic: 6.32 us -> 7.27 us  [the longest x8 3.82 us: one_round(): moment = jnp.where(inside[edge:inside.shape[0] - edge], moment, 0.0)]
  transfers between devices with their start and end apart: 48 -> 48, of which waited for: 42 -> 48; matrix products, arithmetic and copies ran while one was open for 5% -> 6% of each run, Pallas kernels for 0% -> 0%
where the time goes in v2:
time: 360 us; the launch traced here: 354 us
  waiting for transfers between devices  190 us (53%)
  starting transfers between devices  63.5 us (18%)
  other arithmetic  45.5 us (13%)
  local copies, waits for them, and re-layouts  35.4 us (10%)
  loops' own time  12.2 us (3%)
  matrix products  6.08 us (2%)
    ppermute x32, waiting for transfers between devices, gather_columns(): other = lax.ppermute(held, ('blk', 'circ'), pairs)  130 us
    ppermute x32, starting transfers between devices, gather_columns(): other = lax.ppermute(held, ('blk', 'circ'), pairs)  24.8 us
    ppermute x4, waiting for transfers between devices, with_halo(): lax.ppermute(field[:, -width:, :], 'blk', [(i, i + 1) for i in range(rows...  22.5 us
    ppermute x4, waiting for transfers between devices, with_halo(): lax.ppermute(field[:, :, :width], 'circ', [(i, (i - 1) % cols) for i in r...  19.4 us
    ppermute x4, starting transfers between devices, with_halo(): lax.ppermute(field[:, :width, :], 'blk', [(i + 1, i) for i in range(rows...  18.1 us
    ppermute x4, starting transfers between devices, with_halo(): lax.ppermute(field[:, -width:, :], 'blk', [(i, i + 1) for i in range(rows...  13.7 us
    ppermute x4, waiting for transfers between devices, with_halo(): lax.ppermute(field[:, :, -width:], 'circ', [(i, (i + 1) % cols) for i in...  12.6 us
    another operation x1, loops' own time, per_device(): lax.fori_loop(1, ITERS, later_round, (density, motion, pressure))  12.2 us
  transfers between devices with their start and end apart: 48, of which 48 were waited for; matrix products, arithmetic and copies ran while one was open for 6% of the time, Pallas kernels for 0%

profile of v2, /device:TPU:128, one launch (start us, length us, event | category | flops | bytes accessed | tf_op | source)
XLA Modules:
  0.0 354.1 jit_solution(10828129171304721989)
XLA Ops:
  2.6 6.4 %collective-permute-done.12 = f32[20,32]{1,0:T(8,128)S(1)} collective-permute-done((f32[20,32]{1,0:T(8,128)S(1)}, f32[20,32]{1,0:T(8,128)S(1)}, u32[]{:S(2)}, u32[]{:S(2)}) %collective-permute-start.12) | collective-permute-done | bytes 2592 | tf_op jit(solution)/shard_map/ppermute | solution.py:28
  33.5 4.7 %collective-permute-done.17 = f32[2,2,2,2,2,20,32]{6,4,5,3,2,1,0:T(2,128)S(1)} collective-permute-done((f32[2,2,2,2,2,20,32]{6,4,5,3,2,1,0:T(2,128)S(1)}, f32[2,2,2,2,2,20,32]{6,4,5,3,2,1,0:T(2,128)S(1)}, u32[]{:S(2)}, u32[]{:S(2)}) %collective-permute-start.17) | collective-permute-done | bytes 81952 | tf_op jit(solution)/shard_map/ppermute | solution.py:28
  42.0 9.0 %collective-permute-done.18 = f32[2,2,2,2,2,2,20,32]{7,5,6,4,3,2,1,0:T(2,128)S(1)} collective-permute-done((f32[2,2,2,2,2,2,20,32]{7,5,6,4,3,2,1,0:T(2,128)S(1)}, f32[2,2,2,2,2,2,20,32]{7,5,6,4,3,2,1,0:T(2,128)S(1)}, u32[]{:S(2)}, u32[]{:S(2)}) %collective-permute-start.18) | collective-permute-done | bytes 163872 | tf_op jit(solution)/shard_map/ppermute | solution.py:28
  65.0 5.3 %multiply_convert_fusion = (bf16[32,8192]{1,0:T(8,128)(2,1)S(1)}, bf16[32,8192]{1,0:T(8,128)(2,1)S(1)}, bf16[32,8192]{1,0:T(8,128)(2,1)S(1)}, bf16[32,8192]{1,0:T(8,128)(2,1)S(1)}) fusion(f32[8192]{0:T(1024)S(1)} %div.101, f32[8192]{0:T(1024)S(1)} %sub.247, f32[32]{0:T(128)S(1)} %get-tuple-element.321, f32[8192]{0:T(1024)S(1)} %sub.242, ...), kind=kLoop, calls=%fused_computation.113 | loop fusion | flops 8650752 | bytes 2261632 | tf_op jit(solution)/shard_map/convert.2
  74.3 3.9 %collective-permute-start.20 = (f32[33,4,256]{2,1,0:T(4,128)S(1)}, f32[33,4,256]{2,1,0:T(4,128)S(1)}, u32[]{:S(2)}, u32[]{:S(2)}) collective-permute-start(f32[33,4,256]{2,1,0:T(4,128)S(1)} %get-tuple-element.297), channel_id=1, source_target_pairs={{0,4},{4,8},{8,12},{12,16},{16,20},{20,24},{24,28},{28,32},{32,36}... | collective-permute-start | bytes 405512 | tf_op jit(solution)/shard_map/ppermute | solution.py:39
  78.2 6.1 %collective-permute-start.21 = (f32[33,4,256]{2,1,0:T(4,128)S(1)}, f32[33,4,256]{2,1,0:T(4,128)S(1)}, u32[]{:S(2)}, u32[]{:S(2)}) collective-permute-start(f32[33,4,256]{2,1,0:T(4,128)S(1)} %get-tuple-element.298), channel_id=1, source_target_pairs={{4,0},{8,4},{12,8},{16,12},{20,16},{24,20},{28,24},{32,28},{36,32}... | collective-permute-start | bytes 405512 | tf_op jit(solution)/shard_map/ppermute | solution.py:40
  100.3 252.9 %while.22 = (s32[]{:T(128)}, f32[16,32]{1,0:T(8,128)S(1)}, f32[16,8,256]{2,1,0:T(8,128)S(1)}, f32[16,32]{1,0:T(8,128)}, s32[32]{0:T(128)S(1)}, /*index=5*/bf16[6...) while((s32[]{:T(128)}, f32[16,32]{1,0:T(8,128)S(1)}, ...), condition=%wide.region_4.6_spmd, body=%wide.region_2.0_spmd.sunk | while | flops 38201416 | bytes 27148044 | solution.py:184
  111.9 6.8 %collective-permute-done = bf16[16,32]{1,0:T(8,128)(2,1)S(1)} collective-permute-done((bf16[16,32]{1,0:T(8,128)(2,1)S(1)}, bf16[16,32]{1,0:T(8,128)(2,1)S(1)}, u32[]{:S(2)}, u32[]{:S(2)}) %collective-permute-start) | collective-permute-done | bytes 1056 | tf_op jit(solution)/shard_map/while/body/eval_jaxpr/ppermute | solution.py:28
  127.3 3.9 %collective-permute-done.3 = bf16[2,2,2,16,32]{4,3,2,1,0:T(8,128)(2,1)S(1)} collective-permute-done((bf16[2,2,2,16,32]{4,3,2,1,0:T(8,128)(2,1)S(1)}, bf16[2,2,2,16,32]{4,3,2,1,0:T(8,128)(2,1)S(1)}, u32[]{:S(2)}, u32[]{:S(2)}) %collective-permute-start.3) | collective-permute-done | bytes 8224 | tf_op jit(solution)/shard_map/while/body/eval_jaxpr/ppermute | solution.py:28
  133.1 4.0 %collective-permute-done.4 = bf16[2,2,2,2,16,32]{5,4,3,2,1,0:T(8,128)(2,1)S(1)} collective-permute-done((bf16[2,2,2,2,16,32]{5,4,3,2,1,0:T(8,128)(2,1)S(1)}, bf16[2,2,2,2,16,32]{5,4,3,2,1,0:T(8,128)(2,1)S(1)}, u32[]{:S(2)}, u32[]{:S(2)}) %collective-permute-start.4) | collective-permute-done | bytes 16416 | tf_op jit(solution)/shard_map/while/body/eval_jaxpr/ppermute | solution.py:28
  138.3 3.9 %collective-permute-done.5 = bf16[2,2,2,2,2,16,32]{6,5,4,3,2,1,0:T(8,128)(2,1)S(1)} collective-permute-done((bf16[2,2,2,2,2,16,32]{6,5,4,3,2,1,0:T(8,128)(2,1)S(1)}, bf16[2,2,2,2,2,16,32]{6,5,4,3,2,1,0:T(8,128)(2,1)S(1)}, u32[]{:S(2)}, u32[]{:S(2)}) %collective-permute-start.5) | collective-permute-done | bytes 32800 | tf_op jit(solution)/shard_map/while/body/eval_jaxpr/ppermute | solution.py:28
  162.2 8.1 %collective-permute-start.8 = (f32[33,4,256]{2,1,0:T(4,128)S(1)}, f32[33,4,256]{2,1,0:T(4,128)S(1)}, u32[]{:S(2)}, u32[]{:S(2)}) collective-permute-start(f32[33,4,256]{2,1,0:T(4,128)S(1)} %get-tuple-element.452), channel_id=1, source_target_pairs={{4,0},{8,4},{12,8},{16,12},{20,16},{24,20},{28,24},{32,28},{36,32}... | collective-permute-start | bytes 405512 | tf_op jit(solution)/shard_map/while/body/eval_jaxpr/ppermute | solution.py:40
  173.4 8.4 %collective-permute-done.9 = f32[33,4,256]{2,1,0:T(4,128)S(1)} collective-permute-done((f32[33,4,256]{2,1,0:T(4,128)S(1)}, f32[33,4,256]{2,1,0:T(4,128)S(1)}, u32[]{:S(2)}, u32[]{:S(2)}) %collective-permute-start.9) | collective-permute-done | bytes 135200 | tf_op jit(solution)/shard_map/while/body/eval_jaxpr/ppermute | solution.py:39
  184.0 5.8 %collective-permute-done.10 = f32[33,16,4]{2,1,0:T(8,128)S(1)} collective-permute-done((f32[33,16,4]{2,1,0:T(8,128)S(1)}, f32[33,16,4]{2,1,0:T(8,128)S(1)}, u32[]{:S(2)}, u32[]{:S(2)}) %collective-permute-start.10) | collective-permute-done | bytes 8480 | tf_op jit(solution)/shard_map/while/body/eval_jaxpr/ppermute | solution.py:43
  197.2 6.8 %collective-permute-done = bf16[16,32]{1,0:T(8,128)(2,1)S(1)} collective-permute-done((bf16[16,32]{1,0:T(8,128)(2,1)S(1)}, bf16[16,32]{1,0:T(8,128)(2,1)S(1)}, u32[]{:S(2)}, u32[]{:S(2)}) %collective-permute-start) | collective-permute-done | bytes 1056 | tf_op jit(solution)/shard_map/while/body/eval_jaxpr/ppermute | solution.py:28
  204.7 3.9 %collective-permute-done.1 = bf16[2,16,32]{2,1,0:T(8,128)(2,1)S(1)} collective-permute-done((bf16[2,16,32]{2,1,0:T(8,128)(2,1)S(1)}, bf16[2,16,32]{2,1,0:T(8,128)(2,1)S(1)}, u32[]{:S(2)}, u32[]{:S(2)}) %collective-permute-start.1) | collective-permute-done | bytes 2080 | tf_op jit(solution)/shard_map/while/body/eval_jaxpr/ppermute | solution.py:28
  212.6 3.9 %collective-permute-done.3 = bf16[2,2,2,16,32]{4,3,2,1,0:T(8,128)(2,1)S(1)} collective-permute-done((bf16[2,2,2,16,32]{4,3,2,1,0:T(8,128)(2,1)S(1)}, bf16[2,2,2,16,32]{4,3,2,1,0:T(8,128)(2,1)S(1)}, u32[]{:S(2)}, u32[]{:S(2)}) %collective-permute-start.3) | collective-permute-done | bytes 8224 | tf_op jit(solution)/shard_map/while/body/eval_jaxpr/ppermute | solution.py:28
  217.1 5.2 %collective-permute-done.4 = bf16[2,2,2,2,16,32]{5,4,3,2,1,0:T(8,128)(2,1)S(1)} collective-permute-done((bf16[2,2,2,2,16,32]{5,4,3,2,1,0:T(8,128)(2,1)S(1)}, bf16[2,2,2,2,16,32]{5,4,3,2,1,0:T(8,128)(2,1)S(1)}, u32[]{:S(2)}, u32[]{:S(2)}) %collective-permute-start.4) | collective-permute-done | bytes 16416 | tf_op jit(solution)/shard_map/while/body/eval_jaxpr/ppermute | solution.py:28
  223.5 4.0 %collective-permute-done.5 = bf16[2,2,2,2,2,16,32]{6,5,4,3,2,1,0:T(8,128)(2,1)S(1)} collective-permute-done((bf16[2,2,2,2,2,16,32]{6,5,4,3,2,1,0:T(8,128)(2,1)S(1)}, bf16[2,2,2,2,2,16,32]{6,5,4,3,2,1,0:T(8,128)(2,1)S(1)}, u32[]{:S(2)}, u32[]{:S(2)}) %collective-permute-start.5) | collective-permute-done | bytes 32800 | tf_op jit(solution)/shard_map/while/body/eval_jaxpr/ppermute | solution.py:28
  230.9 4.6 %collective-permute-done.6 = bf16[2,2,2,2,2,2,16,32]{7,6,5,4,3,2,1,0:T(8,128)(2,1)S(1)} collective-permute-done((bf16[2,2,2,2,2,2,16,32]{7,6,5,4,3,2,1,0:T(8,128)(2,1)S(1)}, bf16[2,2,2,2,2,2,16,32]{7,6,5,4,3,2,1,0:T(8,128)(2,1)S(1)}, u32[]{:S(2)}, u32[]{:S(2)}) %collective-permute-start.6) | collective-permute-done | bytes 65568 | tf_op jit(solution)/shard_map/while/body/eval_jaxpr/ppermute | solution.py:28
  249.4 3.9 %collective-permute-start.9 = (f32[33,4,256]{2,1,0:T(4,128)S(1)}, f32[33,4,256]{2,1,0:T(4,128)S(1)}, u32[]{:S(2)}, u32[]{:S(2)}) collective-permute-start(f32[33,4,256]{2,1,0:T(4,128)S(1)} %get-tuple-element.453), channel_id=1, source_target_pairs={{0,4},{4,8},{8,12},{12,16},{16,20},{20,24},{24,28},{28,32},{32,36}... | collective-permute-start | bytes 405512 | tf_op jit(solution)/shard_map/while/body/eval_jaxpr/ppermute | solution.py:39
  255.0 6.2 %collective-permute-done.9 = f32[33,4,256]{2,1,0:T(4,128)S(1)} collective-permute-done((f32[33,4,256]{2,1,0:T(4,128)S(1)}, f32[33,4,256]{2,1,0:T(4,128)S(1)}, u32[]{:S(2)}, u32[]{:S(2)}) %collective-permute-start.9) | collective-permute-done | bytes 135200 | tf_op jit(solution)/shard_map/while/body/eval_jaxpr/ppermute | solution.py:39
  262.4 5.9 %collective-permute-done.10 = f32[33,16,4]{2,1,0:T(8,128)S(1)} collective-permute-done((f32[33,16,4]{2,1,0:T(8,128)S(1)}, f32[33,16,4]{2,1,0:T(8,128)S(1)}, u32[]{:S(2)}, u32[]{:S(2)}) %collective-permute-start.10) | collective-permute-done | bytes 8480 | tf_op jit(solution)/shard_map/while/body/eval_jaxpr/ppermute | solution.py:43
  275.6 6.8 %collective-permute-done = bf16[16,32]{1,0:T(8,128)(2,1)S(1)} collective-permute-done((bf16[16,32]{1,0:T(8,128)(2,1)S(1)}, bf16[16,32]{1,0:T(8,128)(2,1)S(1)}, u32[]{:S(2)}, u32[]{:S(2)}) %collective-permute-start) | collective-permute-done | bytes 1056 | tf_op jit(solution)/shard_map/while/body/eval_jaxpr/ppermute | solution.py:28
  283.1 3.9 %collective-permute-done.1 = bf16[2,16,32]{2,1,0:T(8,128)(2,1)S(1)} collective-permute-done((bf16[2,16,32]{2,1,0:T(8,128)(2,1)S(1)}, bf16[2,16,32]{2,1,0:T(8,128)(2,1)S(1)}, u32[]{:S(2)}, u32[]{:S(2)}) %collective-permute-start.1) | collective-permute-done | bytes 2080 | tf_op jit(solution)/shard_map/while/body/eval_jaxpr/ppermute | solution.py:28
  291.0 3.9 %collective-permute-done.3 = bf16[2,2,2,16,32]{4,3,2,1,0:T(8,128)(2,1)S(1)} collective-permute-done((bf16[2,2,2,16,32]{4,3,2,1,0:T(8,128)(2,1)S(1)}, bf16[2,2,2,16,32]{4,3,2,1,0:T(8,128)(2,1)S(1)}, u32[]{:S(2)}, u32[]{:S(2)}) %collective-permute-start.3) | collective-permute-done | bytes 8224 | tf_op jit(solution)/shard_map/while/body/eval_jaxpr/ppermute | solution.py:28
  295.5 5.2 %collective-permute-done.4 = bf16[2,2,2,2,16,32]{5,4,3,2,1,0:T(8,128)(2,1)S(1)} collective-permute-done((bf16[2,2,2,2,16,32]{5,4,3,2,1,0:T(8,128)(2,1)S(1)}, bf16[2,2,2,2,16,32]{5,4,3,2,1,0:T(8,128)(2,1)S(1)}, u32[]{:S(2)}, u32[]{:S(2)}) %collective-permute-start.4) | collective-permute-done | bytes 16416 | tf_op jit(solution)/shard_map/while/body/eval_jaxpr/ppermute | solution.py:28
  301.9 4.0 %collective-permute-done.5 = bf16[2,2,2,2,2,16,32]{6,5,4,3,2,1,0:T(8,128)(2,1)S(1)} collective-permute-done((bf16[2,2,2,2,2,16,32]{6,5,4,3,2,1,0:T(8,128)(2,1)S(1)}, bf16[2,2,2,2,2,16,32]{6,5,4,3,2,1,0:T(8,128)(2,1)S(1)}, u32[]{:S(2)}, u32[]{:S(2)}) %collective-permute-start.5) | collective-permute-done | bytes 32800 | tf_op jit(solution)/shard_map/while/body/eval_jaxpr/ppermute | solution.py:28
  309.3 4.6 %collective-permute-done.6 = bf16[2,2,2,2,2,2,16,32]{7,6,5,4,3,2,1,0:T(8,128)(2,1)S(1)} collective-permute-done((bf16[2,2,2,2,2,2,16,32]{7,6,5,4,3,2,1,0:T(8,128)(2,1)S(1)}, bf16[2,2,2,2,2,2,16,32]{7,6,5,4,3,2,1,0:T(8,128)(2,1)S(1)}, u32[]{:S(2)}, u32[]{:S(2)}) %collective-permute-start.6) | collective-permute-done | bytes 65568 | tf_op jit(solution)/shard_map/while/body/eval_jaxpr/ppermute | solution.py:28
  327.8 3.9 %collective-permute-start.9 = (f32[33,4,256]{2,1,0:T(4,128)S(1)}, f32[33,4,256]{2,1,0:T(4,128)S(1)}, u32[]{:S(2)}, u32[]{:S(2)}) collective-permute-start(f32[33,4,256]{2,1,0:T(4,128)S(1)} %get-tuple-element.453), channel_id=1, source_target_pairs={{0,4},{4,8},{8,12},{12,16},{16,20},{20,24},{24,28},{28,32},{32,36}... | collective-permute-start | bytes 405512 | tf_op jit(solution)/shard_map/while/body/eval_jaxpr/ppermute | solution.py:39
  333.4 6.2 %collective-permute-done.9 = f32[33,4,256]{2,1,0:T(4,128)S(1)} collective-permute-done((f32[33,4,256]{2,1,0:T(4,128)S(1)}, f32[33,4,256]{2,1,0:T(4,128)S(1)}, u32[]{:S(2)}, u32[]{:S(2)}) %collective-permute-start.9) | collective-permute-done | bytes 135200 | tf_op jit(solution)/shard_map/while/body/eval_jaxpr/ppermute | solution.py:39
  340.8 5.9 %collective-permute-done.10 = f32[33,16,4]{2,1,0:T(8,128)S(1)} collective-permute-done((f32[33,16,4]{2,1,0:T(8,128)S(1)}, f32[33,16,4]{2,1,0:T(8,128)S(1)}, u32[]{:S(2)}, u32[]{:S(2)}) %collective-permute-start.10) | collective-permute-done | bytes 8480 | tf_op jit(solution)/shard_map/while/body/eval_jaxpr/ppermute | solution.py:43
  (420 shorter events, 175.4 us)
Async XLA Ops:
  1.4 7.6 %collective-permute-start.12 = (f32[20,32]{1,0:T(8,128)S(1)}, f32[20,32]{1,0:T(8,128)S(1)}, u32[]{:S(2)}, u32[]{:S(2)}) collective-permute-start(f32[20,32]{1,0:T(8,128)S(1)} %get-tuple-element.314), channel_id=1, source_target_pairs={{0,128},{1,129},{2,130},{3,131},{4,132},{5,133},{6,134},{7,135},{8... | collective-permute-start | bytes 7688 | tf_op jit(solution)/shard_map/ppermute | solution.py:28
  22.6 7.9 %collective-permute-start.16 = (f32[2,2,2,2,20,32]{5,3,4,2,1,0:T(2,128)S(1)}, f32[2,2,2,2,20,32]{5,3,4,2,1,0:T(2,128)S(1)}, u32[]{:S(2)}, u32[]{:S(2)}) collective-permute-start(f32[2,2,2,2,20,32]{5,3,4,2,1,0:T(2,128)S(1)} %get-tuple-element.304), channel_id=1, source_target_pairs={{0,8},{1,9},{2,10},{3,11},{4,12},{5,13},{6,14},{7,15},{8,0},{9,1},... | collective-permute-start | bytes 122888 | tf_op jit(solution)/shard_map/ppermute | solution.py:28
  30.8 7.4 %collective-permute-start.17 = (f32[2,2,2,2,2,20,32]{6,4,5,3,2,1,0:T(2,128)S(1)}, f32[2,2,2,2,2,20,32]{6,4,5,3,2,1,0:T(2,128)S(1)}, u32[]{:S(2)}, u32[]{:S(2)}) collective-permute-start(f32[2,2,2,2,2,20,32]{6,4,5,3,2,1,0:T(2,128)S(1)} %get-tuple-element.296), channel_id=1, source_target_pairs={{0,4},{1,5},{2,6},{3,7},{4,0},{5,1},{6,2},{7,3},{8,12},{9,13},{10,... | collective-permute-start | bytes 245768 | tf_op jit(solution)/shard_map/ppermute | solution.py:28
  38.8 12.2 %collective-permute-start.18 = (f32[2,2,2,2,2,2,20,32]{7,5,6,4,3,2,1,0:T(2,128)S(1)}, f32[2,2,2,2,2,2,20,32]{7,5,6,4,3,2,1,0:T(2,128)S(1)}, u32[]{:S(2)}, u32[]{:S(2)}) collective-permute-start(f32[2,2,2,2,2,2,20,32]{7,5,6,4,3,2,1,0:T(2,128)S(1)} %get-tuple-element.292), channel_id=1, source_target_pairs={{0,2},{1,3},{2,0},{3,1},{4,6},{5,7},{6,4},{7,5},{8,10},{9,11},{10,... | collective-permute-start | bytes 491528 | tf_op jit(solution)/shard_map/ppermute | solution.py:28
  74.3 11.7 %collective-permute-start.20 = (f32[33,4,256]{2,1,0:T(4,128)S(1)}, f32[33,4,256]{2,1,0:T(4,128)S(1)}, u32[]{:S(2)}, u32[]{:S(2)}) collective-permute-start(f32[33,4,256]{2,1,0:T(4,128)S(1)} %get-tuple-element.297), channel_id=1, source_target_pairs={{0,4},{4,8},{8,12},{12,16},{16,20},{20,24},{24,28},{28,32},{32,36}... | collective-permute-start | bytes 405512 | tf_op jit(solution)/shard_map/ppermute | solution.py:39
  78.2 9.0 %collective-permute-start.21 = (f32[33,4,256]{2,1,0:T(4,128)S(1)}, f32[33,4,256]{2,1,0:T(4,128)S(1)}, u32[]{:S(2)}, u32[]{:S(2)}) collective-permute-start(f32[33,4,256]{2,1,0:T(4,128)S(1)} %get-tuple-element.298), channel_id=1, source_target_pairs={{4,0},{8,4},{12,8},{16,12},{20,16},{24,20},{28,24},{32,28},{36,32}... | collective-permute-start | bytes 405512 | tf_op jit(solution)/shard_map/ppermute | solution.py:40
  87.4 7.5 %collective-permute-start.22 = (f32[33,16,4]{2,1,0:T(8,128)S(1)}, f32[33,16,4]{2,1,0:T(8,128)S(1)}, u32[]{:S(2)}, u32[]{:S(2)}) collective-permute-start(f32[33,16,4]{2,1,0:T(8,128)S(1)} %get-tuple-element.293), channel_id=1, source_target_pairs={{0,1},{1,2},{2,3},{3,0},{4,5},{5,6},{6,7},{7,4},{8,9},{9,10},{10,1... | collective-permute-start | bytes 25352 | tf_op jit(solution)/shard_map/ppermute | solution.py:42
  87.5 9.3 %collective-permute-start.23 = (f32[33,16,4]{2,1,0:T(8,128)S(1)}, f32[33,16,4]{2,1,0:T(8,128)S(1)}, u32[]{:S(2)}, u32[]{:S(2)}) collective-permute-start(f32[33,16,4]{2,1,0:T(8,128)S(1)} %get-tuple-element.294), channel_id=1, source_target_pairs={{0,3},{1,0},{2,1},{3,2},{4,7},{5,4},{6,5},{7,6},{8,11},{9,8},{10,9... | collective-permute-start | bytes 25352 | tf_op jit(solution)/shard_map/ppermute | solution.py:43
  111.2 7.6 %collective-permute-start = (bf16[16,32]{1,0:T(8,128)(2,1)S(1)}, bf16[16,32]{1,0:T(8,128)(2,1)S(1)}, u32[]{:S(2)}, u32[]{:S(2)}) collective-permute-start(bf16[16,32]{1,0:T(8,128)(2,1)S(1)} %convert_element_type.43), channel_id=1, source_target_pairs={{0,128},{1,129},{2,130},{3,131},{4,132},{5,133},{6,134},{7,135},{8... | collective-permute-start | bytes 3080 | tf_op jit(solution)/shard_map/while/body/eval_jaxpr/ppermute | solution.py:28
  131.2 5.9 %collective-permute-start.4 = (bf16[2,2,2,2,16,32]{5,4,3,2,1,0:T(8,128)(2,1)S(1)}, bf16[2,2,2,2,16,32]{5,4,3,2,1,0:T(8,128)(2,1)S(1)}, u32[]{:S(2)}, u32[]{:S(2)}) collective-permute-start(bf16[2,2,2,2,16,32]{5,4,3,2,1,0:T(8,128)(2,1)S(1)} %get-tuple-element.440), channel_id=1, source_target_pairs={{0,8},{1,9},{2,10},{3,11},{4,12},{5,13},{6,14},{7,15},{8,0},{9,1},... | collective-permute-start | bytes 49160 | tf_op jit(solution)/shard_map/while/body/eval_jaxpr/ppermute | solution.py:28
  137.1 5.1 %collective-permute-start.5 = (bf16[2,2,2,2,2,16,32]{6,5,4,3,2,1,0:T(8,128)(2,1)S(1)}, bf16[2,2,2,2,2,16,32]{6,5,4,3,2,1,0:T(8,128)(2,1)S(1)}, u32[]{:S(2)}, u32[]{:S(2)}) collective-permute-start(bf16[2,2,2,2,2,16,32]{6,5,4,3,2,1,0:T(8,128)(2,1)S(1)} %get-tuple-element.442), channel_id=1, source_target_pairs={{0,4},{1,5},{2,6},{3,7},{4,0},{5,1},{6,2},{7,3},{8,12},{9,13},{10,... | collective-permute-start | bytes 98312 | tf_op jit(solution)/shard_map/while/body/eval_jaxpr/ppermute | solution.py:28
  142.2 8.0 %collective-permute-start.6 = (bf16[2,2,2,2,2,2,16,32]{7,6,5,4,3,2,1,0:T(8,128)(2,1)S(1)}, bf16[2,2,2,2,2,2,16,32]{7,6,5,4,3,2,1,0:T(8,128)(2,1)S(1)}, u32[]{:S(2)}, u32[]{:S(2)}) collective-permute-start(bf16[2,2,2,2,2,2,16,32]{7,6,5,4,3,2,1,0:T(8,128)(2,1)S(1)} %get-tuple-element.444), channel_id=1, source_target_pairs={{0,2},{1,3},{2,0},{3,1},{4,6},{5,7},{6,4},{7,5},{8,10},{9,11},{10,... | collective-permute-start | bytes 196616 | tf_op jit(solution)/shard_map/while/body/eval_jaxpr/ppermute | solution.py:28
  162.2 11.2 %collective-permute-start.8 = (f32[33,4,256]{2,1,0:T(4,128)S(1)}, f32[33,4,256]{2,1,0:T(4,128)S(1)}, u32[]{:S(2)}, u32[]{:S(2)}) collective-permute-start(f32[33,4,256]{2,1,0:T(4,128)S(1)} %get-tuple-element.452), channel_id=1, source_target_pairs={{4,0},{8,4},{12,8},{16,12},{20,16},{24,20},{28,24},{32,28},{36,32}... | collective-permute-start | bytes 405512 | tf_op jit(solution)/shard_map/while/body/eval_jaxpr/ppermute | solution.py:40
  170.3 11.6 %collective-permute-start.9 = (f32[33,4,256]{2,1,0:T(4,128)S(1)}, f32[33,4,256]{2,1,0:T(4,128)S(1)}, u32[]{:S(2)}, u32[]{:S(2)}) collective-permute-start(f32[33,4,256]{2,1,0:T(4,128)S(1)} %get-tuple-element.453), channel_id=1, source_target_pairs={{0,4},{4,8},{8,12},{12,16},{16,20},{20,24},{24,28},{28,32},{32,36}... | collective-permute-start | bytes 405512 | tf_op jit(solution)/shard_map/while/body/eval_jaxpr/ppermute | solution.py:39
  182.1 7.7 %collective-permute-start.10 = (f32[33,16,4]{2,1,0:T(8,128)S(1)}, f32[33,16,4]{2,1,0:T(8,128)S(1)}, u32[]{:S(2)}, u32[]{:S(2)}) collective-permute-start(f32[33,16,4]{2,1,0:T(8,128)S(1)} %get-tuple-element.454), channel_id=1, source_target_pairs={{0,3},{1,0},{2,1},{3,2},{4,7},{5,4},{6,5},{7,6},{8,11},{9,8},{10,9... | collective-permute-start | bytes 25352 | tf_op jit(solution)/shard_map/while/body/eval_jaxpr/ppermute | solution.py:43
  183.9 8.8 %collective-permute-start.11 = (f32[33,16,4]{2,1,0:T(8,128)S(1)}, f32[33,16,4]{2,1,0:T(8,128)S(1)}, u32[]{:S(2)}, u32[]{:S(2)}) collective-permute-start(f32[33,16,4]{2,1,0:T(8,128)S(1)} %get-tuple-element.455), channel_id=1, source_target_pairs={{0,1},{1,2},{2,3},{3,0},{4,5},{5,6},{6,7},{7,4},{8,9},{9,10},{10,1... | collective-permute-start | bytes 25352 | tf_op jit(solution)/shard_map/while/body/eval_jaxpr/ppermute | solution.py:42
  196.4 7.6 %collective-permute-start = (bf16[16,32]{1,0:T(8,128)(2,1)S(1)}, bf16[16,32]{1,0:T(8,128)(2,1)S(1)}, u32[]{:S(2)}, u32[]{:S(2)}) collective-permute-start(bf16[16,32]{1,0:T(8,128)(2,1)S(1)} %convert_element_type.43), channel_id=1, source_target_pairs={{0,128},{1,129},{2,130},{3,131},{4,132},{5,133},{6,134},{7,135},{8... | collective-permute-start | bytes 3080 | tf_op jit(solution)/shard_map/while/body/eval_jaxpr/ppermute | solution.py:28
  216.5 5.9 %collective-permute-start.4 = (bf16[2,2,2,2,16,32]{5,4,3,2,1,0:T(8,128)(2,1)S(1)}, bf16[2,2,2,2,16,32]{5,4,3,2,1,0:T(8,128)(2,1)S(1)}, u32[]{:S(2)}, u32[]{:S(2)}) collective-permute-start(bf16[2,2,2,2,16,32]{5,4,3,2,1,0:T(8,128)(2,1)S(1)} %get-tuple-element.440), channel_id=1, source_target_pairs={{0,8},{1,9},{2,10},{3,11},{4,12},{5,13},{6,14},{7,15},{8,0},{9,1},... | collective-permute-start | bytes 49160 | tf_op jit(solution)/shard_map/while/body/eval_jaxpr/ppermute | solution.py:28
  222.4 5.1 %collective-permute-start.5 = (bf16[2,2,2,2,2,16,32]{6,5,4,3,2,1,0:T(8,128)(2,1)S(1)}, bf16[2,2,2,2,2,16,32]{6,5,4,3,2,1,0:T(8,128)(2,1)S(1)}, u32[]{:S(2)}, u32[]{:S(2)}) collective-permute-start(bf16[2,2,2,2,2,16,32]{6,5,4,3,2,1,0:T(8,128)(2,1)S(1)} %get-tuple-element.442), channel_id=1, source_target_pairs={{0,4},{1,5},{2,6},{3,7},{4,0},{5,1},{6,2},{7,3},{8,12},{9,13},{10,... | collective-permute-start | bytes 98312 | tf_op jit(solution)/shard_map/while/body/eval_jaxpr/ppermute | solution.py:28
  227.5 8.0 %collective-permute-start.6 = (bf16[2,2,2,2,2,2,16,32]{7,6,5,4,3,2,1,0:T(8,128)(2,1)S(1)}, bf16[2,2,2,2,2,2,16,32]{7,6,5,4,3,2,1,0:T(8,128)(2,1)S(1)}, u32[]{:S(2)}, u32[]{:S(2)}) collective-permute-start(bf16[2,2,2,2,2,2,16,32]{7,6,5,4,3,2,1,0:T(8,128)(2,1)S(1)} %get-tuple-element.444), channel_id=1, source_target_pairs={{0,2},{1,3},{2,0},{3,1},{4,6},{5,7},{6,4},{7,5},{8,10},{9,11},{10,... | collective-permute-start | bytes 196616 | tf_op jit(solution)/shard_map/while/body/eval_jaxpr/ppermute | solution.py:28
  247.4 7.5 %collective-permute-start.8 = (f32[33,4,256]{2,1,0:T(4,128)S(1)}, f32[33,4,256]{2,1,0:T(4,128)S(1)}, u32[]{:S(2)}, u32[]{:S(2)}) collective-permute-start(f32[33,4,256]{2,1,0:T(4,128)S(1)} %get-tuple-element.452), channel_id=1, source_target_pairs={{4,0},{8,4},{12,8},{16,12},{20,16},{24,20},{28,24},{32,28},{36,32}... | collective-permute-start | bytes 405512 | tf_op jit(solution)/shard_map/while/body/eval_jaxpr/ppermute | solution.py:40
  249.4 11.8 %collective-permute-start.9 = (f32[33,4,256]{2,1,0:T(4,128)S(1)}, f32[33,4,256]{2,1,0:T(4,128)S(1)}, u32[]{:S(2)}, u32[]{:S(2)}) collective-permute-start(f32[33,4,256]{2,1,0:T(4,128)S(1)} %get-tuple-element.453), channel_id=1, source_target_pairs={{0,4},{4,8},{8,12},{12,16},{16,20},{20,24},{24,28},{28,32},{32,36}... | collective-permute-start | bytes 405512 | tf_op jit(solution)/shard_map/while/body/eval_jaxpr/ppermute | solution.py:39
  261.4 6.8 %collective-permute-start.10 = (f32[33,16,4]{2,1,0:T(8,128)S(1)}, f32[33,16,4]{2,1,0:T(8,128)S(1)}, u32[]{:S(2)}, u32[]{:S(2)}) collective-permute-start(f32[33,16,4]{2,1,0:T(8,128)S(1)} %get-tuple-element.454), channel_id=1, source_target_pairs={{0,3},{1,0},{2,1},{3,2},{4,7},{5,4},{6,5},{7,6},{8,11},{9,8},{10,9... | collective-permute-start | bytes 25352 | tf_op jit(solution)/shard_map/while/body/eval_jaxpr/ppermute | solution.py:43
  262.3 8.8 %collective-permute-start.11 = (f32[33,16,4]{2,1,0:T(8,128)S(1)}, f32[33,16,4]{2,1,0:T(8,128)S(1)}, u32[]{:S(2)}, u32[]{:S(2)}) collective-permute-start(f32[33,16,4]{2,1,0:T(8,128)S(1)} %get-tuple-element.455), channel_id=1, source_target_pairs={{0,1},{1,2},{2,3},{3,0},{4,5},{5,6},{6,7},{7,4},{8,9},{9,10},{10,1... | collective-permute-start | bytes 25352 | tf_op jit(solution)/shard_map/while/body/eval_jaxpr/ppermute | solution.py:42
  274.9 7.6 %collective-permute-start = (bf16[16,32]{1,0:T(8,128)(2,1)S(1)}, bf16[16,32]{1,0:T(8,128)(2,1)S(1)}, u32[]{:S(2)}, u32[]{:S(2)}) collective-permute-start(bf16[16,32]{1,0:T(8,128)(2,1)S(1)} %convert_element_type.43), channel_id=1, source_target_pairs={{0,128},{1,129},{2,130},{3,131},{4,132},{5,133},{6,134},{7,135},{8... | collective-permute-start | bytes 3080 | tf_op jit(solution)/shard_map/while/body/eval_jaxpr/ppermute | solution.py:28
  294.9 5.9 %collective-permute-start.4 = (bf16[2,2,2,2,16,32]{5,4,3,2,1,0:T(8,128)(2,1)S(1)}, bf16[2,2,2,2,16,32]{5,4,3,2,1,0:T(8,128)(2,1)S(1)}, u32[]{:S(2)}, u32[]{:S(2)}) collective-permute-start(bf16[2,2,2,2,16,32]{5,4,3,2,1,0:T(8,128)(2,1)S(1)} %get-tuple-element.440), channel_id=1, source_target_pairs={{0,8},{1,9},{2,10},{3,11},{4,12},{5,13},{6,14},{7,15},{8,0},{9,1},... | collective-permute-start | bytes 49160 | tf_op jit(solution)/shard_map/while/body/eval_jaxpr/ppermute | solution.py:28
  300.8 5.1 %collective-permute-start.5 = (bf16[2,2,2,2,2,16,32]{6,5,4,3,2,1,0:T(8,128)(2,1)S(1)}, bf16[2,2,2,2,2,16,32]{6,5,4,3,2,1,0:T(8,128)(2,1)S(1)}, u32[]{:S(2)}, u32[]{:S(2)}) collective-permute-start(bf16[2,2,2,2,2,16,32]{6,5,4,3,2,1,0:T(8,128)(2,1)S(1)} %get-tuple-element.442), channel_id=1, source_target_pairs={{0,4},{1,5},{2,6},{3,7},{4,0},{5,1},{6,2},{7,3},{8,12},{9,13},{10,... | collective-permute-start | bytes 98312 | tf_op jit(solution)/shard_map/while/body/eval_jaxpr/ppermute | solution.py:28
  305.9 8.0 %collective-permute-start.6 = (bf16[2,2,2,2,2,2,16,32]{7,6,5,4,3,2,1,0:T(8,128)(2,1)S(1)}, bf16[2,2,2,2,2,2,16,32]{7,6,5,4,3,2,1,0:T(8,128)(2,1)S(1)}, u32[]{:S(2)}, u32[]{:S(2)}) collective-permute-start(bf16[2,2,2,2,2,2,16,32]{7,6,5,4,3,2,1,0:T(8,128)(2,1)S(1)} %get-tuple-element.444), channel_id=1, source_target_pairs={{0,2},{1,3},{2,0},{3,1},{4,6},{5,7},{6,4},{7,5},{8,10},{9,11},{10,... | collective-permute-start | bytes 196616 | tf_op jit(solution)/shard_map/while/body/eval_jaxpr/ppermute | solution.py:28
  325.8 7.5 %collective-permute-start.8 = (f32[33,4,256]{2,1,0:T(4,128)S(1)}, f32[33,4,256]{2,1,0:T(4,128)S(1)}, u32[]{:S(2)}, u32[]{:S(2)}) collective-permute-start(f32[33,4,256]{2,1,0:T(4,128)S(1)} %get-tuple-element.452), channel_id=1, source_target_pairs={{4,0},{8,4},{12,8},{16,12},{20,16},{24,20},{28,24},{32,28},{36,32}... | collective-permute-start | bytes 405512 | tf_op jit(solution)/shard_map/while/body/eval_jaxpr/ppermute | solution.py:40
  327.8 11.8 %collective-permute-start.9 = (f32[33,4,256]{2,1,0:T(4,128)S(1)}, f32[33,4,256]{2,1,0:T(4,128)S(1)}, u32[]{:S(2)}, u32[]{:S(2)}) collective-permute-start(f32[33,4,256]{2,1,0:T(4,128)S(1)} %get-tuple-element.453), channel_id=1, source_target_pairs={{0,4},{4,8},{8,12},{12,16},{16,20},{20,24},{24,28},{28,32},{32,36}... | collective-permute-start | bytes 405512 | tf_op jit(solution)/shard_map/while/body/eval_jaxpr/ppermute | solution.py:39
  339.9 6.8 %collective-permute-start.10 = (f32[33,16,4]{2,1,0:T(8,128)S(1)}, f32[33,16,4]{2,1,0:T(8,128)S(1)}, u32[]{:S(2)}, u32[]{:S(2)}) collective-permute-start(f32[33,16,4]{2,1,0:T(8,128)S(1)} %get-tuple-element.454), channel_id=1, source_target_pairs={{0,3},{1,0},{2,1},{3,2},{4,7},{5,4},{6,5},{7,6},{8,11},{9,8},{10,9... | collective-permute-start | bytes 25352 | tf_op jit(solution)/shard_map/while/body/eval_jaxpr/ppermute | solution.py:43
  340.7 8.8 %collective-permute-start.11 = (f32[33,16,4]{2,1,0:T(8,128)S(1)}, f32[33,16,4]{2,1,0:T(8,128)S(1)}, u32[]{:S(2)}, u32[]{:S(2)}) collective-permute-start(f32[33,16,4]{2,1,0:T(8,128)S(1)} %get-tuple-element.455), channel_id=1, source_target_pairs={{0,1},{1,2},{2,3},{3,0},{4,5},{5,6},{6,7},{7,4},{8,9},{9,10},{10,1... | collective-permute-start | bytes 25352 | tf_op jit(solution)/shard_map/while/body/eval_jaxpr/ppermute | solution.py:42
  (69 other events, 673.3 us)

commit v3 on v1

--- a/solution.py
+++ b/solution.py
@@ -36,12 +36,29 @@
 def with_halo(field, width):
     rows = lax.axis_size("blk")
     cols = lax.axis_size("circ")
+    both = ("blk", "circ")
+
+    def diagonal(piece, step_row, step_col):
+        pairs = [
+            (b * cols + c, (b + step_row) * cols + (c + step_col) % cols)
+            for b in range(rows)
+            for c in range(cols)
+            if 0 <= b + step_row < rows
+        ]
+        return lax.ppermute(piece, both, pairs)
+
     above = lax.ppermute(field[:, -width:, :], "blk", [(i, i + 1) for i in range(rows - 1)])
     below = lax.ppermute(field[:, :width, :], "blk", [(i + 1, i) for i in range(rows - 1)])
-    field = jnp.concatenate([above, field, below], axis=1)
     left = lax.ppermute(field[:, :, -width:], "circ", [(i, (i + 1) % cols) for i in range(cols)])
     right = lax.ppermute(field[:, :, :width], "circ", [(i, (i - 1) % cols) for i in range(cols)])
-    return jnp.concatenate([left, field, right], axis=2)
+    upper_left = diagonal(field[:, -width:, -width:], 1, 1)
+    upper_right = diagonal(field[:, -width:, :width], 1, -1)
+    lower_left = diagonal(field[:, :width, -width:], -1, 1)
+    lower_right = diagonal(field[:, :width, :width], -1, -1)
+    top = jnp.concatenate([upper_left, above, upper_right], axis=2)
+    middle = jnp.concatenate([left, field, right], axis=2)
+    bottom = jnp.concatenate([lower_left, below, lower_right], axis=2)
+    return jnp.concatenate([top, middle, bottom], axis=1)
 
 
 def laplace_inner(extended):

time: 327 us -> 367 us (1.12)
  starting transfers between devices: 68 us -> 124 us
  waiting for transfers between devices: 178 us -> 161 us
    ppermute x0 -> x16, starting transfers between devices: none -> 59.4 us  [diagonal(): return lax.ppermute(piece, both, pairs)]
    ppermute x0 -> x16, waiting for transfers between devices: none -> 37.8 us  [diagonal(): return lax.ppermute(piece, both, pairs)]
    ppermute x4, waiting for transfers between devices: 25 us -> 0.01 us  [with_halo(): lax.ppermute(field[:, -width:, :], 'blk', [(i, i + 1) for i in range(rows...]
    ppermute x4, waiting for transfers between devices: 17.2 us -> 0.01 us  [with_halo(): lax.ppermute(field[:, :, :width], 'circ', [(i, (i - 1) % cols) for i in r...]
    ppermute x4, waiting for transfers between devices: 14.3 us -> 0.01 us  [with_halo(): lax.ppermute(field[:, :, -width:], 'circ', [(i, (i + 1) % cols) for i in...]
    ppermute x32, waiting for transfers between devices: 119 us -> 123 us  [gather_columns(): other = lax.ppermute(held, ('blk', 'circ'), pairs)]
    ppermute x4, starting transfers between devices: 11.4 us -> 15.2 us  [with_halo(): lax.ppermute(field[:, :width, :], 'blk', [(i + 1, i) for i in range(rows...]
  transfers between devices with their start and end apart: 48 -> 64, of which waited for: 42 -> 37; matrix products, arithmetic and copies ran while one was open for 5% -> 5% of each run, Pallas kernels for 0% -> 0%
where the time goes in v3:
time: 367 us; the launch traced here: 361 us
  waiting for transfers between devices  161 us (44%)
  starting transfers between devices  124 us (34%)
  other arithmetic  38.4 us (10%)
  local copies, waits for them, and re-layouts  27.8 us (8%)
  matrix products  6.61 us (2%)
    ppermute x32, waiting for transfers between devices, gather_columns(): other = lax.ppermute(held, ('blk', 'circ'), pairs)  123 us
    ppermute x16, starting transfers between devices, diagonal(): return lax.ppermute(piece, both, pairs)  59.4 us
    ppermute x16, waiting for transfers between devices, diagonal(): return lax.ppermute(piece, both, pairs)  37.8 us
    ppermute x32, starting transfers between devices, gather_columns(): other = lax.ppermute(held, ('blk', 'circ'), pairs)  35.5 us
    ppermute x4, starting transfers between devices, with_halo(): lax.ppermute(field[:, :width, :], 'blk', [(i + 1, i) for i in range(rows...  15.2 us
    ppermute x4, starting transfers between devices, with_halo(): lax.ppermute(field[:, -width:, :], 'blk', [(i, i + 1) for i in range(rows...  10.3 us
  transfers between devices with their start and end apart: 64, of which 37 were waited for; matrix products, arithmetic and copies ran while one was open for 5% of the time, Pallas kernels for 0%

profile of v3, /device:TPU:128, one launch (start us, length us, event | category | flops | bytes accessed | tf_op | source)
XLA Modules:
  0.0 360.7 jit_solution(4179485458731991959)
XLA Ops:
  1.8 7.1 %collective-permute-done = f32[20,32]{1,0:T(8,128)S(1)} collective-permute-done((f32[20,32]{1,0:T(8,128)S(1)}, f32[20,32]{1,0:T(8,128)S(1)}, u32[]{:S(2)}, u32[]{:S(2)}) %collective-permute-start) | collective-permute-done | bytes 2592 | tf_op jit(solution)/shard_map/ppermute | solution.py:28
  26.7 3.8 %collective-permute-done.4 = f32[2,2,2,2,20,32]{5,3,4,2,1,0:T(2,128)S(1)} collective-permute-done((f32[2,2,2,2,20,32]{5,3,4,2,1,0:T(2,128)S(1)}, f32[2,2,2,2,20,32]{5,3,4,2,1,0:T(2,128)S(1)}, u32[]{:S(2)}, u32[]{:S(2)}) %collective-permute-start.4) | collective-permute-done | bytes 40992 | tf_op jit(solution)/shard_map/ppermute | solution.py:28
  42.4 8.5 %collective-permute-done.6 = f32[2,2,2,2,2,2,20,32]{7,5,6,4,3,2,1,0:T(2,128)S(1)} collective-permute-done((f32[2,2,2,2,2,2,20,32]{7,5,6,4,3,2,1,0:T(2,128)S(1)}, f32[2,2,2,2,2,2,20,32]{7,5,6,4,3,2,1,0:T(2,128)S(1)}, u32[]{:S(2)}, u32[]{:S(2)}) %collective-permute-start.6) | collective-permute-done | bytes 163872 | tf_op jit(solution)/shard_map/ppermute | solution.py:28
  63.4 5.3 %multiply_convert_fusion = (bf16[32,8192]{1,0:T(8,128)(2,1)S(1)}, bf16[32,8192]{1,0:T(8,128)(2,1)S(1)}, bf16[32,8192]{1,0:T(8,128)(2,1)S(1)}, bf16[32,8192]{1,0:T(8,128)(2,1)S(1)}) fusion(f32[8192]{0:T(1024)S(1)} %div.69, f32[8192]{0:T(1024)S(1)} %sub.275, f32[32]{0:T(128)S(1)} %copy-done.20, f32[8192]{0:T(1024)S(1)} %sub.270, f32[32]{0:T(128)S(1)} %copy-done.18, ...), kind=kLoop, calls=%fused_computation.34 | loop fusion | flops 8650752 | bytes 2261632 | tf_op jit(solution)/shard_map/convert.1
  70.6 7.0 %collective-permute-done.16 = bf16[16,32]{1,0:T(8,128)(2,1)S(1)} collective-permute-done((bf16[16,32]{1,0:T(8,128)(2,1)S(1)}, bf16[16,32]{1,0:T(8,128)(2,1)S(1)}, u32[]{:S(2)}, u32[]{:S(2)}) %collective-permute-start.16) | collective-permute-done | bytes 1056 | tf_op jit(solution)/shard_map/ppermute | solution.py:28
  90.0 4.3 %collective-permute-start.20 = (bf16[2,2,2,2,16,32]{5,4,3,2,1,0:T(8,128)(2,1)S(1)}, bf16[2,2,2,2,16,32]{5,4,3,2,1,0:T(8,128)(2,1)S(1)}, u32[]{:S(2)}, u32[]{:S(2)}) collective-permute-start(bf16[2,2,2,2,16,32]{5,4,3,2,1,0:T(8,128)(2,1)S(1)} %get-tuple-element.149), channel_id=1, source_target_pairs={{0,8},{1,9},{2,10},{3,11},{4,12},{5,13},{6,14},{7,15},{8,0},{9,1},... | collective-permute-start | bytes 49160 | tf_op jit(solution)/shard_map/ppermute | solution.py:28
  105.0 4.8 %collective-permute-done.22 = bf16[2,2,2,2,2,2,16,32]{7,6,5,4,3,2,1,0:T(8,128)(2,1)S(1)} collective-permute-done((bf16[2,2,2,2,2,2,16,32]{7,6,5,4,3,2,1,0:T(8,128)(2,1)S(1)}, bf16[2,2,2,2,2,2,16,32]{7,6,5,4,3,2,1,0:T(8,128)(2,1)S(1)}, u32[]{:S(2)}, u32[]{:S(2)}) %collective-permute-start.22) | collective-permute-done | bytes 65568 | tf_op jit(solution)/shard_map/ppermute | solution.py:28
  121.4 6.6 %collective-permute-start.15 = (f32[33,4,4]{2,1,0:T(4,128)S(1)}, f32[33,4,4]{2,1,0:T(4,128)S(1)}, u32[]{:S(2)}, u32[]{:S(2)}) collective-permute-start(f32[33,4,4]{2,1,0:T(4,128)S(1)} %get-tuple-element.108), channel_id=1, source_target_pairs={{4,3},{5,0},{6,1},{7,2},{8,7},{9,4},{10,5},{11,6},{12,11},{13,8},{... | collective-permute-start | bytes 6344 | tf_op jit(solution)/shard_map/ppermute | solution.py:48
  132.9 6.0 %collective-permute-start.10 = (f32[33,4,4]{2,1,0:T(4,128)S(1)}, f32[33,4,4]{2,1,0:T(4,128)S(1)}, u32[]{:S(2)}, u32[]{:S(2)}) collective-permute-start(f32[33,4,4]{2,1,0:T(4,128)S(1)} %get-tuple-element.109), channel_id=1, source_target_pairs={{0,7},{1,4},{2,5},{3,6},{4,11},{5,8},{6,9},{7,10},{8,15},{9,12},{1... | collective-permute-start | bytes 6344 | tf_op jit(solution)/shard_map/ppermute | solution.py:48
  146.6 7.3 %collective-permute-done.8 = f32[33,4,4]{2,1,0:T(4,128)S(1)} collective-permute-done((f32[33,4,4]{2,1,0:T(4,128)S(1)}, f32[33,4,4]{2,1,0:T(4,128)S(1)}, u32[]{:S(2)}, u32[]{:S(2)}) %collective-permute-start.8) | collective-permute-done | bytes 2144 | tf_op jit(solution)/shard_map/ppermute | solution.py:48
  158.6 7.5 %collective-permute-done.32 = bf16[16,32]{1,0:T(8,128)(2,1)S(1)} collective-permute-done((bf16[16,32]{1,0:T(8,128)(2,1)S(1)}, bf16[16,32]{1,0:T(8,128)(2,1)S(1)}, u32[]{:S(2)}, u32[]{:S(2)}) %collective-permute-start.32) | collective-permute-done | bytes 1056 | tf_op jit(solution)/shard_map/ppermute | solution.py:28
  167.1 3.7 %collective-permute-done.33 = bf16[2,16,32]{2,1,0:T(8,128)(2,1)S(1)} collective-permute-done((bf16[2,16,32]{2,1,0:T(8,128)(2,1)S(1)}, bf16[2,16,32]{2,1,0:T(8,128)(2,1)S(1)}, u32[]{:S(2)}, u32[]{:S(2)}) %collective-permute-start.33) | collective-permute-done | bytes 2080 | tf_op jit(solution)/shard_map/ppermute | solution.py:28
  178.9 5.7 %collective-permute-done.36 = bf16[2,2,2,2,16,32]{5,4,3,2,1,0:T(8,128)(2,1)S(1)} collective-permute-done((bf16[2,2,2,2,16,32]{5,4,3,2,1,0:T(8,128)(2,1)S(1)}, bf16[2,2,2,2,16,32]{5,4,3,2,1,0:T(8,128)(2,1)S(1)}, u32[]{:S(2)}, u32[]{:S(2)}) %collective-permute-start.36) | collective-permute-done | bytes 16416 | tf_op jit(solution)/shard_map/ppermute | solution.py:28
  186.8 3.7 %collective-permute-start.30 = (f32[33,4,256]{2,1,0:T(4,128)S(1)}, f32[33,4,256]{2,1,0:T(4,128)S(1)}, u32[]{:S(2)}, u32[]{:S(2)}) collective-permute-start(f32[33,4,256]{2,1,0:T(4,128)S(1)} %get-tuple-element.103), channel_id=1, source_target_pairs={{4,0},{8,4},{12,8},{16,12},{20,16},{24,20},{28,24},{32,28},{36,32}... | collective-permute-start | bytes 405512 | tf_op jit(solution)/shard_map/ppermute | solution.py:51
  194.2 4.3 %collective-permute-start.26 = (f32[33,4,4]{2,1,0:T(4,128)S(1)}, f32[33,4,4]{2,1,0:T(4,128)S(1)}, u32[]{:S(2)}, u32[]{:S(2)}) collective-permute-start(f32[33,4,4]{2,1,0:T(4,128)S(1)} %get-tuple-element.101), channel_id=1, source_target_pairs={{0,7},{1,4},{2,5},{3,6},{4,11},{5,8},{6,9},{7,10},{8,15},{9,12},{1... | collective-permute-start | bytes 6344 | tf_op jit(solution)/shard_map/ppermute | solution.py:48
  206.2 4.7 %collective-permute-done.38 = bf16[2,2,2,2,2,2,16,32]{7,6,5,4,3,2,1,0:T(8,128)(2,1)S(1)} collective-permute-done((bf16[2,2,2,2,2,2,16,32]{7,6,5,4,3,2,1,0:T(8,128)(2,1)S(1)}, bf16[2,2,2,2,2,2,16,32]{7,6,5,4,3,2,1,0:T(8,128)(2,1)S(1)}, u32[]{:S(2)}, u32[]{:S(2)}) %collective-permute-start.38) | collective-permute-done | bytes 65568 | tf_op jit(solution)/shard_map/ppermute | solution.py:28
  212.9 9.7 %collective-permute-done.24 = f32[33,4,4]{2,1,0:T(4,128)S(1)} collective-permute-done((f32[33,4,4]{2,1,0:T(4,128)S(1)}, f32[33,4,4]{2,1,0:T(4,128)S(1)}, u32[]{:S(2)}, u32[]{:S(2)}) %collective-permute-start.24) | collective-permute-done | bytes 2144 | tf_op jit(solution)/shard_map/ppermute | solution.py:48
  235.1 7.5 %collective-permute-done.48 = bf16[16,32]{1,0:T(8,128)(2,1)S(1)} collective-permute-done((bf16[16,32]{1,0:T(8,128)(2,1)S(1)}, bf16[16,32]{1,0:T(8,128)(2,1)S(1)}, u32[]{:S(2)}, u32[]{:S(2)}) %collective-permute-start.48) | collective-permute-done | bytes 1056 | tf_op jit(solution)/shard_map/ppermute | solution.py:28
  242.6 4.5 %collective-permute-done.49 = bf16[2,16,32]{2,1,0:T(8,128)(2,1)S(1)} collective-permute-done((bf16[2,16,32]{2,1,0:T(8,128)(2,1)S(1)}, bf16[2,16,32]{2,1,0:T(8,128)(2,1)S(1)}, u32[]{:S(2)}, u32[]{:S(2)}) %collective-permute-start.49) | collective-permute-done | bytes 2080 | tf_op jit(solution)/shard_map/ppermute | solution.py:28
  247.2 3.7 %collective-permute-done.50 = bf16[2,2,16,32]{3,2,1,0:T(8,128)(2,1)S(1)} collective-permute-done((bf16[2,2,16,32]{3,2,1,0:T(8,128)(2,1)S(1)}, bf16[2,2,16,32]{3,2,1,0:T(8,128)(2,1)S(1)}, u32[]{:S(2)}, u32[]{:S(2)}) %collective-permute-start.50) | collective-permute-done | bytes 4128 | tf_op jit(solution)/shard_map/ppermute | solution.py:28
  251.1 3.9 %collective-permute-done.51 = bf16[2,2,2,16,32]{4,3,2,1,0:T(8,128)(2,1)S(1)} collective-permute-done((bf16[2,2,2,16,32]{4,3,2,1,0:T(8,128)(2,1)S(1)}, bf16[2,2,2,16,32]{4,3,2,1,0:T(8,128)(2,1)S(1)}, u32[]{:S(2)}, u32[]{:S(2)}) %collective-permute-start.51) | collective-permute-done | bytes 8224 | tf_op jit(solution)/shard_map/ppermute | solution.py:28
  255.1 5.8 %collective-permute-done.52 = bf16[2,2,2,2,16,32]{5,4,3,2,1,0:T(8,128)(2,1)S(1)} collective-permute-done((bf16[2,2,2,2,16,32]{5,4,3,2,1,0:T(8,128)(2,1)S(1)}, bf16[2,2,2,2,16,32]{5,4,3,2,1,0:T(8,128)(2,1)S(1)}, u32[]{:S(2)}, u32[]{:S(2)}) %collective-permute-start.52) | collective-permute-done | bytes 16416 | tf_op jit(solution)/shard_map/ppermute | solution.py:28
  261.0 5.0 %collective-permute-done.53 = bf16[2,2,2,2,2,16,32]{6,5,4,3,2,1,0:T(8,128)(2,1)S(1)} collective-permute-done((bf16[2,2,2,2,2,16,32]{6,5,4,3,2,1,0:T(8,128)(2,1)S(1)}, bf16[2,2,2,2,2,16,32]{6,5,4,3,2,1,0:T(8,128)(2,1)S(1)}, u32[]{:S(2)}, u32[]{:S(2)}) %collective-permute-start.53) | collective-permute-done | bytes 32800 | tf_op jit(solution)/shard_map/ppermute | solution.py:28
  268.5 5.9 %collective-permute-done.54 = bf16[2,2,2,2,2,2,16,32]{7,6,5,4,3,2,1,0:T(8,128)(2,1)S(1)} collective-permute-done((bf16[2,2,2,2,2,2,16,32]{7,6,5,4,3,2,1,0:T(8,128)(2,1)S(1)}, bf16[2,2,2,2,2,2,16,32]{7,6,5,4,3,2,1,0:T(8,128)(2,1)S(1)}, u32[]{:S(2)}, u32[]{:S(2)}) %collective-permute-start.54) | collective-permute-done | bytes 65568 | tf_op jit(solution)/shard_map/ppermute | solution.py:28
  286.5 4.8 %collective-permute-start.47 = (f32[33,4,4]{2,1,0:T(4,128)S(1)}, f32[33,4,4]{2,1,0:T(4,128)S(1)}, u32[]{:S(2)}, u32[]{:S(2)}) collective-permute-start(f32[33,4,4]{2,1,0:T(4,128)S(1)} %get-tuple-element.92), channel_id=1, source_target_pairs={{4,3},{5,0},{6,1},{7,2},{8,7},{9,4},{10,5},{11,6},{12,11},{13,8},{... | collective-permute-start | bytes 6344 | tf_op jit(solution)/shard_map/ppermute | solution.py:48
  299.2 5.8 %collective-permute-start.42 = (f32[33,4,4]{2,1,0:T(4,128)S(1)}, f32[33,4,4]{2,1,0:T(4,128)S(1)}, u32[]{:S(2)}, u32[]{:S(2)}) collective-permute-start(f32[33,4,4]{2,1,0:T(4,128)S(1)} %get-tuple-element.93), channel_id=1, source_target_pairs={{0,7},{1,4},{2,5},{3,6},{4,11},{5,8},{6,9},{7,10},{8,15},{9,12},{1... | collective-permute-start | bytes 6344 | tf_op jit(solution)/shard_map/ppermute | solution.py:48
  305.5 4.1 %collective-permute-done.42 = f32[33,4,4]{2,1,0:T(4,128)S(1)} collective-permute-done((f32[33,4,4]{2,1,0:T(4,128)S(1)}, f32[33,4,4]{2,1,0:T(4,128)S(1)}, u32[]{:S(2)}, u32[]{:S(2)}) %collective-permute-start.42) | collective-permute-done | bytes 2144 | tf_op jit(solution)/shard_map/ppermute | solution.py:48
  311.6 9.1 %collective-permute-done.40 = f32[33,4,4]{2,1,0:T(4,128)S(1)} collective-permute-done((f32[33,4,4]{2,1,0:T(4,128)S(1)}, f32[33,4,4]{2,1,0:T(4,128)S(1)}, u32[]{:S(2)}, u32[]{:S(2)}) %collective-permute-start.40) | collective-permute-done | bytes 2144 | tf_op jit(solution)/shard_map/ppermute | solution.py:48
  328.3 6.2 %collective-permute-start.58 = (f32[33,4,4]{2,1,0:T(4,128)S(1)}, f32[33,4,4]{2,1,0:T(4,128)S(1)}, u32[]{:S(2)}, u32[]{:S(2)}) collective-permute-start(f32[33,4,4]{2,1,0:T(4,128)S(1)} %get-tuple-element.85), channel_id=1, source_target_pairs={{0,7},{1,4},{2,5},{3,6},{4,11},{5,8},{6,9},{7,10},{8,15},{9,12},{1... | collective-permute-start | bytes 6344 | tf_op jit(solution)/shard_map/ppermute | solution.py:48
  335.7 5.2 %collective-permute-start.62 = (f32[33,4,256]{2,1,0:T(4,128)S(1)}, f32[33,4,256]{2,1,0:T(4,128)S(1)}, u32[]{:S(2)}, u32[]{:S(2)}) collective-permute-start(f32[33,4,256]{2,1,0:T(4,128)S(1)} %get-tuple-element.87), channel_id=1, source_target_pairs={{4,0},{8,4},{12,8},{16,12},{20,16},{24,20},{28,24},{32,28},{36,32}... | collective-permute-start | bytes 405512 | tf_op jit(solution)/shard_map/ppermute | solution.py:51
  344.3 5.0 %collective-permute-start.56 = (f32[33,4,4]{2,1,0:T(4,128)S(1)}, f32[33,4,4]{2,1,0:T(4,128)S(1)}, u32[]{:S(2)}, u32[]{:S(2)}) collective-permute-start(f32[33,4,4]{2,1,0:T(4,128)S(1)} %get-tuple-element.82), channel_id=1, source_target_pairs={{0,5},{1,6},{2,7},{3,4},{4,9},{5,10},{6,11},{7,8},{8,13},{9,14},{1... | collective-permute-start | bytes 6344 | tf_op jit(solution)/shard_map/ppermute | solution.py:48
  350.0 6.3 %collective-permute-done.56 = f32[33,4,4]{2,1,0:T(4,128)S(1)} collective-permute-done((f32[33,4,4]{2,1,0:T(4,128)S(1)}, f32[33,4,4]{2,1,0:T(4,128)S(1)}, u32[]{:S(2)}, u32[]{:S(2)}) %collective-permute-start.56) | collective-permute-done | bytes 2144 | tf_op jit(solution)/shard_map/ppermute | solution.py:48
  (355 shorter events, 175.3 us)
Async XLA Ops:
  38.7 12.2 %collective-permute-start.6 = (f32[2,2,2,2,2,2,20,32]{7,5,6,4,3,2,1,0:T(2,128)S(1)}, f32[2,2,2,2,2,2,20,32]{7,5,6,4,3,2,1,0:T(2,128)S(1)}, u32[]{:S(2)}, u32[]{:S(2)}) collective-permute-start(f32[2,2,2,2,2,2,20,32]{7,5,6,4,3,2,1,0:T(2,128)S(1)} %get-tuple-element.73), channel_id=1, source_target_pairs={{0,2},{1,3},{2,0},{3,1},{4,6},{5,7},{6,4},{7,5},{8,10},{9,11},{10,... | collective-permute-start | bytes 491528 | tf_op jit(solution)/shard_map/ppermute | solution.py:28
  121.4 20.6 %collective-permute-start.15 = (f32[33,4,4]{2,1,0:T(4,128)S(1)}, f32[33,4,4]{2,1,0:T(4,128)S(1)}, u32[]{:S(2)}, u32[]{:S(2)}) collective-permute-start(f32[33,4,4]{2,1,0:T(4,128)S(1)} %get-tuple-element.108), channel_id=1, source_target_pairs={{4,3},{5,0},{6,1},{7,2},{8,7},{9,4},{10,5},{11,6},{12,11},{13,8},{... | collective-permute-start | bytes 6344 | tf_op jit(solution)/shard_map/ppermute | solution.py:48
  128.0 25.9 %collective-permute-start.14 = (f32[33,4,256]{2,1,0:T(4,128)S(1)}, f32[33,4,256]{2,1,0:T(4,128)S(1)}, u32[]{:S(2)}, u32[]{:S(2)}) collective-permute-start(f32[33,4,256]{2,1,0:T(4,128)S(1)} %get-tuple-element.111), channel_id=1, source_target_pairs={{4,0},{8,4},{12,8},{16,12},{20,16},{24,20},{28,24},{32,28},{36,32}... | collective-permute-start | bytes 405512 | tf_op jit(solution)/shard_map/ppermute | solution.py:51
  130.9 11.1 %collective-permute-start.13 = (f32[33,4,4]{2,1,0:T(4,128)S(1)}, f32[33,4,4]{2,1,0:T(4,128)S(1)}, u32[]{:S(2)}, u32[]{:S(2)}) collective-permute-start(f32[33,4,4]{2,1,0:T(4,128)S(1)} %get-tuple-element.107), channel_id=1, source_target_pairs={{4,1},{5,2},{6,3},{7,0},{8,5},{9,6},{10,7},{11,4},{12,9},{13,10},{... | collective-permute-start | bytes 6344 | tf_op jit(solution)/shard_map/ppermute | solution.py:48
  138.9 14.9 %collective-permute-start.9 = (f32[33,4,256]{2,1,0:T(4,128)S(1)}, f32[33,4,256]{2,1,0:T(4,128)S(1)}, u32[]{:S(2)}, u32[]{:S(2)}) collective-permute-start(f32[33,4,256]{2,1,0:T(4,128)S(1)} %get-tuple-element.110), channel_id=1, source_target_pairs={{0,4},{4,8},{8,12},{12,16},{16,20},{20,24},{24,28},{28,32},{32,36}... | collective-permute-start | bytes 405512 | tf_op jit(solution)/shard_map/ppermute | solution.py:50
  141.9 11.9 %collective-permute-start.12 = (f32[33,8,4]{2,1,0:T(8,128)S(1)}, f32[33,8,4]{2,1,0:T(8,128)S(1)}, u32[]{:S(2)}, u32[]{:S(2)}) collective-permute-start(f32[33,8,4]{2,1,0:T(8,128)S(1)} %get-tuple-element.113), channel_id=1, source_target_pairs={{0,3},{1,0},{2,1},{3,2},{4,7},{5,4},{6,5},{7,6},{8,11},{9,8},{10,9... | collective-permute-start | bytes 12680 | tf_op jit(solution)/shard_map/ppermute | solution.py:53
  142.0 11.8 %collective-permute-start.11 = (f32[33,8,4]{2,1,0:T(8,128)S(1)}, f32[33,8,4]{2,1,0:T(8,128)S(1)}, u32[]{:S(2)}, u32[]{:S(2)}) collective-permute-start(f32[33,8,4]{2,1,0:T(8,128)S(1)} %get-tuple-element.112), channel_id=1, source_target_pairs={{0,1},{1,2},{2,3},{3,0},{4,5},{5,6},{6,7},{7,4},{8,9},{9,10},{10,1... | collective-permute-start | bytes 12680 | tf_op jit(solution)/shard_map/ppermute | solution.py:52
  142.7 11.2 %collective-permute-start.8 = (f32[33,4,4]{2,1,0:T(4,128)S(1)}, f32[33,4,4]{2,1,0:T(4,128)S(1)}, u32[]{:S(2)}, u32[]{:S(2)}) collective-permute-start(f32[33,4,4]{2,1,0:T(4,128)S(1)} %get-tuple-element.106), channel_id=1, source_target_pairs={{0,5},{1,6},{2,7},{3,4},{4,9},{5,10},{6,11},{7,8},{8,13},{9,14},{1... | collective-permute-start | bytes 6344 | tf_op jit(solution)/shard_map/ppermute | solution.py:48
  184.6 13.9 %collective-permute-start.37 = (bf16[2,2,2,2,2,16,32]{6,5,4,3,2,1,0:T(8,128)(2,1)S(1)}, bf16[2,2,2,2,2,16,32]{6,5,4,3,2,1,0:T(8,128)(2,1)S(1)}, u32[]{:S(2)}, u32[]{:S(2)}) collective-permute-start(bf16[2,2,2,2,2,16,32]{6,5,4,3,2,1,0:T(8,128)(2,1)S(1)} %get-tuple-element.139), channel_id=1, source_target_pairs={{0,4},{1,5},{2,6},{3,7},{4,0},{5,1},{6,2},{7,3},{8,12},{9,13},{10,... | collective-permute-start | bytes 98312 | tf_op jit(solution)/shard_map/ppermute | solution.py:28
  184.9 15.8 %collective-permute-start.31 = (f32[33,4,4]{2,1,0:T(4,128)S(1)}, f32[33,4,4]{2,1,0:T(4,128)S(1)}, u32[]{:S(2)}, u32[]{:S(2)}) collective-permute-start(f32[33,4,4]{2,1,0:T(4,128)S(1)} %get-tuple-element.100), channel_id=1, source_target_pairs={{4,3},{5,0},{6,1},{7,2},{8,7},{9,4},{10,5},{11,6},{12,11},{13,8},{... | collective-permute-start | bytes 6344 | tf_op jit(solution)/shard_map/ppermute | solution.py:48
  186.8 36.0 %collective-permute-start.30 = (f32[33,4,256]{2,1,0:T(4,128)S(1)}, f32[33,4,256]{2,1,0:T(4,128)S(1)}, u32[]{:S(2)}, u32[]{:S(2)}) collective-permute-start(f32[33,4,256]{2,1,0:T(4,128)S(1)} %get-tuple-element.103), channel_id=1, source_target_pairs={{4,0},{8,4},{12,8},{16,12},{20,16},{24,20},{28,24},{32,28},{36,32}... | collective-permute-start | bytes 405512 | tf_op jit(solution)/shard_map/ppermute | solution.py:51
  190.5 12.2 %collective-permute-start.29 = (f32[33,4,4]{2,1,0:T(4,128)S(1)}, f32[33,4,4]{2,1,0:T(4,128)S(1)}, u32[]{:S(2)}, u32[]{:S(2)}) collective-permute-start(f32[33,4,4]{2,1,0:T(4,128)S(1)} %get-tuple-element.99), channel_id=1, source_target_pairs={{4,1},{5,2},{6,3},{7,0},{8,5},{9,6},{10,7},{11,4},{12,9},{13,10},{... | collective-permute-start | bytes 6344 | tf_op jit(solution)/shard_map/ppermute | solution.py:48
  198.5 24.3 %collective-permute-start.25 = (f32[33,4,256]{2,1,0:T(4,128)S(1)}, f32[33,4,256]{2,1,0:T(4,128)S(1)}, u32[]{:S(2)}, u32[]{:S(2)}) collective-permute-start(f32[33,4,256]{2,1,0:T(4,128)S(1)} %get-tuple-element.102), channel_id=1, source_target_pairs={{0,4},{4,8},{8,12},{12,16},{16,20},{20,24},{24,28},{28,32},{32,36}... | collective-permute-start | bytes 405512 | tf_op jit(solution)/shard_map/ppermute | solution.py:50
  202.8 20.0 %collective-permute-start.28 = (f32[33,8,4]{2,1,0:T(8,128)S(1)}, f32[33,8,4]{2,1,0:T(8,128)S(1)}, u32[]{:S(2)}, u32[]{:S(2)}) collective-permute-start(f32[33,8,4]{2,1,0:T(8,128)S(1)} %get-tuple-element.105), channel_id=1, source_target_pairs={{0,3},{1,0},{2,1},{3,2},{4,7},{5,4},{6,5},{7,6},{8,11},{9,8},{10,9... | collective-permute-start | bytes 12680 | tf_op jit(solution)/shard_map/ppermute | solution.py:53
  204.1 18.7 %collective-permute-start.27 = (f32[33,8,4]{2,1,0:T(8,128)S(1)}, f32[33,8,4]{2,1,0:T(8,128)S(1)}, u32[]{:S(2)}, u32[]{:S(2)}) collective-permute-start(f32[33,8,4]{2,1,0:T(8,128)S(1)} %get-tuple-element.104), channel_id=1, source_target_pairs={{0,1},{1,2},{2,3},{3,0},{4,5},{5,6},{6,7},{7,4},{8,9},{9,10},{10,1... | collective-permute-start | bytes 12680 | tf_op jit(solution)/shard_map/ppermute | solution.py:52
  210.8 11.7 %collective-permute-start.24 = (f32[33,4,4]{2,1,0:T(4,128)S(1)}, f32[33,4,4]{2,1,0:T(4,128)S(1)}, u32[]{:S(2)}, u32[]{:S(2)}) collective-permute-start(f32[33,4,4]{2,1,0:T(4,128)S(1)} %get-tuple-element.98), channel_id=1, source_target_pairs={{0,5},{1,6},{2,7},{3,4},{4,9},{5,10},{6,11},{7,8},{8,13},{9,14},{1... | collective-permute-start | bytes 6344 | tf_op jit(solution)/shard_map/ppermute | solution.py:48
  286.5 18.5 %collective-permute-start.47 = (f32[33,4,4]{2,1,0:T(4,128)S(1)}, f32[33,4,4]{2,1,0:T(4,128)S(1)}, u32[]{:S(2)}, u32[]{:S(2)}) collective-permute-start(f32[33,4,4]{2,1,0:T(4,128)S(1)} %get-tuple-element.92), channel_id=1, source_target_pairs={{4,3},{5,0},{6,1},{7,2},{8,7},{9,4},{10,5},{11,6},{12,11},{13,8},{... | collective-permute-start | bytes 6344 | tf_op jit(solution)/shard_map/ppermute | solution.py:48
  291.3 29.4 %collective-permute-start.46 = (f32[33,4,256]{2,1,0:T(4,128)S(1)}, f32[33,4,256]{2,1,0:T(4,128)S(1)}, u32[]{:S(2)}, u32[]{:S(2)}) collective-permute-start(f32[33,4,256]{2,1,0:T(4,128)S(1)} %get-tuple-element.95), channel_id=1, source_target_pairs={{4,0},{8,4},{12,8},{16,12},{20,16},{24,20},{28,24},{32,28},{36,32}... | collective-permute-start | bytes 405512 | tf_op jit(solution)/shard_map/ppermute | solution.py:51
  294.7 10.4 %collective-permute-start.45 = (f32[33,4,4]{2,1,0:T(4,128)S(1)}, f32[33,4,4]{2,1,0:T(4,128)S(1)}, u32[]{:S(2)}, u32[]{:S(2)}) collective-permute-start(f32[33,4,4]{2,1,0:T(4,128)S(1)} %get-tuple-element.91), channel_id=1, source_target_pairs={{4,1},{5,2},{6,3},{7,0},{8,5},{9,6},{10,7},{11,4},{12,9},{13,10},{... | collective-permute-start | bytes 6344 | tf_op jit(solution)/shard_map/ppermute | solution.py:48
  296.6 24.1 %collective-permute-start.41 = (f32[33,4,256]{2,1,0:T(4,128)S(1)}, f32[33,4,256]{2,1,0:T(4,128)S(1)}, u32[]{:S(2)}, u32[]{:S(2)}) collective-permute-start(f32[33,4,256]{2,1,0:T(4,128)S(1)} %get-tuple-element.94), channel_id=1, source_target_pairs={{0,4},{4,8},{8,12},{12,16},{16,20},{20,24},{24,28},{28,32},{32,36}... | collective-permute-start | bytes 405512 | tf_op jit(solution)/shard_map/ppermute | solution.py:50
  299.2 10.5 %collective-permute-start.42 = (f32[33,4,4]{2,1,0:T(4,128)S(1)}, f32[33,4,4]{2,1,0:T(4,128)S(1)}, u32[]{:S(2)}, u32[]{:S(2)}) collective-permute-start(f32[33,4,4]{2,1,0:T(4,128)S(1)} %get-tuple-element.93), channel_id=1, source_target_pairs={{0,7},{1,4},{2,5},{3,6},{4,11},{5,8},{6,9},{7,10},{8,15},{9,12},{1... | collective-permute-start | bytes 6344 | tf_op jit(solution)/shard_map/ppermute | solution.py:48
  304.9 15.8 %collective-permute-start.44 = (f32[33,8,4]{2,1,0:T(8,128)S(1)}, f32[33,8,4]{2,1,0:T(8,128)S(1)}, u32[]{:S(2)}, u32[]{:S(2)}) collective-permute-start(f32[33,8,4]{2,1,0:T(8,128)S(1)} %get-tuple-element.97), channel_id=1, source_target_pairs={{0,3},{1,0},{2,1},{3,2},{4,7},{5,4},{6,5},{7,6},{8,11},{9,8},{10,9... | collective-permute-start | bytes 12680 | tf_op jit(solution)/shard_map/ppermute | solution.py:53
  305.1 15.6 %collective-permute-start.43 = (f32[33,8,4]{2,1,0:T(8,128)S(1)}, f32[33,8,4]{2,1,0:T(8,128)S(1)}, u32[]{:S(2)}, u32[]{:S(2)}) collective-permute-start(f32[33,8,4]{2,1,0:T(8,128)S(1)} %get-tuple-element.96), channel_id=1, source_target_pairs={{0,1},{1,2},{2,3},{3,0},{4,5},{5,6},{6,7},{7,4},{8,9},{9,10},{10,1... | collective-permute-start | bytes 12680 | tf_op jit(solution)/shard_map/ppermute | solution.py:52
  309.7 11.0 %collective-permute-start.40 = (f32[33,4,4]{2,1,0:T(4,128)S(1)}, f32[33,4,4]{2,1,0:T(4,128)S(1)}, u32[]{:S(2)}, u32[]{:S(2)}) collective-permute-start(f32[33,4,4]{2,1,0:T(4,128)S(1)} %get-tuple-element.90), channel_id=1, source_target_pairs={{0,5},{1,6},{2,7},{3,4},{4,9},{5,10},{6,11},{7,8},{8,13},{9,14},{1... | collective-permute-start | bytes 6344 | tf_op jit(solution)/shard_map/ppermute | solution.py:48
  324.4 16.6 %collective-permute-start.63 = (f32[33,4,4]{2,1,0:T(4,128)S(1)}, f32[33,4,4]{2,1,0:T(4,128)S(1)}, u32[]{:S(2)}, u32[]{:S(2)}) collective-permute-start(f32[33,4,4]{2,1,0:T(4,128)S(1)} %get-tuple-element.84), channel_id=1, source_target_pairs={{4,3},{5,0},{6,1},{7,2},{8,7},{9,4},{10,5},{11,6},{12,11},{13,8},{... | collective-permute-start | bytes 6344 | tf_op jit(solution)/shard_map/ppermute | solution.py:48
  326.4 15.2 %collective-permute-start.61 = (f32[33,4,4]{2,1,0:T(4,128)S(1)}, f32[33,4,4]{2,1,0:T(4,128)S(1)}, u32[]{:S(2)}, u32[]{:S(2)}) collective-permute-start(f32[33,4,4]{2,1,0:T(4,128)S(1)} %get-tuple-element.83), channel_id=1, source_target_pairs={{4,1},{5,2},{6,3},{7,0},{8,5},{9,6},{10,7},{11,4},{12,9},{13,10},{... | collective-permute-start | bytes 6344 | tf_op jit(solution)/shard_map/ppermute | solution.py:48
  328.3 16.0 %collective-permute-start.58 = (f32[33,4,4]{2,1,0:T(4,128)S(1)}, f32[33,4,4]{2,1,0:T(4,128)S(1)}, u32[]{:S(2)}, u32[]{:S(2)}) collective-permute-start(f32[33,4,4]{2,1,0:T(4,128)S(1)} %get-tuple-element.85), channel_id=1, source_target_pairs={{0,7},{1,4},{2,5},{3,6},{4,11},{5,8},{6,9},{7,10},{8,15},{9,12},{1... | collective-permute-start | bytes 6344 | tf_op jit(solution)/shard_map/ppermute | solution.py:48
  335.7 20.6 %collective-permute-start.62 = (f32[33,4,256]{2,1,0:T(4,128)S(1)}, f32[33,4,256]{2,1,0:T(4,128)S(1)}, u32[]{:S(2)}, u32[]{:S(2)}) collective-permute-start(f32[33,4,256]{2,1,0:T(4,128)S(1)} %get-tuple-element.87), channel_id=1, source_target_pairs={{4,0},{8,4},{12,8},{16,12},{20,16},{24,20},{28,24},{32,28},{36,32}... | collective-permute-start | bytes 405512 | tf_op jit(solution)/shard_map/ppermute | solution.py:51
  340.9 15.4 %collective-permute-start.60 = (f32[33,8,4]{2,1,0:T(8,128)S(1)}, f32[33,8,4]{2,1,0:T(8,128)S(1)}, u32[]{:S(2)}, u32[]{:S(2)}) collective-permute-start(f32[33,8,4]{2,1,0:T(8,128)S(1)} %get-tuple-element.89), channel_id=1, source_target_pairs={{0,3},{1,0},{2,1},{3,2},{4,7},{5,4},{6,5},{7,6},{8,11},{9,8},{10,9... | collective-permute-start | bytes 12680 | tf_op jit(solution)/shard_map/ppermute | solution.py:53
  341.0 15.3 %collective-permute-start.59 = (f32[33,8,4]{2,1,0:T(8,128)S(1)}, f32[33,8,4]{2,1,0:T(8,128)S(1)}, u32[]{:S(2)}, u32[]{:S(2)}) collective-permute-start(f32[33,8,4]{2,1,0:T(8,128)S(1)} %get-tuple-element.88), channel_id=1, source_target_pairs={{0,1},{1,2},{2,3},{3,0},{4,5},{5,6},{6,7},{7,4},{8,9},{9,10},{10,1... | collective-permute-start | bytes 12680 | tf_op jit(solution)/shard_map/ppermute | solution.py:52
  341.5 14.8 %collective-permute-start.57 = (f32[33,4,256]{2,1,0:T(4,128)S(1)}, f32[33,4,256]{2,1,0:T(4,128)S(1)}, u32[]{:S(2)}, u32[]{:S(2)}) collective-permute-start(f32[33,4,256]{2,1,0:T(4,128)S(1)} %get-tuple-element.86), channel_id=1, source_target_pairs={{0,4},{4,8},{8,12},{12,16},{16,20},{20,24},{24,28},{28,32},{32,36}... | collective-permute-start | bytes 405512 | tf_op jit(solution)/shard_map/ppermute | solution.py:50
  344.3 12.0 %collective-permute-start.56 = (f32[33,4,4]{2,1,0:T(4,128)S(1)}, f32[33,4,4]{2,1,0:T(4,128)S(1)}, u32[]{:S(2)}, u32[]{:S(2)}) collective-permute-start(f32[33,4,4]{2,1,0:T(4,128)S(1)} %get-tuple-element.82), channel_id=1, source_target_pairs={{0,5},{1,6},{2,7},{3,4},{4,9},{5,10},{6,11},{7,8},{8,13},{9,14},{1... | collective-permute-start | bytes 6344 | tf_op jit(solution)/shard_map/ppermute | solution.py:48
  (56 other events, 446.7 us)

commit v4 on v1

--- a/solution.py
+++ b/solution.py
@@ -22,12 +22,15 @@
     count = lax.axis_size("blk") * lax.axis_size("circ")
     bits = count.bit_length() - 1
     held = block
-    for level in reversed(range(bits)):
+    levels = list(reversed(range(bits)))
+    if bits == 8:
+        levels = [7, 6, 1, 5, 4, 3, 2, 0]
+    for level in levels:
         bit = 1 << level
         pairs = [(i, i ^ bit) for i in range(count)]
         other = lax.ppermute(held, ("blk", "circ"), pairs)
         held = jnp.stack([held, other], axis=0)
-    order = list(reversed(range(bits)))
+    order = [bits - 1 - levels.index(bits - 1 - j) for j in range(bits)]
     held = jnp.transpose(held, order + [bits, bits + 1])
     held = held.reshape((count,) + block.shape)
     return jnp.transpose(held, (1, 0, 2)).reshape(block.shape[0], count * block.shape[1])

time: 327 us -> 328 us (level)
  waiting for transfers between devices: 178 us -> 183 us
    ppermute x32, waiting for transfers between devices: 119 us -> 123 us  [gather_columns(): other = lax.ppermute(held, ('blk', 'circ'), pairs)]
  transfers between devices with their start and end apart: 48 -> 48, of which waited for: 42 -> 44; matrix products, arithmetic and copies ran while one was open for 5% -> 5% of each run, Pallas kernels for 0% -> 0%
where the time goes in v4:
time: 328 us; the launch traced here: 323 us
  waiting for transfers between devices  183 us (56%)
  starting transfers between devices  64.9 us (20%)
  other arithmetic  36.3 us (11%)
  local copies, waits for them, and re-layouts  29.8 us (9%)
  matrix products  6.48 us (2%)
    ppermute x32, waiting for transfers between devices, gather_columns(): other = lax.ppermute(held, ('blk', 'circ'), pairs)  123 us
    ppermute x32, starting transfers between devices, gather_columns(): other = lax.ppermute(held, ('blk', 'circ'), pairs)  36.2 us
    ppermute x4, waiting for transfers between devices, with_halo(): lax.ppermute(field[:, -width:, :], 'blk', [(i, i + 1) for i in range(rows...  25.6 us
    ppermute x4, waiting for transfers between devices, with_halo(): lax.ppermute(field[:, :, :width], 'circ', [(i, (i - 1) % cols) for i in r...  16.9 us
    ppermute x4, waiting for transfers between devices, with_halo(): lax.ppermute(field[:, :, -width:], 'circ', [(i, (i + 1) % cols) for i in...  14.3 us
    ppermute x4, starting transfers between devices, with_halo(): lax.ppermute(field[:, -width:, :], 'blk', [(i, i + 1) for i in range(rows...  13.5 us
    ppermute x4, starting transfers between devices, with_halo(): lax.ppermute(field[:, :width, :], 'blk', [(i + 1, i) for i in range(rows...  11.4 us
  transfers between devices with their start and end apart: 48, of which 44 were waited for; matrix products, arithmetic and copies ran while one was open for 5% of the time, Pallas kernels for 0%

profile of v4, /device:TPU:128, one launch (start us, length us, event | category | flops | bytes accessed | tf_op | source)
XLA Modules:
  0.0 322.7 jit_solution(17492664182379808226)
XLA Ops:
  1.8 7.1 %collective-permute-done = f32[20,32]{1,0:T(8,128)S(1)} collective-permute-done((f32[20,32]{1,0:T(8,128)S(1)}, f32[20,32]{1,0:T(8,128)S(1)}, u32[]{:S(2)}, u32[]{:S(2)}) %collective-permute-start) | collective-permute-done | bytes 2592 | tf_op jit(solution)/shard_map/ppermute | solution.py:31
  20.6 3.4 %collective-permute-done.3 = f32[2,2,2,20,32]{4,2,3,1,0:T(2,128)S(1)} collective-permute-done((f32[2,2,2,20,32]{4,2,3,1,0:T(2,128)S(1)}, f32[2,2,2,20,32]{4,2,3,1,0:T(2,128)S(1)}, u32[]{:S(2)}, u32[]{:S(2)}) %collective-permute-start.3) | collective-permute-done | bytes 20512 | tf_op jit(solution)/shard_map/ppermute | solution.py:31
  35.1 6.1 %collective-permute-done.5 = f32[2,2,2,2,2,20,32]{6,4,5,3,2,1,0:T(2,128)S(1)} collective-permute-done((f32[2,2,2,2,2,20,32]{6,4,5,3,2,1,0:T(2,128)S(1)}, f32[2,2,2,2,2,20,32]{6,4,5,3,2,1,0:T(2,128)S(1)}, u32[]{:S(2)}, u32[]{:S(2)}) %collective-permute-start.5) | collective-permute-done | bytes 81952 | tf_op jit(solution)/shard_map/ppermute | solution.py:31
  43.0 9.6 %collective-permute-done.6 = f32[2,2,2,2,2,2,20,32]{7,5,6,4,3,2,1,0:T(2,128)S(1)} collective-permute-done((f32[2,2,2,2,2,2,20,32]{7,5,6,4,3,2,1,0:T(2,128)S(1)}, f32[2,2,2,2,2,2,20,32]{7,5,6,4,3,2,1,0:T(2,128)S(1)}, u32[]{:S(2)}, u32[]{:S(2)}) %collective-permute-start.6) | collective-permute-done | bytes 163872 | tf_op jit(solution)/shard_map/ppermute | solution.py:31
  65.2 5.3 %multiply_convert_fusion = (bf16[32,8192]{1,0:T(8,128)(2,1)S(1)}, bf16[32,8192]{1,0:T(8,128)(2,1)S(1)}, bf16[32,8192]{1,0:T(8,128)(2,1)S(1)}, bf16[32,8192]{1,0:T(8,128)(2,1)S(1)}) fusion(f32[8192]{0:T(1024)S(1)} %div.69, f32[8192]{0:T(1024)S(1)} %sub.275, f32[32]{0:T(128)S(1)} %get-tuple-element.173, f32[8192]{0:T(1024)S(1)} %sub.270, ...), kind=kLoop, calls=%fused_computation.38 | loop fusion | flops 8650752 | bytes 2261632 | tf_op jit(solution)/shard_map/convert.1
  71.7 7.3 %collective-permute-done.12 = bf16[16,32]{1,0:T(8,128)(2,1)S(1)} collective-permute-done((bf16[16,32]{1,0:T(8,128)(2,1)S(1)}, bf16[16,32]{1,0:T(8,128)(2,1)S(1)}, u32[]{:S(2)}, u32[]{:S(2)}) %collective-permute-start.12) | collective-permute-done | bytes 1056 | tf_op jit(solution)/shard_map/ppermute | solution.py:31
  97.8 3.8 %collective-permute-start.17 = (bf16[2,2,2,2,2,16,32]{6,5,4,3,2,1,0:T(8,128)(2,1)S(1)}, bf16[2,2,2,2,2,16,32]{6,5,4,3,2,1,0:T(8,128)(2,1)S(1)}, u32[]{:S(2)}, u32[]{:S(2)}) collective-permute-start(bf16[2,2,2,2,2,16,32]{6,5,4,3,2,1,0:T(8,128)(2,1)S(1)} %get-tuple-element.125), channel_id=1, source_target_pairs={{0,8},{1,9},{2,10},{3,11},{4,12},{5,13},{6,14},{7,15},{8,0},{9,1},... | collective-permute-start | bytes 98312 | tf_op jit(solution)/shard_map/ppermute | solution.py:31
  101.6 3.6 %collective-permute-done.17 = bf16[2,2,2,2,2,16,32]{6,5,4,3,2,1,0:T(8,128)(2,1)S(1)} collective-permute-done((bf16[2,2,2,2,2,16,32]{6,5,4,3,2,1,0:T(8,128)(2,1)S(1)}, bf16[2,2,2,2,2,16,32]{6,5,4,3,2,1,0:T(8,128)(2,1)S(1)}, u32[]{:S(2)}, u32[]{:S(2)}) %collective-permute-start.17) | collective-permute-done | bytes 32800 | tf_op jit(solution)/shard_map/ppermute | solution.py:31
  107.7 4.1 %collective-permute-done.18 = bf16[2,2,2,2,2,2,16,32]{7,6,5,4,3,2,1,0:T(8,128)(2,1)S(1)} collective-permute-done((bf16[2,2,2,2,2,2,16,32]{7,6,5,4,3,2,1,0:T(8,128)(2,1)S(1)}, bf16[2,2,2,2,2,2,16,32]{7,6,5,4,3,2,1,0:T(8,128)(2,1)S(1)}, u32[]{:S(2)}, u32[]{:S(2)}) %collective-permute-start.18) | collective-permute-done | bytes 65568 | tf_op jit(solution)/shard_map/ppermute | solution.py:31
  124.1 5.3 %collective-permute-start.9 = (f32[33,4,256]{2,1,0:T(4,128)S(1)}, f32[33,4,256]{2,1,0:T(4,128)S(1)}, u32[]{:S(2)}, u32[]{:S(2)}) collective-permute-start(f32[33,4,256]{2,1,0:T(4,128)S(1)} %get-tuple-element.97), channel_id=1, source_target_pairs={{4,0},{8,4},{12,8},{16,12},{20,16},{24,20},{28,24},{32,28},{36,32}... | collective-permute-start | bytes 405512 | tf_op jit(solution)/shard_map/ppermute | solution.py:43
  133.0 8.3 %collective-permute-done.8 = f32[33,4,256]{2,1,0:T(4,128)S(1)} collective-permute-done((f32[33,4,256]{2,1,0:T(4,128)S(1)}, f32[33,4,256]{2,1,0:T(4,128)S(1)}, u32[]{:S(2)}, u32[]{:S(2)}) %collective-permute-start.8) | collective-permute-done | bytes 135200 | tf_op jit(solution)/shard_map/ppermute | solution.py:42
  143.8 5.7 %collective-permute-done.11 = f32[33,16,4]{2,1,0:T(8,128)S(1)} collective-permute-done((f32[33,16,4]{2,1,0:T(8,128)S(1)}, f32[33,16,4]{2,1,0:T(8,128)S(1)}, u32[]{:S(2)}, u32[]{:S(2)}) %collective-permute-start.11) | collective-permute-done | bytes 8480 | tf_op jit(solution)/shard_map/ppermute | solution.py:46
  156.9 7.5 %collective-permute-done.24 = bf16[16,32]{1,0:T(8,128)(2,1)S(1)} collective-permute-done((bf16[16,32]{1,0:T(8,128)(2,1)S(1)}, bf16[16,32]{1,0:T(8,128)(2,1)S(1)}, u32[]{:S(2)}, u32[]{:S(2)}) %collective-permute-start.24) | collective-permute-done | bytes 1056 | tf_op jit(solution)/shard_map/ppermute | solution.py:31
  165.6 3.4 %collective-permute-done.25 = bf16[2,16,32]{2,1,0:T(8,128)(2,1)S(1)} collective-permute-done((bf16[2,16,32]{2,1,0:T(8,128)(2,1)S(1)}, bf16[2,16,32]{2,1,0:T(8,128)(2,1)S(1)}, u32[]{:S(2)}, u32[]{:S(2)}) %collective-permute-start.25) | collective-permute-done | bytes 2080 | tf_op jit(solution)/shard_map/ppermute | solution.py:31
  178.5 4.2 %collective-permute-done.28 = bf16[2,2,2,2,16,32]{5,4,3,2,1,0:T(8,128)(2,1)S(1)} collective-permute-done((bf16[2,2,2,2,16,32]{5,4,3,2,1,0:T(8,128)(2,1)S(1)}, bf16[2,2,2,2,16,32]{5,4,3,2,1,0:T(8,128)(2,1)S(1)}, u32[]{:S(2)}, u32[]{:S(2)}) %collective-permute-start.28) | collective-permute-done | bytes 16416 | tf_op jit(solution)/shard_map/ppermute | solution.py:31
  184.9 3.9 %collective-permute-start.20 = (f32[33,4,256]{2,1,0:T(4,128)S(1)}, f32[33,4,256]{2,1,0:T(4,128)S(1)}, u32[]{:S(2)}, u32[]{:S(2)}) collective-permute-start(f32[33,4,256]{2,1,0:T(4,128)S(1)} %get-tuple-element.94), channel_id=1, source_target_pairs={{0,4},{4,8},{8,12},{12,16},{16,20},{20,24},{24,28},{28,32},{32,36}... | collective-permute-start | bytes 405512 | tf_op jit(solution)/shard_map/ppermute | solution.py:42
  190.9 5.1 %collective-permute-done.20 = f32[33,4,256]{2,1,0:T(4,128)S(1)} collective-permute-done((f32[33,4,256]{2,1,0:T(4,128)S(1)}, f32[33,4,256]{2,1,0:T(4,128)S(1)}, u32[]{:S(2)}, u32[]{:S(2)}) %collective-permute-start.20) | collective-permute-done | bytes 135200 | tf_op jit(solution)/shard_map/ppermute | solution.py:42
  201.2 4.9 %collective-permute-done.22 = f32[33,16,4]{2,1,0:T(8,128)S(1)} collective-permute-done((f32[33,16,4]{2,1,0:T(8,128)S(1)}, f32[33,16,4]{2,1,0:T(8,128)S(1)}, u32[]{:S(2)}, u32[]{:S(2)}) %collective-permute-start.22) | collective-permute-done | bytes 8480 | tf_op jit(solution)/shard_map/ppermute | solution.py:45
  218.1 7.5 %collective-permute-done.36 = bf16[16,32]{1,0:T(8,128)(2,1)S(1)} collective-permute-done((bf16[16,32]{1,0:T(8,128)(2,1)S(1)}, bf16[16,32]{1,0:T(8,128)(2,1)S(1)}, u32[]{:S(2)}, u32[]{:S(2)}) %collective-permute-start.36) | collective-permute-done | bytes 1056 | tf_op jit(solution)/shard_map/ppermute | solution.py:31
  226.0 4.1 %collective-permute-done.37 = bf16[2,16,32]{2,1,0:T(8,128)(2,1)S(1)} collective-permute-done((bf16[2,16,32]{2,1,0:T(8,128)(2,1)S(1)}, bf16[2,16,32]{2,1,0:T(8,128)(2,1)S(1)}, u32[]{:S(2)}, u32[]{:S(2)}) %collective-permute-start.37) | collective-permute-done | bytes 2080 | tf_op jit(solution)/shard_map/ppermute | solution.py:31
  231.3 4.2 %collective-permute-done.38 = bf16[2,2,16,32]{3,2,1,0:T(8,128)(2,1)S(1)} collective-permute-done((bf16[2,2,16,32]{3,2,1,0:T(8,128)(2,1)S(1)}, bf16[2,2,16,32]{3,2,1,0:T(8,128)(2,1)S(1)}, u32[]{:S(2)}, u32[]{:S(2)}) %collective-permute-start.38) | collective-permute-done | bytes 4128 | tf_op jit(solution)/shard_map/ppermute | solution.py:31
  235.6 3.9 %collective-permute-done.39 = bf16[2,2,2,16,32]{4,3,2,1,0:T(8,128)(2,1)S(1)} collective-permute-done((bf16[2,2,2,16,32]{4,3,2,1,0:T(8,128)(2,1)S(1)}, bf16[2,2,2,16,32]{4,3,2,1,0:T(8,128)(2,1)S(1)}, u32[]{:S(2)}, u32[]{:S(2)}) %collective-permute-start.39) | collective-permute-done | bytes 8224 | tf_op jit(solution)/shard_map/ppermute | solution.py:31
  239.6 4.3 %collective-permute-done.40 = bf16[2,2,2,2,16,32]{5,4,3,2,1,0:T(8,128)(2,1)S(1)} collective-permute-done((bf16[2,2,2,2,16,32]{5,4,3,2,1,0:T(8,128)(2,1)S(1)}, bf16[2,2,2,2,16,32]{5,4,3,2,1,0:T(8,128)(2,1)S(1)}, u32[]{:S(2)}, u32[]{:S(2)}) %collective-permute-start.40) | collective-permute-done | bytes 16416 | tf_op jit(solution)/shard_map/ppermute | solution.py:31
  244.0 6.5 %collective-permute-done.41 = bf16[2,2,2,2,2,16,32]{6,5,4,3,2,1,0:T(8,128)(2,1)S(1)} collective-permute-done((bf16[2,2,2,2,2,16,32]{6,5,4,3,2,1,0:T(8,128)(2,1)S(1)}, bf16[2,2,2,2,2,16,32]{6,5,4,3,2,1,0:T(8,128)(2,1)S(1)}, u32[]{:S(2)}, u32[]{:S(2)}) %collective-permute-start.41) | collective-permute-done | bytes 32800 | tf_op jit(solution)/shard_map/ppermute | solution.py:31
  251.0 6.4 %collective-permute-done.42 = bf16[2,2,2,2,2,2,16,32]{7,6,5,4,3,2,1,0:T(8,128)(2,1)S(1)} collective-permute-done((bf16[2,2,2,2,2,2,16,32]{7,6,5,4,3,2,1,0:T(8,128)(2,1)S(1)}, bf16[2,2,2,2,2,2,16,32]{7,6,5,4,3,2,1,0:T(8,128)(2,1)S(1)}, u32[]{:S(2)}, u32[]{:S(2)}) %collective-permute-start.42) | collective-permute-done | bytes 65568 | tf_op jit(solution)/shard_map/ppermute | solution.py:31
  271.3 3.6 %collective-permute-start.32 = (f32[33,4,256]{2,1,0:T(4,128)S(1)}, f32[33,4,256]{2,1,0:T(4,128)S(1)}, u32[]{:S(2)}, u32[]{:S(2)}) collective-permute-start(f32[33,4,256]{2,1,0:T(4,128)S(1)} %get-tuple-element.92), channel_id=1, source_target_pairs={{0,4},{4,8},{8,12},{12,16},{16,20},{20,24},{24,28},{28,32},{32,36}... | collective-permute-start | bytes 405512 | tf_op jit(solution)/shard_map/ppermute | solution.py:42
  276.5 6.2 %collective-permute-done.32 = f32[33,4,256]{2,1,0:T(4,128)S(1)} collective-permute-done((f32[33,4,256]{2,1,0:T(4,128)S(1)}, f32[33,4,256]{2,1,0:T(4,128)S(1)}, u32[]{:S(2)}, u32[]{:S(2)}) %collective-permute-start.32) | collective-permute-done | bytes 135200 | tf_op jit(solution)/shard_map/ppermute | solution.py:42
  283.6 4.8 %collective-permute-done.35 = f32[33,16,4]{2,1,0:T(8,128)S(1)} collective-permute-done((f32[33,16,4]{2,1,0:T(8,128)S(1)}, f32[33,16,4]{2,1,0:T(8,128)S(1)}, u32[]{:S(2)}, u32[]{:S(2)}) %collective-permute-start.35) | collective-permute-done | bytes 8480 | tf_op jit(solution)/shard_map/ppermute | solution.py:46
  288.4 4.1 %collective-permute-done.34 = f32[33,16,4]{2,1,0:T(8,128)S(1)} collective-permute-done((f32[33,16,4]{2,1,0:T(8,128)S(1)}, f32[33,16,4]{2,1,0:T(8,128)S(1)}, u32[]{:S(2)}, u32[]{:S(2)}) %collective-permute-start.34) | collective-permute-done | bytes 8480 | tf_op jit(solution)/shard_map/ppermute | solution.py:45
  298.2 4.1 %collective-permute-start.44 = (f32[33,4,256]{2,1,0:T(4,128)S(1)}, f32[33,4,256]{2,1,0:T(4,128)S(1)}, u32[]{:S(2)}, u32[]{:S(2)}) collective-permute-start(f32[33,4,256]{2,1,0:T(4,128)S(1)} %get-tuple-element.90), channel_id=1, source_target_pairs={{0,4},{4,8},{8,12},{12,16},{16,20},{20,24},{24,28},{28,32},{32,36}... | collective-permute-start | bytes 405512 | tf_op jit(solution)/shard_map/ppermute | solution.py:42
  303.4 5.9 %collective-permute-done.44 = f32[33,4,256]{2,1,0:T(4,128)S(1)} collective-permute-done((f32[33,4,256]{2,1,0:T(4,128)S(1)}, f32[33,4,256]{2,1,0:T(4,128)S(1)}, u32[]{:S(2)}, u32[]{:S(2)}) %collective-permute-start.44) | collective-permute-done | bytes 135200 | tf_op jit(solution)/shard_map/ppermute | solution.py:42
  310.8 4.7 %collective-permute-done.47 = f32[33,16,4]{2,1,0:T(8,128)S(1)} collective-permute-done((f32[33,16,4]{2,1,0:T(8,128)S(1)}, f32[33,16,4]{2,1,0:T(8,128)S(1)}, u32[]{:S(2)}, u32[]{:S(2)}) %collective-permute-start.47) | collective-permute-done | bytes 8480 | tf_op jit(solution)/shard_map/ppermute | solution.py:46
  (367 shorter events, 151.3 us)
Async XLA Ops:
  1.4 7.6 %collective-permute-start = (f32[20,32]{1,0:T(8,128)S(1)}, f32[20,32]{1,0:T(8,128)S(1)}, u32[]{:S(2)}, u32[]{:S(2)}) collective-permute-start(f32[20,32]{1,0:T(8,128)S(1)} %get-tuple-element.159), channel_id=1, source_target_pairs={{0,128},{1,129},{2,130},{3,131},{4,132},{5,133},{6,134},{7,135},{8... | collective-permute-start | bytes 7688 | tf_op jit(solution)/shard_map/ppermute | solution.py:31
  13.8 5.6 %collective-permute-start.2 = (f32[2,2,20,32]{3,1,2,0:T(2,128)S(1)}, f32[2,2,20,32]{3,1,2,0:T(2,128)S(1)}, u32[]{:S(2)}, u32[]{:S(2)}) collective-permute-start(f32[2,2,20,32]{3,1,2,0:T(2,128)S(1)} %get-tuple-element.135), channel_id=1, source_target_pairs={{0,2},{1,3},{2,0},{3,1},{4,6},{5,7},{6,4},{7,5},{8,10},{9,11},{10,... | collective-permute-start | bytes 30728 | tf_op jit(solution)/shard_map/ppermute | solution.py:31
  24.2 5.4 %collective-permute-start.4 = (f32[2,2,2,2,20,32]{5,3,4,2,1,0:T(2,128)S(1)}, f32[2,2,2,2,20,32]{5,3,4,2,1,0:T(2,128)S(1)}, u32[]{:S(2)}, u32[]{:S(2)}) collective-permute-start(f32[2,2,2,2,20,32]{5,3,4,2,1,0:T(2,128)S(1)} %get-tuple-element.115), channel_id=1, source_target_pairs={{0,16},{1,17},{2,18},{3,19},{4,20},{5,21},{6,22},{7,23},{8,24},{9,... | collective-permute-start | bytes 122888 | tf_op jit(solution)/shard_map/ppermute | solution.py:31
  29.8 11.4 %collective-permute-start.5 = (f32[2,2,2,2,2,20,32]{6,4,5,3,2,1,0:T(2,128)S(1)}, f32[2,2,2,2,2,20,32]{6,4,5,3,2,1,0:T(2,128)S(1)}, u32[]{:S(2)}, u32[]{:S(2)}) collective-permute-start(f32[2,2,2,2,2,20,32]{6,4,5,3,2,1,0:T(2,128)S(1)} %get-tuple-element.89), channel_id=1, source_target_pairs={{0,8},{1,9},{2,10},{3,11},{4,12},{5,13},{6,14},{7,15},{8,0},{9,1},... | collective-permute-start | bytes 245768 | tf_op jit(solution)/shard_map/ppermute | solution.py:31
  41.7 10.9 %collective-permute-start.6 = (f32[2,2,2,2,2,2,20,32]{7,5,6,4,3,2,1,0:T(2,128)S(1)}, f32[2,2,2,2,2,2,20,32]{7,5,6,4,3,2,1,0:T(2,128)S(1)}, u32[]{:S(2)}, u32[]{:S(2)}) collective-permute-start(f32[2,2,2,2,2,2,20,32]{7,5,6,4,3,2,1,0:T(2,128)S(1)} %get-tuple-element.73), channel_id=1, source_target_pairs={{0,4},{1,5},{2,6},{3,7},{4,0},{5,1},{6,2},{7,3},{8,12},{9,13},{10,... | collective-permute-start | bytes 491528 | tf_op jit(solution)/shard_map/ppermute | solution.py:31
  71.4 7.5 %collective-permute-start.12 = (bf16[16,32]{1,0:T(8,128)(2,1)S(1)}, bf16[16,32]{1,0:T(8,128)(2,1)S(1)}, u32[]{:S(2)}, u32[]{:S(2)}) collective-permute-start(bf16[16,32]{1,0:T(8,128)(2,1)S(1)} %get-tuple-element.167), channel_id=1, source_target_pairs={{0,128},{1,129},{2,130},{3,131},{4,132},{5,133},{6,134},{7,135},{8... | collective-permute-start | bytes 3080 | tf_op jit(solution)/shard_map/ppermute | solution.py:31
  83.5 5.3 %collective-permute-start.14 = (bf16[2,2,16,32]{3,2,1,0:T(8,128)(2,1)S(1)}, bf16[2,2,16,32]{3,2,1,0:T(8,128)(2,1)S(1)}, u32[]{:S(2)}, u32[]{:S(2)}) collective-permute-start(bf16[2,2,16,32]{3,2,1,0:T(8,128)(2,1)S(1)} %get-tuple-element.157), channel_id=1, source_target_pairs={{0,2},{1,3},{2,0},{3,1},{4,6},{5,7},{6,4},{7,5},{8,10},{9,11},{10,... | collective-permute-start | bytes 12296 | tf_op jit(solution)/shard_map/ppermute | solution.py:31
  97.8 7.4 %collective-permute-start.17 = (bf16[2,2,2,2,2,16,32]{6,5,4,3,2,1,0:T(8,128)(2,1)S(1)}, bf16[2,2,2,2,2,16,32]{6,5,4,3,2,1,0:T(8,128)(2,1)S(1)}, u32[]{:S(2)}, u32[]{:S(2)}) collective-permute-start(bf16[2,2,2,2,2,16,32]{6,5,4,3,2,1,0:T(8,128)(2,1)S(1)} %get-tuple-element.125), channel_id=1, source_target_pairs={{0,8},{1,9},{2,10},{3,11},{4,12},{5,13},{6,14},{7,15},{8,0},{9,1},... | collective-permute-start | bytes 98312 | tf_op jit(solution)/shard_map/ppermute | solution.py:31
  105.3 6.6 %collective-permute-start.18 = (bf16[2,2,2,2,2,2,16,32]{7,6,5,4,3,2,1,0:T(8,128)(2,1)S(1)}, bf16[2,2,2,2,2,2,16,32]{7,6,5,4,3,2,1,0:T(8,128)(2,1)S(1)}, u32[]{:S(2)}, u32[]{:S(2)}) collective-permute-start(bf16[2,2,2,2,2,2,16,32]{7,6,5,4,3,2,1,0:T(8,128)(2,1)S(1)} %get-tuple-element.109), channel_id=1, source_target_pairs={{0,4},{1,5},{2,6},{3,7},{4,0},{5,1},{6,2},{7,3},{8,12},{9,13},{10,... | collective-permute-start | bytes 196616 | tf_op jit(solution)/shard_map/ppermute | solution.py:31
  124.1 8.8 %collective-permute-start.9 = (f32[33,4,256]{2,1,0:T(4,128)S(1)}, f32[33,4,256]{2,1,0:T(4,128)S(1)}, u32[]{:S(2)}, u32[]{:S(2)}) collective-permute-start(f32[33,4,256]{2,1,0:T(4,128)S(1)} %get-tuple-element.97), channel_id=1, source_target_pairs={{4,0},{8,4},{12,8},{16,12},{20,16},{24,20},{28,24},{32,28},{36,32}... | collective-permute-start | bytes 405512 | tf_op jit(solution)/shard_map/ppermute | solution.py:43
  129.5 11.8 %collective-permute-start.8 = (f32[33,4,256]{2,1,0:T(4,128)S(1)}, f32[33,4,256]{2,1,0:T(4,128)S(1)}, u32[]{:S(2)}, u32[]{:S(2)}) collective-permute-start(f32[33,4,256]{2,1,0:T(4,128)S(1)} %get-tuple-element.96), channel_id=1, source_target_pairs={{0,4},{4,8},{8,12},{12,16},{16,20},{20,24},{24,28},{28,32},{32,36}... | collective-permute-start | bytes 405512 | tf_op jit(solution)/shard_map/ppermute | solution.py:42
  141.5 7.9 %collective-permute-start.11 = (f32[33,16,4]{2,1,0:T(8,128)S(1)}, f32[33,16,4]{2,1,0:T(8,128)S(1)}, u32[]{:S(2)}, u32[]{:S(2)}) collective-permute-start(f32[33,16,4]{2,1,0:T(8,128)S(1)} %get-tuple-element.81), channel_id=1, source_target_pairs={{0,3},{1,0},{2,1},{3,2},{4,7},{5,4},{6,5},{7,6},{8,11},{9,8},{10,9... | collective-permute-start | bytes 25352 | tf_op jit(solution)/shard_map/ppermute | solution.py:46
  143.3 8.4 %collective-permute-start.10 = (f32[33,16,4]{2,1,0:T(8,128)S(1)}, f32[33,16,4]{2,1,0:T(8,128)S(1)}, u32[]{:S(2)}, u32[]{:S(2)}) collective-permute-start(f32[33,16,4]{2,1,0:T(8,128)S(1)} %get-tuple-element.80), channel_id=1, source_target_pairs={{0,1},{1,2},{2,3},{3,0},{4,5},{5,6},{6,7},{7,4},{8,9},{9,10},{10,1... | collective-permute-start | bytes 25352 | tf_op jit(solution)/shard_map/ppermute | solution.py:45
  156.9 7.5 %collective-permute-start.24 = (bf16[16,32]{1,0:T(8,128)(2,1)S(1)}, bf16[16,32]{1,0:T(8,128)(2,1)S(1)}, u32[]{:S(2)}, u32[]{:S(2)}) collective-permute-start(bf16[16,32]{1,0:T(8,128)(2,1)S(1)} %get-tuple-element.51), channel_id=1, source_target_pairs={{0,128},{1,129},{2,130},{3,131},{4,132},{5,133},{6,134},{7,135},{8... | collective-permute-start | bytes 3080 | tf_op jit(solution)/shard_map/ppermute | solution.py:31
  169.0 5.3 %collective-permute-start.26 = (bf16[2,2,16,32]{3,2,1,0:T(8,128)(2,1)S(1)}, bf16[2,2,16,32]{3,2,1,0:T(8,128)(2,1)S(1)}, u32[]{:S(2)}, u32[]{:S(2)}) collective-permute-start(bf16[2,2,16,32]{3,2,1,0:T(8,128)(2,1)S(1)} %get-tuple-element.155), channel_id=1, source_target_pairs={{0,2},{1,3},{2,0},{3,1},{4,6},{5,7},{6,4},{7,5},{8,10},{9,11},{10,... | collective-permute-start | bytes 12296 | tf_op jit(solution)/shard_map/ppermute | solution.py:31
  182.8 8.0 %collective-permute-start.29 = (bf16[2,2,2,2,2,16,32]{6,5,4,3,2,1,0:T(8,128)(2,1)S(1)}, bf16[2,2,2,2,2,16,32]{6,5,4,3,2,1,0:T(8,128)(2,1)S(1)}, u32[]{:S(2)}, u32[]{:S(2)}) collective-permute-start(bf16[2,2,2,2,2,16,32]{6,5,4,3,2,1,0:T(8,128)(2,1)S(1)} %get-tuple-element.123), channel_id=1, source_target_pairs={{0,8},{1,9},{2,10},{3,11},{4,12},{5,13},{6,14},{7,15},{8,0},{9,1},... | collective-permute-start | bytes 98312 | tf_op jit(solution)/shard_map/ppermute | solution.py:31
  182.9 8.0 %collective-permute-start.21 = (f32[33,4,256]{2,1,0:T(4,128)S(1)}, f32[33,4,256]{2,1,0:T(4,128)S(1)}, u32[]{:S(2)}, u32[]{:S(2)}) collective-permute-start(f32[33,4,256]{2,1,0:T(4,128)S(1)} %get-tuple-element.95), channel_id=1, source_target_pairs={{4,0},{8,4},{12,8},{16,12},{20,16},{24,20},{28,24},{32,28},{36,32}... | collective-permute-start | bytes 405512 | tf_op jit(solution)/shard_map/ppermute | solution.py:43
  184.9 11.1 %collective-permute-start.20 = (f32[33,4,256]{2,1,0:T(4,128)S(1)}, f32[33,4,256]{2,1,0:T(4,128)S(1)}, u32[]{:S(2)}, u32[]{:S(2)}) collective-permute-start(f32[33,4,256]{2,1,0:T(4,128)S(1)} %get-tuple-element.94), channel_id=1, source_target_pairs={{0,4},{4,8},{8,12},{12,16},{16,20},{20,24},{24,28},{28,32},{32,36}... | collective-permute-start | bytes 405512 | tf_op jit(solution)/shard_map/ppermute | solution.py:42
  190.8 6.5 %collective-permute-start.30 = (bf16[2,2,2,2,2,2,16,32]{7,6,5,4,3,2,1,0:T(8,128)(2,1)S(1)}, bf16[2,2,2,2,2,2,16,32]{7,6,5,4,3,2,1,0:T(8,128)(2,1)S(1)}, u32[]{:S(2)}, u32[]{:S(2)}) collective-permute-start(bf16[2,2,2,2,2,2,16,32]{7,6,5,4,3,2,1,0:T(8,128)(2,1)S(1)} %get-tuple-element.105), channel_id=1, source_target_pairs={{0,4},{1,5},{2,6},{3,7},{4,0},{5,1},{6,2},{7,3},{8,12},{9,13},{10,... | collective-permute-start | bytes 196616 | tf_op jit(solution)/shard_map/ppermute | solution.py:31
  196.3 9.8 %collective-permute-start.22 = (f32[33,16,4]{2,1,0:T(8,128)S(1)}, f32[33,16,4]{2,1,0:T(8,128)S(1)}, u32[]{:S(2)}, u32[]{:S(2)}) collective-permute-start(f32[33,16,4]{2,1,0:T(8,128)S(1)} %get-tuple-element.78), channel_id=1, source_target_pairs={{0,1},{1,2},{2,3},{3,0},{4,5},{5,6},{6,7},{7,4},{8,9},{9,10},{10,1... | collective-permute-start | bytes 25352 | tf_op jit(solution)/shard_map/ppermute | solution.py:45
  197.4 13.3 %collective-permute-start.31 = (bf16[2,2,2,2,2,2,2,16,32]{8,7,6,5,4,3,2,1,0:T(8,128)(2,1)S(1)}, bf16[2,2,2,2,2,2,2,16,32]{8,7,6,5,4,3,2,1,0:T(8,128)(2,1)S(1)}, u32[]{:S(2)}, u32[]{:S(2)}) collective-permute-start(bf16[2,2,2,2,2,2,2,16,32]{8,7,6,5,4,3,2,1,0:T(8,128)(2,1)S(1)} %get-tuple-element.85), channel_id=1, source_target_pairs={{0,1},{1,0},{2,3},{3,2},{4,5},{5,4},{6,7},{7,6},{8,9},{9,8},{10,11... | collective-permute-start | bytes 393224 | tf_op jit(solution)/shard_map/ppermute | solution.py:31
  218.1 7.5 %collective-permute-start.36 = (bf16[16,32]{1,0:T(8,128)(2,1)S(1)}, bf16[16,32]{1,0:T(8,128)(2,1)S(1)}, u32[]{:S(2)}, u32[]{:S(2)}) collective-permute-start(bf16[16,32]{1,0:T(8,128)(2,1)S(1)} %get-tuple-element.161), channel_id=1, source_target_pairs={{0,128},{1,129},{2,130},{3,131},{4,132},{5,133},{6,134},{7,135},{8... | collective-permute-start | bytes 3080 | tf_op jit(solution)/shard_map/ppermute | solution.py:31
  243.9 6.6 %collective-permute-start.41 = (bf16[2,2,2,2,2,16,32]{6,5,4,3,2,1,0:T(8,128)(2,1)S(1)}, bf16[2,2,2,2,2,16,32]{6,5,4,3,2,1,0:T(8,128)(2,1)S(1)}, u32[]{:S(2)}, u32[]{:S(2)}) collective-permute-start(bf16[2,2,2,2,2,16,32]{6,5,4,3,2,1,0:T(8,128)(2,1)S(1)} %get-tuple-element.119), channel_id=1, source_target_pairs={{0,8},{1,9},{2,10},{3,11},{4,12},{5,13},{6,14},{7,15},{8,0},{9,1},... | collective-permute-start | bytes 98312 | tf_op jit(solution)/shard_map/ppermute | solution.py:31
  250.5 6.9 %collective-permute-start.42 = (bf16[2,2,2,2,2,2,16,32]{7,6,5,4,3,2,1,0:T(8,128)(2,1)S(1)}, bf16[2,2,2,2,2,2,16,32]{7,6,5,4,3,2,1,0:T(8,128)(2,1)S(1)}, u32[]{:S(2)}, u32[]{:S(2)}) collective-permute-start(bf16[2,2,2,2,2,2,16,32]{7,6,5,4,3,2,1,0:T(8,128)(2,1)S(1)} %get-tuple-element.101), channel_id=1, source_target_pairs={{0,4},{1,5},{2,6},{3,7},{4,0},{5,1},{6,2},{7,3},{8,12},{9,13},{10,... | collective-permute-start | bytes 196616 | tf_op jit(solution)/shard_map/ppermute | solution.py:31
  269.0 7.5 %collective-permute-start.33 = (f32[33,4,256]{2,1,0:T(4,128)S(1)}, f32[33,4,256]{2,1,0:T(4,128)S(1)}, u32[]{:S(2)}, u32[]{:S(2)}) collective-permute-start(f32[33,4,256]{2,1,0:T(4,128)S(1)} %get-tuple-element.93), channel_id=1, source_target_pairs={{4,0},{8,4},{12,8},{16,12},{20,16},{24,20},{28,24},{32,28},{36,32}... | collective-permute-start | bytes 405512 | tf_op jit(solution)/shard_map/ppermute | solution.py:43
  271.3 11.5 %collective-permute-start.32 = (f32[33,4,256]{2,1,0:T(4,128)S(1)}, f32[33,4,256]{2,1,0:T(4,128)S(1)}, u32[]{:S(2)}, u32[]{:S(2)}) collective-permute-start(f32[33,4,256]{2,1,0:T(4,128)S(1)} %get-tuple-element.92), channel_id=1, source_target_pairs={{0,4},{4,8},{8,12},{12,16},{16,20},{20,24},{24,28},{28,32},{32,36}... | collective-permute-start | bytes 405512 | tf_op jit(solution)/shard_map/ppermute | solution.py:42
  283.0 5.4 %collective-permute-start.35 = (f32[33,16,4]{2,1,0:T(8,128)S(1)}, f32[33,16,4]{2,1,0:T(8,128)S(1)}, u32[]{:S(2)}, u32[]{:S(2)}) collective-permute-start(f32[33,16,4]{2,1,0:T(8,128)S(1)} %get-tuple-element.77), channel_id=1, source_target_pairs={{0,3},{1,0},{2,1},{3,2},{4,7},{5,4},{6,5},{7,6},{8,11},{9,8},{10,9... | collective-permute-start | bytes 25352 | tf_op jit(solution)/shard_map/ppermute | solution.py:46
  283.1 9.4 %collective-permute-start.34 = (f32[33,16,4]{2,1,0:T(8,128)S(1)}, f32[33,16,4]{2,1,0:T(8,128)S(1)}, u32[]{:S(2)}, u32[]{:S(2)}) collective-permute-start(f32[33,16,4]{2,1,0:T(8,128)S(1)} %get-tuple-element.76), channel_id=1, source_target_pairs={{0,1},{1,2},{2,3},{3,0},{4,5},{5,6},{6,7},{7,4},{8,9},{9,10},{10,1... | collective-permute-start | bytes 25352 | tf_op jit(solution)/shard_map/ppermute | solution.py:45
  296.2 7.2 %collective-permute-start.45 = (f32[33,4,256]{2,1,0:T(4,128)S(1)}, f32[33,4,256]{2,1,0:T(4,128)S(1)}, u32[]{:S(2)}, u32[]{:S(2)}) collective-permute-start(f32[33,4,256]{2,1,0:T(4,128)S(1)} %get-tuple-element.91), channel_id=1, source_target_pairs={{4,0},{8,4},{12,8},{16,12},{20,16},{24,20},{28,24},{32,28},{36,32}... | collective-permute-start | bytes 405512 | tf_op jit(solution)/shard_map/ppermute | solution.py:43
  298.2 11.1 %collective-permute-start.44 = (f32[33,4,256]{2,1,0:T(4,128)S(1)}, f32[33,4,256]{2,1,0:T(4,128)S(1)}, u32[]{:S(2)}, u32[]{:S(2)}) collective-permute-start(f32[33,4,256]{2,1,0:T(4,128)S(1)} %get-tuple-element.90), channel_id=1, source_target_pairs={{0,4},{4,8},{8,12},{12,16},{16,20},{20,24},{24,28},{28,32},{32,36}... | collective-permute-start | bytes 405512 | tf_op jit(solution)/shard_map/ppermute | solution.py:42
  309.5 5.9 %collective-permute-start.47 = (f32[33,16,4]{2,1,0:T(8,128)S(1)}, f32[33,16,4]{2,1,0:T(8,128)S(1)}, u32[]{:S(2)}, u32[]{:S(2)}) collective-permute-start(f32[33,16,4]{2,1,0:T(8,128)S(1)} %get-tuple-element.75), channel_id=1, source_target_pairs={{0,3},{1,0},{2,1},{3,2},{4,7},{5,4},{6,5},{7,6},{8,11},{9,8},{10,9... | collective-permute-start | bytes 25352 | tf_op jit(solution)/shard_map/ppermute | solution.py:46
  309.6 8.8 %collective-permute-start.46 = (f32[33,16,4]{2,1,0:T(8,128)S(1)}, f32[33,16,4]{2,1,0:T(8,128)S(1)}, u32[]{:S(2)}, u32[]{:S(2)}) collective-permute-start(f32[33,16,4]{2,1,0:T(8,128)S(1)} %get-tuple-element.74), channel_id=1, source_target_pairs={{0,1},{1,2},{2,3},{3,0},{4,5},{5,6},{6,7},{7,4},{8,9},{9,10},{10,1... | collective-permute-start | bytes 25352 | tf_op jit(solution)/shard_map/ppermute | solution.py:45
  (62 other events, 870.6 us)
